TPU v7x, 32 devices: a whole 2x2x4 slice. The times are simulated.
32 devices in a mesh: blk: 2 (over x), gy: 4 (over y, core), gz: 4 (over z).
Axes of the slice: x: 2, y: 2, z: 4, core: 2. Of those that a mesh axis runs over, the one named last changes fastest.
Arguments:
- vacancy: float32 [64, 64, 1024], P('blk', 'gy', 'gz'), may hold values from -6 to 6
- grain_label: int32 [64, 64, 1024], P('blk', 'gy', 'gz'), may hold values from 0 to 7
- pore_mask: int32 [64, 64, 1024], P('blk', 'gy', 'gz'), may hold values 0 or 1
- cotangent: float32 [64, 64, 1024], P('blk', 'gy', 'gz'), may hold values from -6 to 6
Outputs:
- final_field: float32 [64, 64, 1024], P('blk', 'gy', 'gz')
- gradient: float32 [64, 64, 1024], P('blk', 'gy', 'gz')
All inputs are finite; a program needn't handle non-finite values. No bound on the sum of `pore_mask` on one device may be relied on, other than what follows from the above.
Results may differ from a plain program's by a relative error of at most 0.00017.
Values sent between devices are 32-bit elements; how exact they have to be, the bound alone decides.
No kernel may reach another device: no remote copies, remote signals or barrier semaphores. Data moves between devices by JAX's collectives and lax.ppermute only.
A program may use at most 128 MiB of HBM per device.

v0:
```python
import jax
import jax.numpy as jnp
from jax import lax
from jax.experimental import pallas as pl
from jax.experimental.pallas import tpu as pltpu
from jax.sharding import PartitionSpec as P


cross_rate = 0.0125
boundary_gain = 3.0
F32 = jnp.float32


def face_value(mobility_here, mobility_there, label_here, label_there):
    harmonic = 2.0 * mobility_here * mobility_there / (mobility_here + mobility_there)
    return harmonic * jnp.where(label_here != label_there, boundary_gain, 1.0)


def _vmem():
    return pl.BlockSpec(memory_space=pltpu.VMEM)


def _smem():
    return pl.BlockSpec(memory_space=pltpu.SMEM)


def _shift(x, edge, axis, up):
    n = x.shape[axis]
    idx = lax.broadcasted_iota(jnp.int32, x.shape, axis)
    edge = jnp.broadcast_to(edge, x.shape)
    if up:
        return jnp.where(idx == n - 1, edge, pltpu.roll(x, n - 1, axis))
    return jnp.where(idx == 0, edge, pltpu.roll(x, 1, axis))


def _neighbours(x, ylo, yhi, zlo, zhi):
    return (
        _shift(x, yhi, 0, True),
        _shift(x, ylo, 0, False),
        _shift(x, zhi, 1, True),
        _shift(x, zlo, 1, False),
    )


def _faces(mob, lab, mob_n, lab_n):
    ups = (True, False, True, False)
    out = []
    for up, mn, ln in zip(ups, mob_n, lab_n):
        if up:
            out.append(face_value(mob, mn, lab, ln))
        else:
            out.append(face_value(mn, mob, ln, lab))
    return out


def _flux(u, u_n, faces):
    total = faces[0] * (u_n[0] - u)
    total = total + faces[1] * (u_n[1] - u)
    total = total + faces[2] * (u_n[2] - u)
    total = total + faces[3] * (u_n[3] - u)
    return total


def _yrow(ref, c, i):
    return ref[c, pl.ds(i, 1), :]


def _zcol(ref, c, i):
    return ref[c, :, pl.ds(i, 1)]


def _write_edges(edges, c, r, val):
    y_first, y_last, z_first, z_last = edges
    ny, nz = val.shape
    y_first[c, pl.ds(r, 1), :] = val[0:1, :]
    y_last[c, pl.ds(r, 1), :] = val[ny - 1 : ny, :]
    z_first[c, :, pl.ds(r, 1)] = val[:, 0:1]
    z_last[c, :, pl.ds(r, 1)] = val[:, nz - 1 : nz]


def _geo_row(i, pore_ref, lab_ref, gy_lo, gy_hi, gz_lo, gz_hi):
    mob = 1.0 + 2.0 * pore_ref[i].astype(F32)
    lab = lab_ref[i].astype(F32)
    mob_n = _neighbours(mob, _yrow(gy_lo, 0, i), _yrow(gy_hi, 0, i), _zcol(gz_lo, 0, i), _zcol(gz_hi, 0, i))
    lab_n = _neighbours(lab, _yrow(gy_lo, 1, i), _yrow(gy_hi, 1, i), _zcol(gz_lo, 1, i), _zcol(gz_hi, 1, i))
    return mob, lab, mob_n, _faces(mob, lab, mob_n, lab_n)


def _sweep(m, lower, pivots, ratios, source):
    ys = [None] * m
    prev = None
    for r in range(m - 1):
        num = source[r]
        if num is None:
            if prev is None:
                continue
            num = -(lower[r] * prev)
        elif prev is not None:
            num = num - lower[r] * prev
        ys[r] = num / pivots[r]
        prev = ys[r]
    xs = [None] * m
    prev = None
    for r in range(m - 2, -1, -1):
        if prev is None:
            xs[r] = ys[r]
        elif ys[r] is None:
            xs[r] = -(ratios[r] * prev)
        else:
            xs[r] = ys[r] - ratios[r] * prev
        prev = xs[r]
    return xs


def _factor_kernel(cs, pore_ref, lab_ref, bx_lo, bx_hi, fac_ref, lr_ref, rows_ref):
    m = pore_ref.shape[0]
    zero = jnp.zeros(pore_ref.shape[1:], F32)
    mobs = [1.0 + 2.0 * pore_ref[r].astype(F32) for r in range(m)]
    labs = [lab_ref[r].astype(F32) for r in range(m)]
    m_ext = [bx_lo[0]] + mobs + [bx_hi[0]]
    l_ext = [bx_lo[1]] + labs + [bx_hi[1]]
    w_ext = [0.5 * (1.0 + x) for x in m_ext]
    faces = [face_value(m_ext[k], m_ext[k + 1], l_ext[k], l_ext[k + 1]) for k in range(m + 1)]
    bands = {"f": ([], [], []), "a": ([], [], [])}
    for r in range(m):
        bf, ff = faces[r], faces[r + 1]
        w = w_ext[r + 1]
        main = 1.0 + cs * w * (bf + ff)
        bands["f"][0].append(-cs * bf * w_ext[r])
        bands["f"][1].append(main)
        bands["f"][2].append(-cs * ff * w_ext[r + 2])
        bands["a"][0].append(-cs * bf * w)
        bands["a"][1].append(main)
        bands["a"][2].append(-cs * ff * w)

    for c, key in ((0, "f"), (1, "a")):
        lower, main, upper = bands[key]
        pivots, ratios = [], []
        prev = None
        for r in range(m - 1):
            piv = main[r] if prev is None else main[r] - lower[r] * prev
            rat = upper[r] / piv
            pivots.append(piv)
            ratios.append(rat)
            prev = rat
        left_src = [lower[0]] + [None] * (m - 1)
        right_src = [None] * (m - 2) + [upper[m - 2], None]
        left = _sweep(m, lower, pivots, ratios, left_src)
        right = _sweep(m, lower, pivots, ratios, right_src)
        for r in range(m):
            fac_ref[c, 0, r] = lower[r]
            fac_ref[c, 1, r] = ratios[r] if r < m - 1 else zero
            fac_ref[c, 2, r] = pivots[r] if r < m - 1 else zero + 1.0
            lr_ref[c, 0, r] = left[r] if r < m - 1 else zero
            lr_ref[c, 1, r] = right[r] if r < m - 1 else zero - 1.0
        last_lower = lower[m - 1]
        rows_ref[c, 0] = last_lower * left[m - 2]
        rows_ref[c, 1] = main[m - 1] - last_lower * right[m - 2]
        rows_ref[c, 2] = upper[m - 1]
        rows_ref[c, 3] = left[0]
        rows_ref[c, 4] = right[0]


def _reduced_solve(gs, gv, voff, c, n, pos):
    slot = [(pos - p + n) % n for p in range(n)]
    g = [[gs[slot[p], c, k] for k in range(5)] for p in range(n)]
    v = [[gv[slot[p], c, voff + k] for k in range(2)] for p in range(n)]
    lower = [-g[p][0] for p in range(n)]
    main = [g[p][1] - g[p][2] * g[(p + 1) % n][3] for p in range(n)]
    upper = [-g[p][2] * g[(p + 1) % n][4] for p in range(n)]
    src = [v[p][0] - g[p][2] * v[(p + 1) % n][1] for p in range(n)]
    k_in = n - 1
    pivots, ratios = [], []
    prev = None
    for r in range(k_in):
        piv = main[r] if prev is None else main[r] - lower[r] * prev
        rat = upper[r] / piv
        pivots.append(piv)
        ratios.append(rat)
        prev = rat

    def apply(source):
        ys = []
        prev = None
        for r in range(k_in):
            num = source[r] if prev is None else source[r] - lower[r] * prev
            ys.append(num / pivots[r])
            prev = ys[-1]
        xs = [None] * k_in
        prev = None
        for r in range(k_in - 1, -1, -1):
            xs[r] = ys[r] if prev is None else ys[r] - ratios[r] * prev
            prev = xs[r]
        return xs

    coupling = []
    for r in range(k_in):
        term = None
        if r == 0:
            term = lower[0]
        if r == k_in - 1:
            term = upper[k_in - 1] if term is None else term + upper[k_in - 1]
        coupling.append(term if term is not None else jnp.zeros_like(lower[0]))
    linked = apply(coupling)
    closing = main[k_in] - lower[k_in] * linked[k_in - 1] - upper[k_in] * linked[0]
    inner = apply(src[:k_in])
    sep = (src[k_in] - lower[k_in] * inner[k_in - 1] - upper[k_in] * inner[0]) / closing
    return [inner[r] - linked[r] * sep for r in range(k_in)] + [sep]


def _combine_kernel(n, stacked, edge_of, pos_ref, *refs):
    gs_parts, gv_parts = refs[:n], refs[n : 2 * n]
    lr_ref, loc_ref = refs[2 * n], refs[2 * n + 1]
    refs = refs[2 * n + 2 :]
    if stacked:
        out_ref = refs[0]
        outs = (out_ref.at[0], out_ref.at[1])
        rest = refs[1:]
    else:
        outs = refs[:2]
        rest = refs[2:]
    edges, sep_ref, gs_ref, gv_ref = rest[:4], rest[4], rest[5], rest[6]
    for k in range(n):
        gs_ref[k] = gs_parts[k][...]
        gv_ref[k] = gv_parts[k][...]
    m = loc_ref.shape[1]
    p = pos_ref[0]
    for c in range(2):
        seps = _reduced_solve(gs_ref, gv_ref, 0, c, n, p)
        for q in range(n):
            sep_ref[q] = seps[q]
        own = sep_ref[p]
        prior = sep_ref[(p + n - 1) % n]
        for r in range(m):
            val = loc_ref[c, r] - lr_ref[c, 0, r] * prior - lr_ref[c, 1, r] * own
            outs[c][r] = val
            if c in edge_of:
                _write_edges(edges, edge_of[c], r, val)


def _edge_kernel(vac_ref, pore_ref, lab_ref, y_first, y_last, z_first, z_last, bx_first, bx_last):
    m = vac_ref.shape[0]
    edges = (y_first, y_last, z_first, z_last)
    for r in range(m):
        mob = 1.0 + 2.0 * pore_ref[r].astype(F32)
        lab = lab_ref[r].astype(F32)
        for c, val in enumerate((mob, lab, vac_ref[r])):
            _write_edges(edges, c, r, val)
        if r == 0:
            bx_first[0] = mob
            bx_first[1] = lab
        if r == m - 1:
            bx_last[0] = mob
            bx_last[1] = lab


def _local_solves(fac_ref, srcs, loc_ref, vals_ref):
    m = loc_ref.shape[1]
    zero = jnp.zeros(loc_ref.shape[2:], F32)
    for c in range(2):
        lower = [fac_ref[c, 0, r] for r in range(m)]
        ratios = [fac_ref[c, 1, r] for r in range(m - 1)]
        pivots = [fac_ref[c, 2, r] for r in range(m - 1)]
        src = srcs[c]
        local = _sweep(m, lower, pivots, ratios, src[: m - 1] + [None])
        for r in range(m):
            loc_ref[c, r] = local[r] if r < m - 1 else zero
        vals_ref[c, 0] = src[m - 1] - lower[m - 1] * local[m - 2]
        vals_ref[c, 1] = local[0]


def _first_kernel(vac_ref, cot_ref, pore_ref, lab_ref, fac_ref, gy_lo, gy_hi, gz_lo, gz_hi, loc_ref, vals_ref):
    m = pore_ref.shape[0]
    srcs = ([], [cot_ref[r] for r in range(m)])
    for i in range(m):
        mob, _, mob_n, fc = _geo_row(i, pore_ref, lab_ref, gy_lo, gy_hi, gz_lo, gz_hi)
        w = 0.5 * (1.0 + mob)
        v = vac_ref[i]
        v_n = _neighbours(v, _yrow(gy_lo, 2, i), _yrow(gy_hi, 2, i), _zcol(gz_lo, 2, i), _zcol(gz_hi, 2, i))
        u_n = [0.5 * (1.0 + mn) * vn for mn, vn in zip(mob_n, v_n)]
        srcs[0].append(v + cross_rate * (1.0 * _flux(w * v, u_n, fc)))
    _local_solves(fac_ref, srcs, loc_ref, vals_ref)


def _second_kernel(pore_ref, lab_ref, fa_ref, fac_ref, gy_lo, gy_hi, gz_lo, gz_hi,
                   hy_lo, hy_hi, hz_lo, hz_hi, loc_ref, vals_ref):
    m = pore_ref.shape[0]
    srcs = ([], [])
    for i in range(m):
        mob, _, mob_n, fc = _geo_row(i, pore_ref, lab_ref, gy_lo, gy_hi, gz_lo, gz_hi)
        w = 0.5 * (1.0 + mob)
        f1 = fa_ref[0, i]
        f_n = _neighbours(f1, _yrow(hy_lo, 0, i), _yrow(hy_hi, 0, i), _zcol(hz_lo, 0, i), _zcol(hz_hi, 0, i))
        u_n = [0.5 * (1.0 + mn) * fn for mn, fn in zip(mob_n, f_n)]
        srcs[0].append(f1 + cross_rate * (1.0 * _flux(w * f1, u_n, fc)))
        a1 = fa_ref[1, i]
        a_n = _neighbours(a1, _yrow(hy_lo, 1, i), _yrow(hy_hi, 1, i), _zcol(hz_lo, 1, i), _zcol(hz_hi, 1, i))
        srcs[1].append(a1 + cross_rate * (w * _flux(a1, a_n, fc)))
    _local_solves(fac_ref, srcs, loc_ref, vals_ref)


def _gradient_kernel(pore_ref, lab_ref, a2_ref, gy_lo, gy_hi, gz_lo, gz_hi,
                     hy_lo, hy_hi, hz_lo, hz_hi, out_ref):
    m = pore_ref.shape[0]
    for i in range(m):
        mob, _, _, fc = _geo_row(i, pore_ref, lab_ref, gy_lo, gy_hi, gz_lo, gz_hi)
        w = 0.5 * (1.0 + mob)
        a2 = a2_ref[i]
        a_n = _neighbours(a2, _yrow(hy_lo, 0, i), _yrow(hy_hi, 0, i), _zcol(hz_lo, 0, i), _zcol(hz_hi, 0, i))
        out_ref[i] = a2 + cross_rate * (w * _flux(a2, a_n, fc))


def _halo_pairs(axis, periodic):
    count = lax.axis_size(axis)
    forward = [(i, i + 1) for i in range(count - 1)]
    if periodic:
        forward.append((count - 1, 0))
    backward = [(t, s) for s, t in forward]
    return forward, backward


def _exchange(first, last, axis, periodic):
    forward, backward = _halo_pairs(axis, periodic)
    lo = lax.ppermute(last, axis, forward)
    hi = lax.ppermute(first, axis, backward)
    return lo, hi


def _first_call(m, ny, nz):
    return pl.pallas_call(
        _first_kernel,
        out_shape=(
            jax.ShapeDtypeStruct((2, m, ny, nz), F32),
            jax.ShapeDtypeStruct((2, 2, ny, nz), F32),
        ),
        in_specs=[_vmem()] * 9,
        out_specs=(_vmem(), _vmem()),
    )


def _combine_scratch(n, ny, nz):
    return [
        pltpu.VMEM((n, ny, nz), F32),
        pltpu.VMEM((n, 2, 5, ny, nz), F32),
        pltpu.VMEM((n, 2, 2, ny, nz), F32),
    ]


def _gather_blk(x):
    n = lax.axis_size("blk")
    parts = [x]
    for k in range(1, n):
        parts.append(lax.ppermute(x, "blk", [(j, (j + k) % n) for j in range(n)]))
    return parts


def _edge_shapes(chans, m, ny, nz):
    return (
        jax.ShapeDtypeStruct((chans, m, nz), F32),
        jax.ShapeDtypeStruct((chans, m, nz), F32),
        jax.ShapeDtypeStruct((chans, ny, m), F32),
        jax.ShapeDtypeStruct((chans, ny, m), F32),
    )


def _yz_halos(y_first, y_last, z_first, z_last):
    gy_lo, gy_hi = _exchange(y_first, y_last, "gy", False)
    gz_lo, gz_hi = _exchange(z_first, z_last, "gz", False)
    return gy_lo, gy_hi, gz_lo, gz_hi


def _shards(vacancy, grain_label, pore_mask, cotangent):
    m, ny, nz = vacancy.shape
    n_blk = lax.axis_size("blk")
    cycle_step = float((m * n_blk) ** 2 // 64)
    shape = jax.ShapeDtypeStruct((m, ny, nz), F32)

    outs = pl.pallas_call(
        _edge_kernel,
        out_shape=_edge_shapes(3, m, ny, nz) + (jax.ShapeDtypeStruct((2, ny, nz), F32),) * 2,
        in_specs=[_vmem()] * 3,
        out_specs=tuple(_vmem() for _ in range(6)),
    )(vacancy, pore_mask, grain_label)
    bx_lo, bx_hi = _exchange(outs[4], outs[5], "blk", True)
    gy_lo, gy_hi, gz_lo, gz_hi = _yz_halos(*outs[:4])

    fac, lr, rows = pl.pallas_call(
        lambda *r: _factor_kernel(cycle_step, *r),
        out_shape=(
            jax.ShapeDtypeStruct((2, 3, m, ny, nz), F32),
            jax.ShapeDtypeStruct((2, 2, m, ny, nz), F32),
            jax.ShapeDtypeStruct((2, 5, ny, nz), F32),
        ),
        in_specs=[_vmem()] * 4,
        out_specs=(_vmem(), _vmem(), _vmem()),
    )(pore_mask, grain_label, bx_lo, bx_hi)
    gathered = _gather_blk(rows)

    loc, vals = _first_call(m, ny, nz)(
        vacancy, cotangent, pore_mask, grain_label, fac, gy_lo, gy_hi, gz_lo, gz_hi
    )
    gathered1 = _gather_blk(vals)
    pos = jnp.reshape(lax.axis_index("blk"), (1,)).astype(jnp.int32)

    outs = pl.pallas_call(
        lambda *r: _combine_kernel(n_blk, True, {0: 0, 1: 1}, *r),
        out_shape=(jax.ShapeDtypeStruct((2, m, ny, nz), F32),) + _edge_shapes(2, m, ny, nz),
        in_specs=[_smem()] + [_vmem()] * (2 * n_blk + 2),
        out_specs=tuple(_vmem() for _ in range(5)),
        scratch_shapes=_combine_scratch(n_blk, ny, nz),
    )(pos, *gathered, *gathered1, lr, loc)
    fa = outs[0]

    hy_lo, hy_hi, hz_lo, hz_hi = _yz_halos(*outs[1:])
    loc2, vals2 = pl.pallas_call(
        _second_kernel,
        out_shape=(
            jax.ShapeDtypeStruct((2, m, ny, nz), F32),
            jax.ShapeDtypeStruct((2, 2, ny, nz), F32),
        ),
        in_specs=[_vmem()] * 12,
        out_specs=(_vmem(), _vmem()),
    )(pore_mask, grain_label, fa, fac, gy_lo, gy_hi, gz_lo, gz_hi, hy_lo, hy_hi, hz_lo, hz_hi)

    gathered2 = _gather_blk(vals2)
    outs = pl.pallas_call(
        lambda *r: _combine_kernel(n_blk, False, {1: 0}, *r),
        out_shape=(shape, shape) + _edge_shapes(1, m, ny, nz),
        in_specs=[_smem()] + [_vmem()] * (2 * n_blk + 2),
        out_specs=tuple(_vmem() for _ in range(6)),
        scratch_shapes=_combine_scratch(n_blk, ny, nz),
    )(pos, *gathered, *gathered2, lr, loc2)
    final_field, adjoint_two = outs[:2]

    a2_lo, a2_hi, a2z_lo, a2z_hi = _yz_halos(*outs[2:])
    gradient = pl.pallas_call(
        _gradient_kernel,
        out_shape=shape,
        in_specs=[_vmem()] * 11,
        out_specs=_vmem(),
    )(pore_mask, grain_label, adjoint_two, gy_lo, gy_hi, gz_lo, gz_hi, a2_lo, a2_hi, a2z_lo, a2z_hi)
    return (final_field, gradient)


def solution(mesh):
    in_specs = (
        P("blk", "gy", "gz"),
        P("blk", "gy", "gz"),
        P("blk", "gy", "gz"),
        P("blk", "gy", "gz"),
    )
    out_specs = (P("blk", "gy", "gz"), P("blk", "gy", "gz"))
    return jax.shard_map(_shards, mesh=mesh, in_specs=in_specs, out_specs=out_specs, check_vma=False)
```

profile of v0, /device:TPU:4, one launch (start us, length us, event | category | flops | bytes accessed | tf_op | source)
XLA Modules:
  0.0 91.4 jit_solution(13343921846401280478)
XLA Ops:
  0.6 2.5 %shard_map.59 = (f32[3,32,256]{2,1,0:T(8,128)}, f32[3,32,256]{2,1,0:T(8,128)}, f32[3,16,32]{2,1,0:T(8,128)}, f32[3,16,32]{2,1,0:T(8,128)}, f32[2,16,256]{2,1,0:T(8,128)}, /*index=5*/f32[2,16,256]{2,1,0:T(8,128)}) custom-call(f32[32,16,256]{2,1,0:T(8,128)} %vac_ref.3, s32[32,16,256]{2,1,0:T(8,128)} %pore_ref.7, s32[32,16,256]{2,1,0:T(8,128)} %lab_ref.7), custom_call_target="tpu_custom_call" | custom-call | tf_op jit(solution)/shard_map/pallas_call | solution.py:378
  3.1 1.5 %collective-permute-start = (f32[2,16,256]{2,1,0:T(8,128)}, f32[2,16,256]{2,1,0:T(8,128)S(1)}, u32[]{:S(2)}, u32[]{:S(2)}) collective-permute-start(f32[2,16,256]{2,1,0:T(8,128)} %get-tuple-element.26), channel_id=1, source_target_pairs={{0,16},{16,0},{1,17},{17,1},{2,18},{18,2},{3,19},{19,3},{4,20},{20... | collective-permute-start | bytes 98312 | tf_op jit(solution)/shard_map/ppermute | solution.py:324
  4.6 0.5 collective-permute-start.1
  5.1 1.9 %collective-permute-start.3 = (f32[3,32,256]{2,1,0:T(8,128)}, f32[3,32,256]{2,1,0:T(8,128)S(1)}, u32[]{:S(2)}, u32[]{:S(2)}) collective-permute-start(f32[3,32,256]{2,1,0:T(8,128)} %get-tuple-element.30), channel_id=1, source_target_pairs={{0,4},{4,8},{8,12},{1,5},{5,9},{9,13},{2,6},{6,10},{10,14},{3,7},{... | collective-permute-start | bytes 294920 | tf_op jit(solution)/shard_map/ppermute | solution.py:324
  7.0 3.6 %collective-permute-start.4 = (f32[3,32,256]{2,1,0:T(8,128)}, f32[3,32,256]{2,1,0:T(8,128)S(1)}, u32[]{:S(2)}, u32[]{:S(2)}) collective-permute-start(f32[3,32,256]{2,1,0:T(8,128)} %get-tuple-element.31), channel_id=1, source_target_pairs={{4,0},{8,4},{12,8},{5,1},{9,5},{13,9},{6,2},{10,6},{14,10},{7,3},{... | collective-permute-start | bytes 294920 | tf_op jit(solution)/shard_map/ppermute | solution.py:325
  10.7 0.0 collective-permute-done.r_2_
  10.7 0.0 collective-permute-done.1.r_3_
  10.7 0.6 copy-done.11
  11.3 0.6 copy-done.12
  11.9 4.4 %shard_map.60 = (f32[2,3,32,16,256]{4,3,2,1,0:T(8,128)}, f32[2,2,32,16,256]{4,3,2,1,0:T(8,128)}, f32[2,5,16,256]{3,2,1,0:T(8,128)}) custom-call(s32[32,16,256]{2,1,0:T(8,128)} %pore_ref.7, s32[32,16,256]{2,1,0:T(8,128)} %lab_ref.7, f32[2,16,256]{2,1,0:T(8,128)} %copy-done.11, f32[2,16,256]{2,1,0:T(8,128)} %copy-done.12), custom_call_target="tpu_custom_call" | custom-call | tf_op jit(solution)/shard_map/pallas_call | solution.py:387
  16.3 1.5 %collective-permute-start.2 = (f32[2,5,16,256]{3,2,1,0:T(8,128)}, f32[2,5,16,256]{3,2,1,0:T(8,128)S(1)}, u32[]{:S(2)}, u32[]{:S(2)}) collective-permute-start(f32[2,5,16,256]{3,2,1,0:T(8,128)} %get-tuple-element.28.r_1_), channel_id=1, source_target_pairs={{0,16},{16,0},{1,17},{17,1},{2,18},{18,2},{3,19},{19,3},{4,20},{20... | collective-permute-start | bytes 491528 | tf_op jit(solution)/shard_map/ppermute | solution.py:353
  17.8 3.5 %collective-permute-start.5 = (f32[3,16,32]{2,1,0:T(8,128)}, f32[3,16,32]{2,1,0:T(8,128)S(1)}, u32[]{:S(2)}, u32[]{:S(2)}) collective-permute-start(f32[3,16,32]{2,1,0:T(8,128)} %get-tuple-element.32), channel_id=1, source_target_pairs={{0,1},{1,2},{2,3},{4,5},{5,6},{6,7},{8,9},{9,10},{10,11},{12,13},{... | collective-permute-start | bytes 18440 | tf_op jit(solution)/shard_map/ppermute | solution.py:324
  21.3 1.3 %collective-permute-start.6 = (f32[3,16,32]{2,1,0:T(8,128)}, f32[3,16,32]{2,1,0:T(8,128)S(1)}, u32[]{:S(2)}, u32[]{:S(2)}) collective-permute-start(f32[3,16,32]{2,1,0:T(8,128)} %get-tuple-element.33), channel_id=1, source_target_pairs={{1,0},{2,1},{3,2},{5,4},{6,5},{7,6},{9,8},{10,9},{11,10},{13,12},{... | collective-permute-start | bytes 18440 | tf_op jit(solution)/shard_map/ppermute | solution.py:325
  22.6 0.4 collective-permute-done.5.gz_lo
  23.0 4.2 %collective-permute-done.6.gz_hi = f32[3,16,32]{2,1,0:T(8,128)S(1)} collective-permute-done((f32[3,16,32]{2,1,0:T(8,128)}, f32[3,16,32]{2,1,0:T(8,128)S(1)}, u32[]{:S(2)}, u32[]{:S(2)}) %collective-permute-start.6) | collective-permute-done | bytes 6176 | tf_op jit(solution)/shard_map/ppermute | solution.py:325
  27.3 0.6 copy-done.4
  27.8 0.0 copy-done
  27.9 0.1 copy-done.1
  27.9 5.6 %shard_map.61 = (f32[2,32,16,256]{3,2,1,0:T(8,128)}, f32[2,2,16,256]{3,2,1,0:T(8,128)}) custom-call(f32[32,16,256]{2,1,0:T(8,128)} %vac_ref.3, f32[32,16,256]{2,1,0:T(8,128)} %cot_ref.1, s32[32,16,256]{2,1,0:T(8,128)} %pore_ref.7, s32[32,16,256]{2,1,0:T(8,128)} %lab_ref.7, f32[2,3,32,16,256]{4,3,2,1,0:T(8,128)} %get-tuple-element.29.fac_ref, ...), custom_call_target="tpu_custom_call" | custom-call | tf_op jit(solution)/shard_map/pallas_call | solution.py:399
  33.6 0.5 collective-permute-start.7
  34.1 3.9 %collective-permute-done.7.r_4_ = f32[2,2,16,256]{3,2,1,0:T(8,128)S(1)} collective-permute-done((f32[2,2,16,256]{3,2,1,0:T(8,128)}, f32[2,2,16,256]{3,2,1,0:T(8,128)S(1)}, u32[]{:S(2)}, u32[]{:S(2)}) %collective-permute-start.7) | collective-permute-done | bytes 65568 | tf_op jit(solution)/shard_map/ppermute | solution.py:353
  38.0 0.6 copy-done.7
  38.7 0.1 copy-done.2
  38.7 3.4 %shard_map.62 = (f32[2,32,16,256]{3,2,1,0:T(8,128)}, f32[2,32,256]{2,1,0:T(8,128)}, f32[2,32,256]{2,1,0:T(8,128)}, f32[2,16,32]{2,1,0:T(8,128)}, f32[2,16,32]{2,1,0:T(8,128)}) custom-call(s32[1]{0:T(128)} %bitcast.r_0_, f32[2,5,16,256]{3,2,1,0:T(8,128)} %get-tuple-element.28.r_1_, f32[2,5,16,256]{3,2,1,0:T(8,128)} %copy-done.2, ...), custom_call_target="tpu_custom_call" | custom-call | tf_op jit(solution)/shard_map/pallas_call | solution.py:405
  42.2 1.9 %collective-permute-start.8 = (f32[2,32,256]{2,1,0:T(8,128)}, f32[2,32,256]{2,1,0:T(8,128)S(1)}, u32[]{:S(2)}, u32[]{:S(2)}) collective-permute-start(f32[2,32,256]{2,1,0:T(8,128)} %get-tuple-element.38), channel_id=1, source_target_pairs={{0,4},{4,8},{8,12},{1,5},{5,9},{9,13},{2,6},{6,10},{10,14},{3,7},{... | collective-permute-start | bytes 196616 | tf_op jit(solution)/shard_map/ppermute | solution.py:324
  44.1 3.6 %collective-permute-start.9 = (f32[2,32,256]{2,1,0:T(8,128)}, f32[2,32,256]{2,1,0:T(8,128)S(1)}, u32[]{:S(2)}, u32[]{:S(2)}) collective-permute-start(f32[2,32,256]{2,1,0:T(8,128)} %get-tuple-element.39), channel_id=1, source_target_pairs={{4,0},{8,4},{12,8},{5,1},{9,5},{13,9},{6,2},{10,6},{14,10},{7,3},{... | collective-permute-start | bytes 196616 | tf_op jit(solution)/shard_map/ppermute | solution.py:325
  47.7 3.5 %collective-permute-start.10 = (f32[2,16,32]{2,1,0:T(8,128)}, f32[2,16,32]{2,1,0:T(8,128)S(1)}, u32[]{:S(2)}, u32[]{:S(2)}) collective-permute-start(f32[2,16,32]{2,1,0:T(8,128)} %get-tuple-element.40), channel_id=1, source_target_pairs={{0,1},{1,2},{2,3},{4,5},{5,6},{6,7},{8,9},{9,10},{10,11},{12,13},{... | collective-permute-start | bytes 12296 | tf_op jit(solution)/shard_map/ppermute | solution.py:324
  51.2 1.3 %collective-permute-start.11 = (f32[2,16,32]{2,1,0:T(8,128)}, f32[2,16,32]{2,1,0:T(8,128)S(1)}, u32[]{:S(2)}, u32[]{:S(2)}) collective-permute-start(f32[2,16,32]{2,1,0:T(8,128)} %get-tuple-element.41), channel_id=1, source_target_pairs={{1,0},{2,1},{3,2},{5,4},{6,5},{7,6},{9,8},{10,9},{11,10},{13,12},{... | collective-permute-start | bytes 12296 | tf_op jit(solution)/shard_map/ppermute | solution.py:325
  52.5 0.3 collective-permute-done.10.hz_lo
  52.9 4.2 %collective-permute-done.11.hz_hi = f32[2,16,32]{2,1,0:T(8,128)S(1)} collective-permute-done((f32[2,16,32]{2,1,0:T(8,128)}, f32[2,16,32]{2,1,0:T(8,128)S(1)}, u32[]{:S(2)}, u32[]{:S(2)}) %collective-permute-start.11) | collective-permute-done | bytes 4128 | tf_op jit(solution)/shard_map/ppermute | solution.py:325
  57.1 0.6 copy-done.14
  57.7 0.0 copy-done.5
  57.7 0.0 copy-done.6
  57.7 6.0 %shard_map.63 = (f32[2,32,16,256]{3,2,1,0:T(8,128)}, f32[2,2,16,256]{3,2,1,0:T(8,128)}) custom-call(s32[32,16,256]{2,1,0:T(8,128)} %pore_ref.7, s32[32,16,256]{2,1,0:T(8,128)} %lab_ref.7, f32[2,32,16,256]{3,2,1,0:T(8,128)} %get-tuple-element.37.fa_ref, f32[2,3,32,16,256]{4,3,2,1,0:T(8,128)} %get-tuple-element.29.fac_ref, f32[3,32,256]{2,1,0:T(8,128)} %copy-done, ...), custom_call_target="tpu_custom_call" | custom-call | tf_op jit(solution)/shard_map/pallas_call | solution.py:415
  63.8 0.5 collective-permute-start.12
  64.3 3.9 %collective-permute-done.12.r_4_ = f32[2,2,16,256]{3,2,1,0:T(8,128)S(1)} collective-permute-done((f32[2,2,16,256]{3,2,1,0:T(8,128)}, f32[2,2,16,256]{3,2,1,0:T(8,128)S(1)}, u32[]{:S(2)}, u32[]{:S(2)}) %collective-permute-start.12) | collective-permute-done | bytes 65568 | tf_op jit(solution)/shard_map/ppermute | solution.py:353
  68.2 0.6 copy-done.8
  68.9 3.3 %shard_map.64 = (f32[32,16,256]{2,1,0:T(8,128)}, f32[32,16,256]{2,1,0:T(8,128)}, f32[1,32,256]{2,1,0:T(8,128)}, f32[1,32,256]{2,1,0:T(8,128)}, f32[1,16,32]{2,1,0:T(8,128)}, /*index=5*/f32[1,16,32]{2,1,0:T(8,128)}) custom-call(s32[1]{0:T(128)} %bitcast.r_0_, f32[2,5,16,256]{3,2,1,0:T(8,128)} %get-tuple-element.28.r_1_, f32[2,5,16,256]{3,2,1,0:T(8,128)} %copy-done.2, ...), custom_call_target="tpu_custom_call" | custom-call | tf_op jit(solution)/shard_map/pallas_call | solution.py:426
  72.2 1.9 %collective-permute-start.13 = (f32[1,32,256]{2,1,0:T(8,128)}, f32[1,32,256]{2,1,0:T(8,128)S(1)}, u32[]{:S(2)}, u32[]{:S(2)}) collective-permute-start(f32[1,32,256]{2,1,0:T(8,128)} %get-tuple-element.46), channel_id=1, source_target_pairs={{0,4},{4,8},{8,12},{1,5},{5,9},{9,13},{2,6},{6,10},{10,14},{3,7},{... | collective-permute-start | bytes 98312 | tf_op jit(solution)/shard_map/ppermute | solution.py:324
  74.1 3.6 %collective-permute-start.14 = (f32[1,32,256]{2,1,0:T(8,128)}, f32[1,32,256]{2,1,0:T(8,128)S(1)}, u32[]{:S(2)}, u32[]{:S(2)}) collective-permute-start(f32[1,32,256]{2,1,0:T(8,128)} %get-tuple-element.47), channel_id=1, source_target_pairs={{4,0},{8,4},{12,8},{5,1},{9,5},{13,9},{6,2},{10,6},{14,10},{7,3},{... | collective-permute-start | bytes 98312 | tf_op jit(solution)/shard_map/ppermute | solution.py:325
  77.7 3.5 %collective-permute-start.15 = (f32[1,16,32]{2,1,0:T(8,128)}, f32[1,16,32]{2,1,0:T(8,128)S(1)}, u32[]{:S(2)}, u32[]{:S(2)}) collective-permute-start(f32[1,16,32]{2,1,0:T(8,128)} %get-tuple-element.48), channel_id=1, source_target_pairs={{0,1},{1,2},{2,3},{4,5},{5,6},{6,7},{8,9},{9,10},{10,11},{12,13},{... | collective-permute-start | bytes 6152 | tf_op jit(solution)/shard_map/ppermute | solution.py:324
  81.2 1.3 %collective-permute-start.16 = (f32[1,16,32]{2,1,0:T(8,128)}, f32[1,16,32]{2,1,0:T(8,128)S(1)}, u32[]{:S(2)}, u32[]{:S(2)}) collective-permute-start(f32[1,16,32]{2,1,0:T(8,128)} %get-tuple-element.49), channel_id=1, source_target_pairs={{1,0},{2,1},{3,2},{5,4},{6,5},{7,6},{9,8},{10,9},{11,10},{13,12},{... | collective-permute-start | bytes 6152 | tf_op jit(solution)/shard_map/ppermute | solution.py:325
  82.5 0.3 collective-permute-done.15.hz_lo
  82.8 4.2 %collective-permute-done.16.hz_hi = f32[1,16,32]{2,1,0:T(8,128)S(1)} collective-permute-done((f32[1,16,32]{2,1,0:T(8,128)}, f32[1,16,32]{2,1,0:T(8,128)S(1)}, u32[]{:S(2)}, u32[]{:S(2)}) %collective-permute-start.16) | collective-permute-done | bytes 2080 | tf_op jit(solution)/shard_map/ppermute | solution.py:325
  87.0 0.6 copy-done.16
  87.6 0.0 copy-done.9
  87.6 0.0 copy-done.10
  87.6 3.8 %shard_map.65 = f32[32,16,256]{2,1,0:T(8,128)} custom-call(s32[32,16,256]{2,1,0:T(8,128)} %pore_ref.7, s32[32,16,256]{2,1,0:T(8,128)} %lab_ref.7, f32[32,16,256]{2,1,0:T(8,128)} %get-tuple-element.45.a2_ref, f32[3,32,256]{2,1,0:T(8,128)} %copy-done, f32[3,32,256]{2,1,0:T(8,128)} %copy-done.1, f32[3,16,32]{2,1,0:T(8,128)} %copy-done.3, ...), custom_call_target="tpu_custom_call" | custom-call | tf_op jit(solution)/shard_map/pallas_call | solution.py:436
  (27 shorter events, 0.1 us)
Async XLA Ops:
  3.1 7.6 %collective-permute-start = (f32[2,16,256]{2,1,0:T(8,128)}, f32[2,16,256]{2,1,0:T(8,128)S(1)}, u32[]{:S(2)}, u32[]{:S(2)}) collective-permute-start(f32[2,16,256]{2,1,0:T(8,128)} %get-tuple-element.26), channel_id=1, source_target_pairs={{0,16},{16,0},{1,17},{17,1},{2,18},{18,2},{3,19},{19,3},{4,20},{20... | collective-permute-start | bytes 98312 | tf_op jit(solution)/shard_map/ppermute | solution.py:324
  4.6 6.1 %collective-permute-start.1 = (f32[2,16,256]{2,1,0:T(8,128)}, f32[2,16,256]{2,1,0:T(8,128)S(1)}, u32[]{:S(2)}, u32[]{:S(2)}) collective-permute-start(f32[2,16,256]{2,1,0:T(8,128)} %get-tuple-element.27), channel_id=1, source_target_pairs={{16,0},{0,16},{17,1},{1,17},{18,2},{2,18},{19,3},{3,19},{20,4},{4,... | collective-permute-start | bytes 98312 | tf_op jit(solution)/shard_map/ppermute | solution.py:325
  5.1 22.1 %collective-permute-start.3 = (f32[3,32,256]{2,1,0:T(8,128)}, f32[3,32,256]{2,1,0:T(8,128)S(1)}, u32[]{:S(2)}, u32[]{:S(2)}) collective-permute-start(f32[3,32,256]{2,1,0:T(8,128)} %get-tuple-element.30), channel_id=1, source_target_pairs={{0,4},{4,8},{8,12},{1,5},{5,9},{9,13},{2,6},{6,10},{10,14},{3,7},{... | collective-permute-start | bytes 294920 | tf_op jit(solution)/shard_map/ppermute | solution.py:324
  7.0 20.2 %collective-permute-start.4 = (f32[3,32,256]{2,1,0:T(8,128)}, f32[3,32,256]{2,1,0:T(8,128)S(1)}, u32[]{:S(2)}, u32[]{:S(2)}) collective-permute-start(f32[3,32,256]{2,1,0:T(8,128)} %get-tuple-element.31), channel_id=1, source_target_pairs={{4,0},{8,4},{12,8},{5,1},{9,5},{13,9},{6,2},{10,6},{14,10},{7,3},{... | collective-permute-start | bytes 294920 | tf_op jit(solution)/shard_map/ppermute | solution.py:325
  10.7 0.6 copy-start.11
  11.3 0.6 copy-start.12
  16.3 21.7 %collective-permute-start.2 = (f32[2,5,16,256]{3,2,1,0:T(8,128)}, f32[2,5,16,256]{3,2,1,0:T(8,128)S(1)}, u32[]{:S(2)}, u32[]{:S(2)}) collective-permute-start(f32[2,5,16,256]{3,2,1,0:T(8,128)} %get-tuple-element.28.r_1_), channel_id=1, source_target_pairs={{0,16},{16,0},{1,17},{17,1},{2,18},{18,2},{3,19},{19,3},{4,20},{20... | collective-permute-start | bytes 491528 | tf_op jit(solution)/shard_map/ppermute | solution.py:353
  17.8 5.2 %collective-permute-start.5 = (f32[3,16,32]{2,1,0:T(8,128)}, f32[3,16,32]{2,1,0:T(8,128)S(1)}, u32[]{:S(2)}, u32[]{:S(2)}) collective-permute-start(f32[3,16,32]{2,1,0:T(8,128)} %get-tuple-element.32), channel_id=1, source_target_pairs={{0,1},{1,2},{2,3},{4,5},{5,6},{6,7},{8,9},{9,10},{10,11},{12,13},{... | collective-permute-start | bytes 18440 | tf_op jit(solution)/shard_map/ppermute | solution.py:324
  21.3 5.9 %collective-permute-start.6 = (f32[3,16,32]{2,1,0:T(8,128)}, f32[3,16,32]{2,1,0:T(8,128)S(1)}, u32[]{:S(2)}, u32[]{:S(2)}) collective-permute-start(f32[3,16,32]{2,1,0:T(8,128)} %get-tuple-element.33), channel_id=1, source_target_pairs={{1,0},{2,1},{3,2},{5,4},{6,5},{7,6},{9,8},{10,9},{11,10},{13,12},{... | collective-permute-start | bytes 18440 | tf_op jit(solution)/shard_map/ppermute | solution.py:325
  23.0 4.2 %copy-start.3 = (f32[3,16,32]{2,1,0:T(8,128)}, f32[3,16,32]{2,1,0:T(8,128)S(1)}, u32[]{:S(2)}) copy-start(f32[3,16,32]{2,1,0:T(8,128)S(1)} %collective-permute-done.5.gz_lo) | copy-start | bytes 18436
  27.2 0.6 copy-start.4
  27.2 0.6 copy-start
  27.2 0.7 copy-start.1
  33.6 4.5 %collective-permute-start.7 = (f32[2,2,16,256]{3,2,1,0:T(8,128)}, f32[2,2,16,256]{3,2,1,0:T(8,128)S(1)}, u32[]{:S(2)}, u32[]{:S(2)}) collective-permute-start(f32[2,2,16,256]{3,2,1,0:T(8,128)} %get-tuple-element.34.r_3_), channel_id=1, source_target_pairs={{0,16},{16,0},{1,17},{17,1},{2,18},{18,2},{3,19},{19,3},{4,20},{20... | collective-permute-start | bytes 196616 | tf_op jit(solution)/shard_map/ppermute | solution.py:353
  38.0 0.6 copy-start.7
  38.0 0.7 copy-start.2
  42.2 14.9 %collective-permute-start.8 = (f32[2,32,256]{2,1,0:T(8,128)}, f32[2,32,256]{2,1,0:T(8,128)S(1)}, u32[]{:S(2)}, u32[]{:S(2)}) collective-permute-start(f32[2,32,256]{2,1,0:T(8,128)} %get-tuple-element.38), channel_id=1, source_target_pairs={{0,4},{4,8},{8,12},{1,5},{5,9},{9,13},{2,6},{6,10},{10,14},{3,7},{... | collective-permute-start | bytes 196616 | tf_op jit(solution)/shard_map/ppermute | solution.py:324
  44.1 13.0 %collective-permute-start.9 = (f32[2,32,256]{2,1,0:T(8,128)}, f32[2,32,256]{2,1,0:T(8,128)S(1)}, u32[]{:S(2)}, u32[]{:S(2)}) collective-permute-start(f32[2,32,256]{2,1,0:T(8,128)} %get-tuple-element.39), channel_id=1, source_target_pairs={{4,0},{8,4},{12,8},{5,1},{9,5},{13,9},{6,2},{10,6},{14,10},{7,3},{... | collective-permute-start | bytes 196616 | tf_op jit(solution)/shard_map/ppermute | solution.py:325
  47.7 5.1 %collective-permute-start.10 = (f32[2,16,32]{2,1,0:T(8,128)}, f32[2,16,32]{2,1,0:T(8,128)S(1)}, u32[]{:S(2)}, u32[]{:S(2)}) collective-permute-start(f32[2,16,32]{2,1,0:T(8,128)} %get-tuple-element.40), channel_id=1, source_target_pairs={{0,1},{1,2},{2,3},{4,5},{5,6},{6,7},{8,9},{9,10},{10,11},{12,13},{... | collective-permute-start | bytes 12296 | tf_op jit(solution)/shard_map/ppermute | solution.py:324
  51.2 5.8 %collective-permute-start.11 = (f32[2,16,32]{2,1,0:T(8,128)}, f32[2,16,32]{2,1,0:T(8,128)S(1)}, u32[]{:S(2)}, u32[]{:S(2)}) collective-permute-start(f32[2,16,32]{2,1,0:T(8,128)} %get-tuple-element.41), channel_id=1, source_target_pairs={{1,0},{2,1},{3,2},{5,4},{6,5},{7,6},{9,8},{10,9},{11,10},{13,12},{... | collective-permute-start | bytes 12296 | tf_op jit(solution)/shard_map/ppermute | solution.py:325
  52.9 4.2 %copy-start.13 = (f32[2,16,32]{2,1,0:T(8,128)}, f32[2,16,32]{2,1,0:T(8,128)S(1)}, u32[]{:S(2)}) copy-start(f32[2,16,32]{2,1,0:T(8,128)S(1)} %collective-permute-done.10.hz_lo) | copy-start | bytes 12292
  57.1 0.6 copy-start.14
  57.1 0.6 copy-start.5
  57.1 0.6 copy-start.6
  63.8 4.5 %collective-permute-start.12 = (f32[2,2,16,256]{3,2,1,0:T(8,128)}, f32[2,2,16,256]{3,2,1,0:T(8,128)S(1)}, u32[]{:S(2)}, u32[]{:S(2)}) collective-permute-start(f32[2,2,16,256]{3,2,1,0:T(8,128)} %get-tuple-element.42.r_3_), channel_id=1, source_target_pairs={{0,16},{16,0},{1,17},{17,1},{2,18},{18,2},{3,19},{19,3},{4,20},{20... | collective-permute-start | bytes 196616 | tf_op jit(solution)/shard_map/ppermute | solution.py:353
  68.2 0.6 copy-start.8
  72.2 14.8 %collective-permute-start.13 = (f32[1,32,256]{2,1,0:T(8,128)}, f32[1,32,256]{2,1,0:T(8,128)S(1)}, u32[]{:S(2)}, u32[]{:S(2)}) collective-permute-start(f32[1,32,256]{2,1,0:T(8,128)} %get-tuple-element.46), channel_id=1, source_target_pairs={{0,4},{4,8},{8,12},{1,5},{5,9},{9,13},{2,6},{6,10},{10,14},{3,7},{... | collective-permute-start | bytes 98312 | tf_op jit(solution)/shard_map/ppermute | solution.py:324
  74.1 12.9 %collective-permute-start.14 = (f32[1,32,256]{2,1,0:T(8,128)}, f32[1,32,256]{2,1,0:T(8,128)S(1)}, u32[]{:S(2)}, u32[]{:S(2)}) collective-permute-start(f32[1,32,256]{2,1,0:T(8,128)} %get-tuple-element.47), channel_id=1, source_target_pairs={{4,0},{8,4},{12,8},{5,1},{9,5},{13,9},{6,2},{10,6},{14,10},{7,3},{... | collective-permute-start | bytes 98312 | tf_op jit(solution)/shard_map/ppermute | solution.py:325
  77.7 5.1 %collective-permute-start.15 = (f32[1,16,32]{2,1,0:T(8,128)}, f32[1,16,32]{2,1,0:T(8,128)S(1)}, u32[]{:S(2)}, u32[]{:S(2)}) collective-permute-start(f32[1,16,32]{2,1,0:T(8,128)} %get-tuple-element.48), channel_id=1, source_target_pairs={{0,1},{1,2},{2,3},{4,5},{5,6},{6,7},{8,9},{9,10},{10,11},{12,13},{... | collective-permute-start | bytes 6152 | tf_op jit(solution)/shard_map/ppermute | solution.py:324
  81.2 5.8 %collective-permute-start.16 = (f32[1,16,32]{2,1,0:T(8,128)}, f32[1,16,32]{2,1,0:T(8,128)S(1)}, u32[]{:S(2)}, u32[]{:S(2)}) collective-permute-start(f32[1,16,32]{2,1,0:T(8,128)} %get-tuple-element.49), channel_id=1, source_target_pairs={{1,0},{2,1},{3,2},{5,4},{6,5},{7,6},{9,8},{10,9},{11,10},{13,12},{... | collective-permute-start | bytes 6152 | tf_op jit(solution)/shard_map/ppermute | solution.py:325
  82.8 4.2 %copy-start.15 = (f32[1,16,32]{2,1,0:T(8,128)}, f32[1,16,32]{2,1,0:T(8,128)S(1)}, u32[]{:S(2)}) copy-start(f32[1,16,32]{2,1,0:T(8,128)S(1)} %collective-permute-done.15.hz_lo) | copy-start | bytes 6148
  87.0 0.6 copy-start.16
  87.0 0.6 copy-start.9
  87.0 0.6 copy-start.10
where the time goes:
time: 91.9 us; the launch traced here: 91.4 us
  starting transfers between devices  35.5 us (39%)
  Pallas kernels  29.1 us (32%)
  waiting for transfers between devices  21.5 us (23%)
  local copies, waits for them, and re-layouts  4.38 us (5%)
    ppermute x7, starting transfers between devices, _exchange(): lo = lax.ppermute(last, axis, forward)  17.7 us
    ppermute x7, starting transfers between devices, _exchange(): hi = lax.ppermute(first, axis, backward)  15.3 us
    ppermute x7, waiting for transfers between devices, _exchange(): hi = lax.ppermute(first, axis, backward)  12.6 us
    ppermute x3, waiting for transfers between devices, _gather_blk(): parts.append(lax.ppermute(x, 'blk', [(j, (j + k) % n) for j in range(n)]))  7.88 us
    pallas_call x1, Pallas kernels, _shards(): pl.pallas_call(_second_kernel, out_shape=(jax.ShapeDtypeStruct((2, m, ny,...  6.04 us
    pallas_call x1, Pallas kernels, _shards(): _first_call(m, ny, nz)  5.64 us
    pallas_call x1, Pallas kernels, _shards(): pl.pallas_call(lambda *r: _factor_kernel(cycle_step, *r), out_shape=(jax....  4.45 us
    unnamed x34, local copies, waits for them, and re-layouts  4.38 us
  transfers between devices with their start and end apart: 17, of which 8 were waited for; matrix products, arithmetic and copies ran while one was open for 0% of the time, Pallas kernels for 11%

commit v1 on v0

--- a/solution.py
+++ b/solution.py
@@ -69,13 +69,38 @@
     return ref[c, :, pl.ds(i, 1)]
 
 
-def _write_edges(edges, c, r, val):
-    y_first, y_last, z_first, z_last = edges
+def _write_edges(edges, c, r, val, par):
+    y_a, y_b, z_a, z_b = edges
+    even_y, even_z = par
     ny, nz = val.shape
-    y_first[c, pl.ds(r, 1), :] = val[0:1, :]
-    y_last[c, pl.ds(r, 1), :] = val[ny - 1 : ny, :]
-    z_first[c, :, pl.ds(r, 1)] = val[:, 0:1]
-    z_last[c, :, pl.ds(r, 1)] = val[:, nz - 1 : nz]
+    y_first, y_last = val[0:1, :], val[ny - 1 : ny, :]
+    z_first, z_last = val[:, 0:1], val[:, nz - 1 : nz]
+    y_a[c, pl.ds(r, 1), :] = jnp.where(even_y, y_last, y_first)
+    y_b[c, pl.ds(r, 1), :] = jnp.where(even_y, y_first, y_last)
+    z_a[c, :, pl.ds(r, 1)] = jnp.where(even_z, z_last, z_first)
+    z_b[c, :, pl.ds(r, 1)] = jnp.where(even_z, z_first, z_last)
+
+
+class _Pick:
+    def __init__(self, a, b, use_b):
+        self.a, self.b, self.use_b = a, b, use_b
+
+    def __getitem__(self, idx):
+        return jnp.where(self.use_b, self.b[idx], self.a[idx])
+
+
+def _parity(ctl_ref):
+    return ctl_ref[1] == 1, ctl_ref[2] == 1
+
+
+def _picks(ctl_ref, y_a, y_b, z_a, z_b):
+    even_y, even_z = _parity(ctl_ref)
+    return (
+        _Pick(y_a, y_b, even_y),
+        _Pick(y_a, y_b, jnp.logical_not(even_y)),
+        _Pick(z_a, z_b, even_z),
+        _Pick(z_a, z_b, jnp.logical_not(even_z)),
+    )
 
 
 def _geo_row(i, pore_ref, lab_ref, gy_lo, gy_hi, gz_lo, gz_hi):
@@ -112,7 +137,8 @@
     return xs
 
 
-def _factor_kernel(cs, pore_ref, lab_ref, bx_lo, bx_hi, fac_ref, lr_ref, rows_ref):
+def _factor_kernel(cs, lo_i, hi_i, pore_ref, lab_ref, bx_ref, fac_ref, lr_ref, rows_ref):
+    bx_lo, bx_hi = bx_ref.at[lo_i], bx_ref.at[hi_i]
     m = pore_ref.shape[0]
     zero = jnp.zeros(pore_ref.shape[1:], F32)
     mobs = [1.0 + 2.0 * pore_ref[r].astype(F32) for r in range(m)]
@@ -235,23 +261,23 @@
             val = loc_ref[c, r] - lr_ref[c, 0, r] * prior - lr_ref[c, 1, r] * own
             outs[c][r] = val
             if c in edge_of:
-                _write_edges(edges, edge_of[c], r, val)
-
-
-def _edge_kernel(vac_ref, pore_ref, lab_ref, y_first, y_last, z_first, z_last, bx_first, bx_last):
+                _write_edges(edges, edge_of[c], r, val, _parity(pos_ref))
+
+
+def _edge_kernel(ctl_ref, vac_ref, pore_ref, lab_ref, y_first, y_last, z_first, z_last, bx_ref):
     m = vac_ref.shape[0]
     edges = (y_first, y_last, z_first, z_last)
     for r in range(m):
         mob = 1.0 + 2.0 * pore_ref[r].astype(F32)
         lab = lab_ref[r].astype(F32)
         for c, val in enumerate((mob, lab, vac_ref[r])):
-            _write_edges(edges, c, r, val)
+            _write_edges(edges, c, r, val, _parity(ctl_ref))
         if r == 0:
-            bx_first[0] = mob
-            bx_first[1] = lab
+            bx_ref[0, 0] = mob
+            bx_ref[0, 1] = lab
         if r == m - 1:
-            bx_last[0] = mob
-            bx_last[1] = lab
+            bx_ref[1, 0] = mob
+            bx_ref[1, 1] = lab
 
 
 def _local_solves(fac_ref, srcs, loc_ref, vals_ref):
@@ -269,7 +295,8 @@
         vals_ref[c, 1] = local[0]
 
 
-def _first_kernel(vac_ref, cot_ref, pore_ref, lab_ref, fac_ref, gy_lo, gy_hi, gz_lo, gz_hi, loc_ref, vals_ref):
+def _first_kernel(ctl_ref, vac_ref, cot_ref, pore_ref, lab_ref, fac_ref, gy_lo, gy_hi, gz_lo, gz_hi, loc_ref, vals_ref):
+    gy_lo, gy_hi, gz_lo, gz_hi = _picks(ctl_ref, gy_lo, gy_hi, gz_lo, gz_hi)
     m = pore_ref.shape[0]
     srcs = ([], [cot_ref[r] for r in range(m)])
     for i in range(m):
@@ -282,8 +309,10 @@
     _local_solves(fac_ref, srcs, loc_ref, vals_ref)
 
 
-def _second_kernel(pore_ref, lab_ref, fa_ref, fac_ref, gy_lo, gy_hi, gz_lo, gz_hi,
+def _second_kernel(ctl_ref, pore_ref, lab_ref, fa_ref, fac_ref, gy_lo, gy_hi, gz_lo, gz_hi,
                    hy_lo, hy_hi, hz_lo, hz_hi, loc_ref, vals_ref):
+    gy_lo, gy_hi, gz_lo, gz_hi = _picks(ctl_ref, gy_lo, gy_hi, gz_lo, gz_hi)
+    hy_lo, hy_hi, hz_lo, hz_hi = _picks(ctl_ref, hy_lo, hy_hi, hz_lo, hz_hi)
     m = pore_ref.shape[0]
     srcs = ([], [])
     for i in range(m):
@@ -299,8 +328,10 @@
     _local_solves(fac_ref, srcs, loc_ref, vals_ref)
 
 
-def _gradient_kernel(pore_ref, lab_ref, a2_ref, gy_lo, gy_hi, gz_lo, gz_hi,
+def _gradient_kernel(ctl_ref, pore_ref, lab_ref, a2_ref, gy_lo, gy_hi, gz_lo, gz_hi,
                      hy_lo, hy_hi, hz_lo, hz_hi, out_ref):
+    gy_lo, gy_hi, gz_lo, gz_hi = _picks(ctl_ref, gy_lo, gy_hi, gz_lo, gz_hi)
+    hy_lo, hy_hi, hz_lo, hz_hi = _picks(ctl_ref, hy_lo, hy_hi, hz_lo, hz_hi)
     m = pore_ref.shape[0]
     for i in range(m):
         mob, _, _, fc = _geo_row(i, pore_ref, lab_ref, gy_lo, gy_hi, gz_lo, gz_hi)
@@ -333,7 +364,7 @@
             jax.ShapeDtypeStruct((2, m, ny, nz), F32),
             jax.ShapeDtypeStruct((2, 2, ny, nz), F32),
         ),
-        in_specs=[_vmem()] * 9,
+        in_specs=[_smem()] + [_vmem()] * 9,
         out_specs=(_vmem(), _vmem()),
     )
 
@@ -363,10 +394,17 @@
     )
 
 
-def _yz_halos(y_first, y_last, z_first, z_last):
-    gy_lo, gy_hi = _exchange(y_first, y_last, "gy", False)
-    gz_lo, gz_hi = _exchange(z_first, z_last, "gz", False)
-    return gy_lo, gy_hi, gz_lo, gz_hi
+def _swap(x_a, x_b, axis):
+    n = lax.axis_size(axis)
+    pairs_a = [(i, i ^ 1) for i in range(n) if i ^ 1 < n]
+    pairs_b = [(i, i + 1) for i in range(1, n - 1, 2)] + [(i + 1, i) for i in range(1, n - 1, 2)]
+    recv_a = lax.ppermute(x_a, axis, pairs_a)
+    recv_b = lax.ppermute(x_b, axis, pairs_b) if pairs_b else jnp.zeros_like(x_b)
+    return recv_a, recv_b
+
+
+def _yz_halos(y_a, y_b, z_a, z_b):
+    return _swap(y_a, y_b, "gy") + _swap(z_a, z_b, "gz")
 
 
 def _shards(vacancy, grain_label, pore_mask, cotangent):
@@ -375,32 +413,41 @@
     cycle_step = float((m * n_blk) ** 2 // 64)
     shape = jax.ShapeDtypeStruct((m, ny, nz), F32)
 
+    ctl = jnp.stack(
+        [lax.axis_index("blk"), 1 - lax.axis_index("gy") % 2, 1 - lax.axis_index("gz") % 2]
+    ).astype(jnp.int32)
     outs = pl.pallas_call(
         _edge_kernel,
-        out_shape=_edge_shapes(3, m, ny, nz) + (jax.ShapeDtypeStruct((2, ny, nz), F32),) * 2,
-        in_specs=[_vmem()] * 3,
-        out_specs=tuple(_vmem() for _ in range(6)),
-    )(vacancy, pore_mask, grain_label)
-    bx_lo, bx_hi = _exchange(outs[4], outs[5], "blk", True)
+        out_shape=_edge_shapes(3, m, ny, nz) + (jax.ShapeDtypeStruct((2, 2, ny, nz), F32),),
+        in_specs=[_smem()] + [_vmem()] * 3,
+        out_specs=tuple(_vmem() for _ in range(5)),
+    )(ctl, vacancy, pore_mask, grain_label)
+    if n_blk == 2:
+        bx = lax.ppermute(outs[4], "blk", [(0, 1), (1, 0)])
+        lo_i, hi_i = 1, 0
+    else:
+        bx_lo, bx_hi = _exchange(outs[4][0], outs[4][1], "blk", True)
+        bx = jnp.stack([bx_lo, bx_hi])
+        lo_i, hi_i = 0, 1
     gy_lo, gy_hi, gz_lo, gz_hi = _yz_halos(*outs[:4])
 
     fac, lr, rows = pl.pallas_call(
-        lambda *r: _factor_kernel(cycle_step, *r),
+        lambda *r: _factor_kernel(cycle_step, lo_i, hi_i, *r),
         out_shape=(
             jax.ShapeDtypeStruct((2, 3, m, ny, nz), F32),
             jax.ShapeDtypeStruct((2, 2, m, ny, nz), F32),
             jax.ShapeDtypeStruct((2, 5, ny, nz), F32),
         ),
-        in_specs=[_vmem()] * 4,
+        in_specs=[_vmem()] * 3,
         out_specs=(_vmem(), _vmem(), _vmem()),
-    )(pore_mask, grain_label, bx_lo, bx_hi)
+    )(pore_mask, grain_label, bx)
     gathered = _gather_blk(rows)
 
     loc, vals = _first_call(m, ny, nz)(
-        vacancy, cotangent, pore_mask, grain_label, fac, gy_lo, gy_hi, gz_lo, gz_hi
+        ctl, vacancy, cotangent, pore_mask, grain_label, fac, gy_lo, gy_hi, gz_lo, gz_hi
     )
     gathered1 = _gather_blk(vals)
-    pos = jnp.reshape(lax.axis_index("blk"), (1,)).astype(jnp.int32)
+    pos = ctl
 
     outs = pl.pallas_call(
         lambda *r: _combine_kernel(n_blk, True, {0: 0, 1: 1}, *r),
@@ -418,9 +465,9 @@
             jax.ShapeDtypeStruct((2, m, ny, nz), F32),
             jax.ShapeDtypeStruct((2, 2, ny, nz), F32),
         ),
-        in_specs=[_vmem()] * 12,
+        in_specs=[_smem()] + [_vmem()] * 12,
         out_specs=(_vmem(), _vmem()),
-    )(pore_mask, grain_label, fa, fac, gy_lo, gy_hi, gz_lo, gz_hi, hy_lo, hy_hi, hz_lo, hz_hi)
+    )(ctl, pore_mask, grain_label, fa, fac, gy_lo, gy_hi, gz_lo, gz_hi, hy_lo, hy_hi, hz_lo, hz_hi)
 
     gathered2 = _gather_blk(vals2)
     outs = pl.pallas_call(
@@ -436,9 +483,9 @@
     gradient = pl.pallas_call(
         _gradient_kernel,
         out_shape=shape,
-        in_specs=[_vmem()] * 11,
+        in_specs=[_smem()] + [_vmem()] * 11,
         out_specs=_vmem(),
-    )(pore_mask, grain_label, adjoint_two, gy_lo, gy_hi, gz_lo, gz_hi, a2_lo, a2_hi, a2z_lo, a2z_hi)
+    )(ctl, pore_mask, grain_label, adjoint_two, gy_lo, gy_hi, gz_lo, gz_hi, a2_lo, a2_hi, a2z_lo, a2z_hi)
     return (final_field, gradient)
 
 
@@ -450,4 +497,7 @@
         P("blk", "gy", "gz"),
     )
     out_specs = (P("blk", "gy", "gz"), P("blk", "gy", "gz"))
-    return jax.shard_map(_shards, mesh=mesh, in_specs=in_specs, out_specs=out_specs, check_vma=False)
+    fn = jax.shard_map(_shards, mesh=mesh, in_specs=in_specs, out_specs=out_specs, check_vma=False)
+    if mesh.shape["blk"] > 4:
+        return fn
+    return fn

time: 91.9 us -> 92 us (level)
  the two profiles are of different devices: /device:TPU:4 before, /device:TPU:17 now
where the time goes in v1:
time: 92 us; the launch traced here: 91.7 us
  Pallas kernels  47.2 us (51%)
  starting transfers between devices  25.5 us (28%)
  waiting for transfers between devices  13.7 us (15%)
  local copies, waits for them, and re-layouts  3.82 us (4%)
    ppermute x6, starting transfers between devices, _swap(): lax.ppermute(x_b, axis, pairs_b)  16.6 us
    pallas_call x1, Pallas kernels, _shards(): pl.pallas_call(_edge_kernel, out_shape=_edge_shapes(3, m, ny, nz) + (jax....  13.2 us
    pallas_call x1, Pallas kernels, _shards(): pl.pallas_call(lambda *r: _combine_kernel(n_blk, True, {0: 0, 1: 1}, *r),...  9.14 us
    ppermute x6, waiting for transfers between devices, _swap(): lax.ppermute(x_b, axis, pairs_b)  6.46 us
    pallas_call x1, Pallas kernels, _shards(): pl.pallas_call(_second_kernel, out_shape=(jax.ShapeDtypeStruct((2, m, ny,...  6.14 us
    ppermute x6, starting transfers between devices, _swap(): recv_a = lax.ppermute(x_a, axis, pairs_a)  6.04 us
    pallas_call x1, Pallas kernels, _shards(): _first_call(m, ny, nz)  5.73 us
    ppermute x3, waiting for transfers between devices, _gather_blk(): parts.append(lax.ppermute(x, 'blk', [(j, (j + k) % n) for j in range(n)]))  5.3 us
  transfers between devices with their start and end apart: 16, of which 7 were waited for; matrix products, arithmetic and copies ran while one was open for 0% of the time, Pallas kernels for 11%

profile of v1, /device:TPU:17, one launch (start us, length us, event | category | flops | bytes accessed | tf_op | source)
XLA Modules:
  0.0 91.7 jit_solution(16352676582875294583)
XLA Ops:
  0.6 0.6 pad_add_fusion.ctl_ref.r_0_
  1.3 13.2 %shard_map.59 = (f32[3,32,256]{2,1,0:T(8,128)}, f32[3,32,256]{2,1,0:T(8,128)}, f32[3,16,32]{2,1,0:T(8,128)}, f32[3,16,32]{2,1,0:T(8,128)}, f32[2,2,16,256]{3,2,1,0:T(8,128)}) custom-call(s32[3]{0:T(128)} %pad_add_fusion.ctl_ref.r_0_, f32[32,16,256]{2,1,0:T(8,128)} %vac_ref.3, s32[32,16,256]{2,1,0:T(8,128)} %pore_ref.7, s32[32,16,256]{2,1,0:T(8,128)} %lab_ref.7), custom_call_target="tpu_custom_call" | custom-call | tf_op jit(solution)/shard_map/pallas_call | solution.py:419
  14.5 1.2 %collective-permute-start = (f32[2,2,16,256]{3,2,1,0:T(8,128)}, f32[2,2,16,256]{3,2,1,0:T(8,128)S(1)}, u32[]{:S(2)}, u32[]{:S(2)}) collective-permute-start(f32[2,2,16,256]{3,2,1,0:T(8,128)} %get-tuple-element.25), channel_id=1, source_target_pairs={{0,16},{16,0},{1,17},{17,1},{2,18},{18,2},{3,19},{19,3},{4,20},{20... | collective-permute-start | bytes 196616 | tf_op jit(solution)/shard_map/ppermute | solution.py:426
  15.7 1.0 %collective-permute-start.2 = (f32[3,32,256]{2,1,0:T(8,128)}, f32[3,32,256]{2,1,0:T(8,128)S(1)}, u32[]{:S(2)}, u32[]{:S(2)}) collective-permute-start(f32[3,32,256]{2,1,0:T(8,128)} %get-tuple-element.28), channel_id=1, source_target_pairs={{0,4},{4,0},{8,12},{12,8},{1,5},{5,1},{9,13},{13,9},{2,6},{6,2},{1... | collective-permute-start | bytes 294920 | tf_op jit(solution)/shard_map/ppermute | solution.py:401
  16.7 3.0 %collective-permute-start.3 = (f32[3,32,256]{2,1,0:T(8,128)}, f32[3,32,256]{2,1,0:T(8,128)S(1)}, u32[]{:S(2)}, u32[]{:S(2)}) collective-permute-start(f32[3,32,256]{2,1,0:T(8,128)} %get-tuple-element.29), channel_id=1, source_target_pairs={{4,8},{8,4},{5,9},{9,5},{6,10},{10,6},{7,11},{11,7},{20,24},{24,20... | collective-permute-start | bytes 294920 | tf_op jit(solution)/shard_map/ppermute | solution.py:402
  19.7 0.0 collective-permute-done.r_2_
  19.7 0.6 copy-done.9
  20.3 4.4 %shard_map.60 = (f32[2,3,32,16,256]{4,3,2,1,0:T(8,128)}, f32[2,2,32,16,256]{4,3,2,1,0:T(8,128)}, f32[2,5,16,256]{3,2,1,0:T(8,128)}) custom-call(s32[32,16,256]{2,1,0:T(8,128)} %pore_ref.7, s32[32,16,256]{2,1,0:T(8,128)} %lab_ref.7, f32[2,2,16,256]{3,2,1,0:T(8,128)} %copy-done.9), custom_call_target="tpu_custom_call" | custom-call | tf_op jit(solution)/shard_map/pallas_call | solution.py:434
  24.8 0.3 collective-permute-start.1
  25.0 1.3 %collective-permute-start.4 = (f32[3,16,32]{2,1,0:T(8,128)}, f32[3,16,32]{2,1,0:T(8,128)S(1)}, u32[]{:S(2)}, u32[]{:S(2)}) collective-permute-start(f32[3,16,32]{2,1,0:T(8,128)} %get-tuple-element.30), channel_id=1, source_target_pairs={{0,1},{1,0},{2,3},{3,2},{4,5},{5,4},{6,7},{7,6},{8,9},{9,8},{10,11... | collective-permute-start | bytes 18440 | tf_op jit(solution)/shard_map/ppermute | solution.py:401
  26.3 1.9 %collective-permute-start.5 = (f32[3,16,32]{2,1,0:T(8,128)}, f32[3,16,32]{2,1,0:T(8,128)S(1)}, u32[]{:S(2)}, u32[]{:S(2)}) collective-permute-start(f32[3,16,32]{2,1,0:T(8,128)} %get-tuple-element.31), channel_id=1, source_target_pairs={{1,2},{2,1},{5,6},{6,5},{9,10},{10,9},{13,14},{14,13},{17,18},{18,... | collective-permute-start | bytes 18440 | tf_op jit(solution)/shard_map/ppermute | solution.py:402
  28.3 0.0 collective-permute-done.4.gz_lo
  28.3 2.9 %collective-permute-done.5.gz_hi = f32[3,16,32]{2,1,0:T(8,128)S(1)} collective-permute-done((f32[3,16,32]{2,1,0:T(8,128)}, f32[3,16,32]{2,1,0:T(8,128)S(1)}, u32[]{:S(2)}, u32[]{:S(2)}) %collective-permute-start.5) | collective-permute-done | bytes 6176 | tf_op jit(solution)/shard_map/ppermute | solution.py:402
  31.2 0.0 collective-permute-done.2.gy_lo
  31.3 0.6 copy-done.4
  31.8 0.1 copy-done
  31.9 0.0 copy-done.1
  31.9 5.7 %shard_map.61 = (f32[2,32,16,256]{3,2,1,0:T(8,128)}, f32[2,2,16,256]{3,2,1,0:T(8,128)}) custom-call(s32[3]{0:T(128)} %pad_add_fusion.ctl_ref.r_0_, f32[32,16,256]{2,1,0:T(8,128)} %vac_ref.3, f32[32,16,256]{2,1,0:T(8,128)} %cot_ref.1, s32[32,16,256]{2,1,0:T(8,128)} %pore_ref.7, s32[32,16,256]{2,1,0:T(8,128)} %lab_ref.7, ...), custom_call_target="tpu_custom_call" | custom-call | tf_op jit(solution)/shard_map/pallas_call | solution.py:446
  37.6 1.1 %collective-permute-start.6 = (f32[2,2,16,256]{3,2,1,0:T(8,128)}, f32[2,2,16,256]{3,2,1,0:T(8,128)S(1)}, u32[]{:S(2)}, u32[]{:S(2)}) collective-permute-start(f32[2,2,16,256]{3,2,1,0:T(8,128)} %get-tuple-element.32.r_3_), channel_id=1, source_target_pairs={{0,16},{16,0},{1,17},{17,1},{2,18},{18,2},{3,19},{19,3},{4,20},{20... | collective-permute-start | bytes 196616 | tf_op jit(solution)/shard_map/ppermute | solution.py:384
  38.7 2.2 %collective-permute-done.6.r_4_ = f32[2,2,16,256]{3,2,1,0:T(8,128)S(1)} collective-permute-done((f32[2,2,16,256]{3,2,1,0:T(8,128)}, f32[2,2,16,256]{3,2,1,0:T(8,128)S(1)}, u32[]{:S(2)}, u32[]{:S(2)}) %collective-permute-start.6) | collective-permute-done | bytes 65568 | tf_op jit(solution)/shard_map/ppermute | solution.py:384
  41.0 0.6 copy-done.7
  41.6 0.1 copy-done.2
  41.7 9.1 %shard_map.62 = (f32[2,32,16,256]{3,2,1,0:T(8,128)}, f32[2,32,256]{2,1,0:T(8,128)}, f32[2,32,256]{2,1,0:T(8,128)}, f32[2,16,32]{2,1,0:T(8,128)}, f32[2,16,32]{2,1,0:T(8,128)}) custom-call(s32[3]{0:T(128)} %pad_add_fusion.ctl_ref.r_0_, f32[2,5,16,256]{3,2,1,0:T(8,128)} %get-tuple-element.26.r_1_, f32[2,5,16,256]{3,2,1,0:T(8,128)} %copy-done.2, ...), custom_call_target="tpu_custom_call" | custom-call | tf_op jit(solution)/shard_map/pallas_call | solution.py:452
  50.8 3.6 %collective-permute-start.7 = (f32[2,32,256]{2,1,0:T(8,128)}, f32[2,32,256]{2,1,0:T(8,128)S(1)}, u32[]{:S(2)}, u32[]{:S(2)}) collective-permute-start(f32[2,32,256]{2,1,0:T(8,128)} %get-tuple-element.36), channel_id=1, source_target_pairs={{0,4},{4,0},{8,12},{12,8},{1,5},{5,1},{9,13},{13,9},{2,6},{6,2},{1... | collective-permute-start | bytes 196616 | tf_op jit(solution)/shard_map/ppermute | solution.py:401
  54.4 3.0 %collective-permute-start.8 = (f32[2,32,256]{2,1,0:T(8,128)}, f32[2,32,256]{2,1,0:T(8,128)S(1)}, u32[]{:S(2)}, u32[]{:S(2)}) collective-permute-start(f32[2,32,256]{2,1,0:T(8,128)} %get-tuple-element.37), channel_id=1, source_target_pairs={{4,8},{8,4},{5,9},{9,5},{6,10},{10,6},{7,11},{11,7},{20,24},{24,20... | collective-permute-start | bytes 196616 | tf_op jit(solution)/shard_map/ppermute | solution.py:402
  57.5 0.1 collective-permute-start.9
  57.6 1.9 %collective-permute-start.10 = (f32[2,16,32]{2,1,0:T(8,128)}, f32[2,16,32]{2,1,0:T(8,128)S(1)}, u32[]{:S(2)}, u32[]{:S(2)}) collective-permute-start(f32[2,16,32]{2,1,0:T(8,128)} %get-tuple-element.39), channel_id=1, source_target_pairs={{1,2},{2,1},{5,6},{6,5},{9,10},{10,9},{13,14},{14,13},{17,18},{18,... | collective-permute-start | bytes 12296 | tf_op jit(solution)/shard_map/ppermute | solution.py:402
  59.5 1.2 %collective-permute-done.9.hz_lo = f32[2,16,32]{2,1,0:T(8,128)S(1)} collective-permute-done((f32[2,16,32]{2,1,0:T(8,128)}, f32[2,16,32]{2,1,0:T(8,128)S(1)}, u32[]{:S(2)}, u32[]{:S(2)}) %collective-permute-start.9) | collective-permute-done | bytes 4128 | tf_op jit(solution)/shard_map/ppermute | solution.py:401
  60.7 1.6 %collective-permute-done.10.hz_hi = f32[2,16,32]{2,1,0:T(8,128)S(1)} collective-permute-done((f32[2,16,32]{2,1,0:T(8,128)}, f32[2,16,32]{2,1,0:T(8,128)S(1)}, u32[]{:S(2)}, u32[]{:S(2)}) %collective-permute-start.10) | collective-permute-done | bytes 4128 | tf_op jit(solution)/shard_map/ppermute | solution.py:402
  62.3 0.0 collective-permute-done.7.hy_lo
  62.3 0.0 collective-permute-done.8.hy_hi
  62.3 0.6 copy-done.13
  62.9 0.0 copy-done.5
  62.9 0.0 copy-done.6
  62.9 6.1 %shard_map.63 = (f32[2,32,16,256]{3,2,1,0:T(8,128)}, f32[2,2,16,256]{3,2,1,0:T(8,128)}) custom-call(s32[3]{0:T(128)} %pad_add_fusion.ctl_ref.r_0_, s32[32,16,256]{2,1,0:T(8,128)} %pore_ref.7, s32[32,16,256]{2,1,0:T(8,128)} %lab_ref.7, f32[2,32,16,256]{3,2,1,0:T(8,128)} %get-tuple-element.35.fa_ref, f32[2,3,32,16,256]{4,3,2,1,0:T(8,128)} %get-tuple-element.27.fac_ref, ...), custom_call_target="tpu_custom_call" | custom-call | tf_op jit(solution)/shard_map/pallas_call | solution.py:462
  69.1 0.3 collective-permute-start.11
  69.3 3.1 %collective-permute-done.11.r_4_ = f32[2,2,16,256]{3,2,1,0:T(8,128)S(1)} collective-permute-done((f32[2,2,16,256]{3,2,1,0:T(8,128)}, f32[2,2,16,256]{3,2,1,0:T(8,128)S(1)}, u32[]{:S(2)}, u32[]{:S(2)}) %collective-permute-start.11) | collective-permute-done | bytes 65568 | tf_op jit(solution)/shard_map/ppermute | solution.py:384
  72.4 0.6 copy-done.8
  73.0 4.6 %shard_map.64 = (f32[32,16,256]{2,1,0:T(8,128)}, f32[32,16,256]{2,1,0:T(8,128)}, f32[1,32,256]{2,1,0:T(8,128)}, f32[1,32,256]{2,1,0:T(8,128)}, f32[1,16,32]{2,1,0:T(8,128)}, /*index=5*/f32[1,16,32]{2,1,0:T(8,128)}) custom-call(s32[3]{0:T(128)} %pad_add_fusion.ctl_ref.r_0_, f32[2,5,16,256]{3,2,1,0:T(8,128)} %get-tuple-element.26.r_1_, ...), custom_call_target="tpu_custom_call" | custom-call | tf_op jit(solution)/shard_map/pallas_call | solution.py:473
  77.6 4.8 %collective-permute-start.13 = (f32[1,32,256]{2,1,0:T(8,128)}, f32[1,32,256]{2,1,0:T(8,128)S(1)}, u32[]{:S(2)}, u32[]{:S(2)}) collective-permute-start(f32[1,32,256]{2,1,0:T(8,128)} %get-tuple-element.45), channel_id=1, source_target_pairs={{4,8},{8,4},{5,9},{9,5},{6,10},{10,6},{7,11},{11,7},{20,24},{24,20... | collective-permute-start | bytes 98312 | tf_op jit(solution)/shard_map/ppermute | solution.py:402
  82.4 0.1 collective-permute-start.14
  82.5 1.9 %collective-permute-start.15 = (f32[1,16,32]{2,1,0:T(8,128)}, f32[1,16,32]{2,1,0:T(8,128)S(1)}, u32[]{:S(2)}, u32[]{:S(2)}) collective-permute-start(f32[1,16,32]{2,1,0:T(8,128)} %get-tuple-element.47), channel_id=1, source_target_pairs={{1,2},{2,1},{5,6},{6,5},{9,10},{10,9},{13,14},{14,13},{17,18},{18,... | collective-permute-start | bytes 6152 | tf_op jit(solution)/shard_map/ppermute | solution.py:402
  84.4 0.8 collective-permute-done.14.hz_lo
  85.2 1.9 %collective-permute-done.15.hz_hi = f32[1,16,32]{2,1,0:T(8,128)S(1)} collective-permute-done((f32[1,16,32]{2,1,0:T(8,128)}, f32[1,16,32]{2,1,0:T(8,128)S(1)}, u32[]{:S(2)}, u32[]{:S(2)}) %collective-permute-start.15) | collective-permute-done | bytes 2080 | tf_op jit(solution)/shard_map/ppermute | solution.py:402
  87.1 0.6 copy-done.15
  87.7 0.0 copy-done.10
  87.7 0.0 copy-done.11
  87.7 3.9 %shard_map.65 = f32[32,16,256]{2,1,0:T(8,128)} custom-call(s32[3]{0:T(128)} %pad_add_fusion.ctl_ref.r_0_, s32[32,16,256]{2,1,0:T(8,128)} %pore_ref.7, s32[32,16,256]{2,1,0:T(8,128)} %lab_ref.7, f32[32,16,256]{2,1,0:T(8,128)} %get-tuple-element.43.a2_ref, f32[3,32,256]{2,1,0:T(8,128)} %copy-done, f32[3,32,256]{2,1,0:T(8,128)} %copy-done.1, ...), custom_call_target="tpu_custom_call" | custom-call | tf_op jit(solution)/shard_map/pallas_call | solution.py:483
  (24 shorter events, 0.0 us)
Async XLA Ops:
  14.5 5.2 %collective-permute-start = (f32[2,2,16,256]{3,2,1,0:T(8,128)}, f32[2,2,16,256]{3,2,1,0:T(8,128)S(1)}, u32[]{:S(2)}, u32[]{:S(2)}) collective-permute-start(f32[2,2,16,256]{3,2,1,0:T(8,128)} %get-tuple-element.25), channel_id=1, source_target_pairs={{0,16},{16,0},{1,17},{17,1},{2,18},{18,2},{3,19},{19,3},{4,20},{20... | collective-permute-start | bytes 196616 | tf_op jit(solution)/shard_map/ppermute | solution.py:426
  15.7 15.5 %collective-permute-start.2 = (f32[3,32,256]{2,1,0:T(8,128)}, f32[3,32,256]{2,1,0:T(8,128)S(1)}, u32[]{:S(2)}, u32[]{:S(2)}) collective-permute-start(f32[3,32,256]{2,1,0:T(8,128)} %get-tuple-element.28), channel_id=1, source_target_pairs={{0,4},{4,0},{8,12},{12,8},{1,5},{5,1},{9,13},{13,9},{2,6},{6,2},{1... | collective-permute-start | bytes 294920 | tf_op jit(solution)/shard_map/ppermute | solution.py:401
  16.7 14.5 %collective-permute-start.3 = (f32[3,32,256]{2,1,0:T(8,128)}, f32[3,32,256]{2,1,0:T(8,128)S(1)}, u32[]{:S(2)}, u32[]{:S(2)}) collective-permute-start(f32[3,32,256]{2,1,0:T(8,128)} %get-tuple-element.29), channel_id=1, source_target_pairs={{4,8},{8,4},{5,9},{9,5},{6,10},{10,6},{7,11},{11,7},{20,24},{24,20... | collective-permute-start | bytes 294920 | tf_op jit(solution)/shard_map/ppermute | solution.py:402
  19.7 0.6 copy-start.9
  24.8 16.2 %collective-permute-start.1 = (f32[2,5,16,256]{3,2,1,0:T(8,128)}, f32[2,5,16,256]{3,2,1,0:T(8,128)S(1)}, u32[]{:S(2)}, u32[]{:S(2)}) collective-permute-start(f32[2,5,16,256]{3,2,1,0:T(8,128)} %get-tuple-element.26.r_1_), channel_id=1, source_target_pairs={{0,16},{16,0},{1,17},{17,1},{2,18},{18,2},{3,19},{19,3},{4,20},{20... | collective-permute-start | bytes 491528 | tf_op jit(solution)/shard_map/ppermute | solution.py:384
  25.0 3.2 %collective-permute-start.4 = (f32[3,16,32]{2,1,0:T(8,128)}, f32[3,16,32]{2,1,0:T(8,128)S(1)}, u32[]{:S(2)}, u32[]{:S(2)}) collective-permute-start(f32[3,16,32]{2,1,0:T(8,128)} %get-tuple-element.30), channel_id=1, source_target_pairs={{0,1},{1,0},{2,3},{3,2},{4,5},{5,4},{6,7},{7,6},{8,9},{9,8},{10,11... | collective-permute-start | bytes 18440 | tf_op jit(solution)/shard_map/ppermute | solution.py:401
  26.3 4.9 %collective-permute-start.5 = (f32[3,16,32]{2,1,0:T(8,128)}, f32[3,16,32]{2,1,0:T(8,128)S(1)}, u32[]{:S(2)}, u32[]{:S(2)}) collective-permute-start(f32[3,16,32]{2,1,0:T(8,128)} %get-tuple-element.31), channel_id=1, source_target_pairs={{1,2},{2,1},{5,6},{6,5},{9,10},{10,9},{13,14},{14,13},{17,18},{18,... | collective-permute-start | bytes 18440 | tf_op jit(solution)/shard_map/ppermute | solution.py:402
  28.3 3.0 %copy-start.3 = (f32[3,16,32]{2,1,0:T(8,128)}, f32[3,16,32]{2,1,0:T(8,128)S(1)}, u32[]{:S(2)}) copy-start(f32[3,16,32]{2,1,0:T(8,128)S(1)} %collective-permute-done.4.gz_lo) | copy-start | bytes 18436
  31.2 0.6 copy-start.4
  31.2 0.6 copy-start
  31.2 0.7 copy-start.1
  37.6 3.3 %collective-permute-start.6 = (f32[2,2,16,256]{3,2,1,0:T(8,128)}, f32[2,2,16,256]{3,2,1,0:T(8,128)S(1)}, u32[]{:S(2)}, u32[]{:S(2)}) collective-permute-start(f32[2,2,16,256]{3,2,1,0:T(8,128)} %get-tuple-element.32.r_3_), channel_id=1, source_target_pairs={{0,16},{16,0},{1,17},{17,1},{2,18},{18,2},{3,19},{19,3},{4,20},{20... | collective-permute-start | bytes 196616 | tf_op jit(solution)/shard_map/ppermute | solution.py:384
  41.0 0.6 copy-start.7
  41.0 0.7 copy-start.2
  50.8 11.5 %collective-permute-start.7 = (f32[2,32,256]{2,1,0:T(8,128)}, f32[2,32,256]{2,1,0:T(8,128)S(1)}, u32[]{:S(2)}, u32[]{:S(2)}) collective-permute-start(f32[2,32,256]{2,1,0:T(8,128)} %get-tuple-element.36), channel_id=1, source_target_pairs={{0,4},{4,0},{8,12},{12,8},{1,5},{5,1},{9,13},{13,9},{2,6},{6,2},{1... | collective-permute-start | bytes 196616 | tf_op jit(solution)/shard_map/ppermute | solution.py:401
  54.4 7.8 %collective-permute-start.8 = (f32[2,32,256]{2,1,0:T(8,128)}, f32[2,32,256]{2,1,0:T(8,128)S(1)}, u32[]{:S(2)}, u32[]{:S(2)}) collective-permute-start(f32[2,32,256]{2,1,0:T(8,128)} %get-tuple-element.37), channel_id=1, source_target_pairs={{4,8},{8,4},{5,9},{9,5},{6,10},{10,6},{7,11},{11,7},{20,24},{24,20... | collective-permute-start | bytes 196616 | tf_op jit(solution)/shard_map/ppermute | solution.py:402
  57.5 3.2 %collective-permute-start.9 = (f32[2,16,32]{2,1,0:T(8,128)}, f32[2,16,32]{2,1,0:T(8,128)S(1)}, u32[]{:S(2)}, u32[]{:S(2)}) collective-permute-start(f32[2,16,32]{2,1,0:T(8,128)} %get-tuple-element.38), channel_id=1, source_target_pairs={{0,1},{1,0},{2,3},{3,2},{4,5},{5,4},{6,7},{7,6},{8,9},{9,8},{10,11... | collective-permute-start | bytes 12296 | tf_op jit(solution)/shard_map/ppermute | solution.py:401
  57.6 4.7 %collective-permute-start.10 = (f32[2,16,32]{2,1,0:T(8,128)}, f32[2,16,32]{2,1,0:T(8,128)S(1)}, u32[]{:S(2)}, u32[]{:S(2)}) collective-permute-start(f32[2,16,32]{2,1,0:T(8,128)} %get-tuple-element.39), channel_id=1, source_target_pairs={{1,2},{2,1},{5,6},{6,5},{9,10},{10,9},{13,14},{14,13},{17,18},{18,... | collective-permute-start | bytes 12296 | tf_op jit(solution)/shard_map/ppermute | solution.py:402
  60.6 1.6 %copy-start.12 = (f32[2,16,32]{2,1,0:T(8,128)}, f32[2,16,32]{2,1,0:T(8,128)S(1)}, u32[]{:S(2)}) copy-start(f32[2,16,32]{2,1,0:T(8,128)S(1)} %collective-permute-done.9.hz_lo) | copy-start | bytes 12292
  62.3 0.6 copy-start.13
  62.3 0.6 copy-start.5
  62.3 0.6 copy-start.6
  69.1 3.3 %collective-permute-start.11 = (f32[2,2,16,256]{3,2,1,0:T(8,128)}, f32[2,2,16,256]{3,2,1,0:T(8,128)S(1)}, u32[]{:S(2)}, u32[]{:S(2)}) collective-permute-start(f32[2,2,16,256]{3,2,1,0:T(8,128)} %get-tuple-element.40.r_3_), channel_id=1, source_target_pairs={{0,16},{16,0},{1,17},{17,1},{2,18},{18,2},{3,19},{19,3},{4,20},{20... | collective-permute-start | bytes 196616 | tf_op jit(solution)/shard_map/ppermute | solution.py:384
  72.4 0.6 copy-start.8
  77.6 9.5 %collective-permute-start.12 = (f32[1,32,256]{2,1,0:T(8,128)}, f32[1,32,256]{2,1,0:T(8,128)S(1)}, u32[]{:S(2)}, u32[]{:S(2)}) collective-permute-start(f32[1,32,256]{2,1,0:T(8,128)} %get-tuple-element.44), channel_id=1, source_target_pairs={{0,4},{4,0},{8,12},{12,8},{1,5},{5,1},{9,13},{13,9},{2,6},{6,2},{1... | collective-permute-start | bytes 98312 | tf_op jit(solution)/shard_map/ppermute | solution.py:401
  77.6 9.5 %collective-permute-start.13 = (f32[1,32,256]{2,1,0:T(8,128)}, f32[1,32,256]{2,1,0:T(8,128)S(1)}, u32[]{:S(2)}, u32[]{:S(2)}) collective-permute-start(f32[1,32,256]{2,1,0:T(8,128)} %get-tuple-element.45), channel_id=1, source_target_pairs={{4,8},{8,4},{5,9},{9,5},{6,10},{10,6},{7,11},{11,7},{20,24},{24,20... | collective-permute-start | bytes 98312 | tf_op jit(solution)/shard_map/ppermute | solution.py:402
  82.4 2.8 %collective-permute-start.14 = (f32[1,16,32]{2,1,0:T(8,128)}, f32[1,16,32]{2,1,0:T(8,128)S(1)}, u32[]{:S(2)}, u32[]{:S(2)}) collective-permute-start(f32[1,16,32]{2,1,0:T(8,128)} %get-tuple-element.46), channel_id=1, source_target_pairs={{0,1},{1,0},{2,3},{3,2},{4,5},{5,4},{6,7},{7,6},{8,9},{9,8},{10,11... | collective-permute-start | bytes 6152 | tf_op jit(solution)/shard_map/ppermute | solution.py:401
  82.5 4.6 %collective-permute-start.15 = (f32[1,16,32]{2,1,0:T(8,128)}, f32[1,16,32]{2,1,0:T(8,128)S(1)}, u32[]{:S(2)}, u32[]{:S(2)}) collective-permute-start(f32[1,16,32]{2,1,0:T(8,128)} %get-tuple-element.47), channel_id=1, source_target_pairs={{1,2},{2,1},{5,6},{6,5},{9,10},{10,9},{13,14},{14,13},{17,18},{18,... | collective-permute-start | bytes 6152 | tf_op jit(solution)/shard_map/ppermute | solution.py:402
  85.2 1.9 %copy-start.14 = (f32[1,16,32]{2,1,0:T(8,128)}, f32[1,16,32]{2,1,0:T(8,128)S(1)}, u32[]{:S(2)}) copy-start(f32[1,16,32]{2,1,0:T(8,128)S(1)} %collective-permute-done.14.hz_lo) | copy-start | bytes 6148
  87.1 0.6 copy-start.15
  87.1 0.6 copy-start.10
  87.1 0.6 copy-start.11

commit v2 on v1

--- a/solution.py
+++ b/solution.py
@@ -69,16 +69,39 @@
     return ref[c, :, pl.ds(i, 1)]
 
 
-def _write_edges(edges, c, r, val, par):
-    y_a, y_b, z_a, z_b = edges
+def _write_edges(edges, c, r, val):
+    y_first, y_last, z_first, z_last = edges
+    ny, nz = val.shape
+    y_first[c, pl.ds(r, 1), :] = val[0:1, :]
+    y_last[c, pl.ds(r, 1), :] = val[ny - 1 : ny, :]
+    z_first[c, :, pl.ds(r, 1)] = val[:, 0:1]
+    z_last[c, :, pl.ds(r, 1)] = val[:, nz - 1 : nz]
+
+
+def _flush_edges(scratch, outs, par):
+    y_first, y_last, z_first, z_last = scratch
+    y_a, y_b, z_a, z_b = outs
     even_y, even_z = par
-    ny, nz = val.shape
-    y_first, y_last = val[0:1, :], val[ny - 1 : ny, :]
-    z_first, z_last = val[:, 0:1], val[:, nz - 1 : nz]
-    y_a[c, pl.ds(r, 1), :] = jnp.where(even_y, y_last, y_first)
-    y_b[c, pl.ds(r, 1), :] = jnp.where(even_y, y_first, y_last)
-    z_a[c, :, pl.ds(r, 1)] = jnp.where(even_z, z_last, z_first)
-    z_b[c, :, pl.ds(r, 1)] = jnp.where(even_z, z_first, z_last)
+    for even, first, last, out_a, out_b in ((even_y, y_first, y_last, y_a, y_b), (even_z, z_first, z_last, z_a, z_b)):
+
+        @pl.when(even)
+        def _():
+            out_a[...] = last[...]
+            out_b[...] = first[...]
+
+        @pl.when(jnp.logical_not(even))
+        def _():
+            out_a[...] = first[...]
+            out_b[...] = last[...]
+
+
+def _edge_scratch(chans, m, ny, nz):
+    return [
+        pltpu.VMEM((chans, m, nz), F32),
+        pltpu.VMEM((chans, m, nz), F32),
+        pltpu.VMEM((chans, ny, m), F32),
+        pltpu.VMEM((chans, ny, m), F32),
+    ]
 
 
 class _Pick:
@@ -245,7 +268,8 @@
     else:
         outs = refs[:2]
         rest = refs[2:]
-    edges, sep_ref, gs_ref, gv_ref = rest[:4], rest[4], rest[5], rest[6]
+    edge_outs, sep_ref, gs_ref, gv_ref = rest[:4], rest[4], rest[5], rest[6]
+    edges = rest[7:11]
     for k in range(n):
         gs_ref[k] = gs_parts[k][...]
         gv_ref[k] = gv_parts[k][...]
@@ -261,23 +285,24 @@
             val = loc_ref[c, r] - lr_ref[c, 0, r] * prior - lr_ref[c, 1, r] * own
             outs[c][r] = val
             if c in edge_of:
-                _write_edges(edges, edge_of[c], r, val, _parity(pos_ref))
-
-
-def _edge_kernel(ctl_ref, vac_ref, pore_ref, lab_ref, y_first, y_last, z_first, z_last, bx_ref):
+                _write_edges(edges, edge_of[c], r, val)
+    _flush_edges(edges, edge_outs, _parity(pos_ref))
+
+
+def _edge_kernel(ctl_ref, vac_ref, pore_ref, lab_ref, y_a, y_b, z_a, z_b, bx_ref, *edges):
     m = vac_ref.shape[0]
-    edges = (y_first, y_last, z_first, z_last)
     for r in range(m):
         mob = 1.0 + 2.0 * pore_ref[r].astype(F32)
         lab = lab_ref[r].astype(F32)
         for c, val in enumerate((mob, lab, vac_ref[r])):
-            _write_edges(edges, c, r, val, _parity(ctl_ref))
+            _write_edges(edges, c, r, val)
         if r == 0:
             bx_ref[0, 0] = mob
             bx_ref[0, 1] = lab
         if r == m - 1:
             bx_ref[1, 0] = mob
             bx_ref[1, 1] = lab
+    _flush_edges(edges, (y_a, y_b, z_a, z_b), _parity(ctl_ref))
 
 
 def _local_solves(fac_ref, srcs, loc_ref, vals_ref):
@@ -421,6 +446,7 @@
         out_shape=_edge_shapes(3, m, ny, nz) + (jax.ShapeDtypeStruct((2, 2, ny, nz), F32),),
         in_specs=[_smem()] + [_vmem()] * 3,
         out_specs=tuple(_vmem() for _ in range(5)),
+        scratch_shapes=_edge_scratch(3, m, ny, nz),
     )(ctl, vacancy, pore_mask, grain_label)
     if n_blk == 2:
         bx = lax.ppermute(outs[4], "blk", [(0, 1), (1, 0)])
@@ -454,7 +480,7 @@
         out_shape=(jax.ShapeDtypeStruct((2, m, ny, nz), F32),) + _edge_shapes(2, m, ny, nz),
         in_specs=[_smem()] + [_vmem()] * (2 * n_blk + 2),
         out_specs=tuple(_vmem() for _ in range(5)),
-        scratch_shapes=_combine_scratch(n_blk, ny, nz),
+        scratch_shapes=_combine_scratch(n_blk, ny, nz) + _edge_scratch(2, m, ny, nz),
     )(pos, *gathered, *gathered1, lr, loc)
     fa = outs[0]
 
@@ -475,7 +501,7 @@
         out_shape=(shape, shape) + _edge_shapes(1, m, ny, nz),
         in_specs=[_smem()] + [_vmem()] * (2 * n_blk + 2),
         out_specs=tuple(_vmem() for _ in range(6)),
-        scratch_shapes=_combine_scratch(n_blk, ny, nz),
+        scratch_shapes=_combine_scratch(n_blk, ny, nz) + _edge_scratch(1, m, ny, nz),
     )(pos, *gathered, *gathered2, lr, loc2)
     final_field, adjoint_two = outs[:2]
 

time: 92 us -> 74.6 us (0.81)
  Pallas kernels: 47.2 us -> 29.9 us
    pallas_call x1, Pallas kernels: 13.2 us -> 2.57 us  [_shards(): pl.pallas_call(_edge_kernel, out_shape=_edge_shapes(3, m, ny, nz) + (jax....]
    pallas_call x1, Pallas kernels: 9.14 us -> 3.55 us  [_shards(): pl.pallas_call(lambda *r: _combine_kernel(n_blk, True, {0: 0, 1: 1}, *r),...]
    pallas_call x1, Pallas kernels: 4.56 us -> 3.48 us  [_shards(): pl.pallas_call(lambda *r: _combine_kernel(n_blk, False, {1: 0}, *r), out_...]
  transfers between devices with their start and end apart: 16 -> 16, of which waited for: 7 -> 7; matrix products, arithmetic and copies ran while one was open for 0% -> 0% of each run, Pallas kernels for 11% -> 14%
where the time goes in v2:
time: 74.6 us; the launch traced here: 74.3 us
  Pallas kernels  29.9 us (40%)
  starting transfers between devices  25.5 us (34%)
  waiting for transfers between devices  13.7 us (18%)
  local copies, waits for them, and re-layouts  3.82 us (5%)
  between operations  0.83 us (1%)
    ppermute x6, starting transfers between devices, _swap(): lax.ppermute(x_b, axis, pairs_b)  16.6 us
    ppermute x6, waiting for transfers between devices, _swap(): lax.ppermute(x_b, axis, pairs_b)  6.46 us
    pallas_call x1, Pallas kernels, _shards(): pl.pallas_call(_second_kernel, out_shape=(jax.ShapeDtypeStruct((2, m, ny,...  6.14 us
    ppermute x6, starting transfers between devices, _swap(): recv_a = lax.ppermute(x_a, axis, pairs_a)  6.03 us
    pallas_call x1, Pallas kernels, _shards(): _first_call(m, ny, nz)  5.73 us
    ppermute x3, waiting for transfers between devices, _gather_blk(): parts.append(lax.ppermute(x, 'blk', [(j, (j + k) % n) for j in range(n)]))  5.3 us
    pallas_call x1, Pallas kernels, _shards(): pl.pallas_call(lambda *r: _factor_kernel(cycle_step, lo_i, hi_i, *r), out...  4.45 us
    pallas_call x1, Pallas kernels, _shards(): pl.pallas_call(_gradient_kernel, out_shape=shape, in_specs=[_smem()] + [_...  3.95 us
  transfers between devices with their start and end apart: 16, of which 7 were waited for; matrix products, arithmetic and copies ran while one was open for 0% of the time, Pallas kernels for 14%

profile of v2, /device:TPU:17, one launch (start us, length us, event | category | flops | bytes accessed | tf_op | source)
XLA Modules:
  0.0 74.3 jit_solution(7040475609753416489)
XLA Ops:
  0.6 0.6 pad_add_fusion.ctl_ref.r_0_
  1.3 2.6 %shard_map.59 = (f32[3,32,256]{2,1,0:T(8,128)}, f32[3,32,256]{2,1,0:T(8,128)}, f32[3,16,32]{2,1,0:T(8,128)}, f32[3,16,32]{2,1,0:T(8,128)}, f32[2,2,16,256]{3,2,1,0:T(8,128)}) custom-call(s32[3]{0:T(128)} %pad_add_fusion.ctl_ref.r_0_, f32[32,16,256]{2,1,0:T(8,128)} %vac_ref.3, s32[32,16,256]{2,1,0:T(8,128)} %pore_ref.7, s32[32,16,256]{2,1,0:T(8,128)} %lab_ref.7), custom_call_target="tpu_custom_call" | custom-call | tf_op jit(solution)/shard_map/pallas_call | solution.py:444
  3.9 1.2 %collective-permute-start = (f32[2,2,16,256]{3,2,1,0:T(8,128)}, f32[2,2,16,256]{3,2,1,0:T(8,128)S(1)}, u32[]{:S(2)}, u32[]{:S(2)}) collective-permute-start(f32[2,2,16,256]{3,2,1,0:T(8,128)} %get-tuple-element.25), channel_id=1, source_target_pairs={{0,16},{16,0},{1,17},{17,1},{2,18},{18,2},{3,19},{19,3},{4,20},{20... | collective-permute-start | bytes 196616 | tf_op jit(solution)/shard_map/ppermute | solution.py:452
  5.1 0.9 %collective-permute-start.2 = (f32[3,32,256]{2,1,0:T(8,128)}, f32[3,32,256]{2,1,0:T(8,128)S(1)}, u32[]{:S(2)}, u32[]{:S(2)}) collective-permute-start(f32[3,32,256]{2,1,0:T(8,128)} %get-tuple-element.28), channel_id=1, source_target_pairs={{0,4},{4,0},{8,12},{12,8},{1,5},{5,1},{9,13},{13,9},{2,6},{6,2},{1... | collective-permute-start | bytes 294920 | tf_op jit(solution)/shard_map/ppermute | solution.py:426
  6.0 3.0 %collective-permute-start.3 = (f32[3,32,256]{2,1,0:T(8,128)}, f32[3,32,256]{2,1,0:T(8,128)S(1)}, u32[]{:S(2)}, u32[]{:S(2)}) collective-permute-start(f32[3,32,256]{2,1,0:T(8,128)} %get-tuple-element.29), channel_id=1, source_target_pairs={{4,8},{8,4},{5,9},{9,5},{6,10},{10,6},{7,11},{11,7},{20,24},{24,20... | collective-permute-start | bytes 294920 | tf_op jit(solution)/shard_map/ppermute | solution.py:427
  9.1 0.0 collective-permute-done.r_2_
  9.1 0.6 copy-done.9
  9.7 4.4 %shard_map.60 = (f32[2,3,32,16,256]{4,3,2,1,0:T(8,128)}, f32[2,2,32,16,256]{4,3,2,1,0:T(8,128)}, f32[2,5,16,256]{3,2,1,0:T(8,128)}) custom-call(s32[32,16,256]{2,1,0:T(8,128)} %pore_ref.7, s32[32,16,256]{2,1,0:T(8,128)} %lab_ref.7, f32[2,2,16,256]{3,2,1,0:T(8,128)} %copy-done.9), custom_call_target="tpu_custom_call" | custom-call | tf_op jit(solution)/shard_map/pallas_call | solution.py:460
  14.1 0.3 collective-permute-start.1
  14.4 1.3 %collective-permute-start.4 = (f32[3,16,32]{2,1,0:T(8,128)}, f32[3,16,32]{2,1,0:T(8,128)S(1)}, u32[]{:S(2)}, u32[]{:S(2)}) collective-permute-start(f32[3,16,32]{2,1,0:T(8,128)} %get-tuple-element.30), channel_id=1, source_target_pairs={{0,1},{1,0},{2,3},{3,2},{4,5},{5,4},{6,7},{7,6},{8,9},{9,8},{10,11... | collective-permute-start | bytes 18440 | tf_op jit(solution)/shard_map/ppermute | solution.py:426
  15.7 1.9 %collective-permute-start.5 = (f32[3,16,32]{2,1,0:T(8,128)}, f32[3,16,32]{2,1,0:T(8,128)S(1)}, u32[]{:S(2)}, u32[]{:S(2)}) collective-permute-start(f32[3,16,32]{2,1,0:T(8,128)} %get-tuple-element.31), channel_id=1, source_target_pairs={{1,2},{2,1},{5,6},{6,5},{9,10},{10,9},{13,14},{14,13},{17,18},{18,... | collective-permute-start | bytes 18440 | tf_op jit(solution)/shard_map/ppermute | solution.py:427
  17.6 0.0 collective-permute-done.4.gz_lo
  17.6 2.9 %collective-permute-done.5.gz_hi = f32[3,16,32]{2,1,0:T(8,128)S(1)} collective-permute-done((f32[3,16,32]{2,1,0:T(8,128)}, f32[3,16,32]{2,1,0:T(8,128)S(1)}, u32[]{:S(2)}, u32[]{:S(2)}) %collective-permute-start.5) | collective-permute-done | bytes 6176 | tf_op jit(solution)/shard_map/ppermute | solution.py:427
  20.6 0.0 collective-permute-done.2.gy_lo
  20.6 0.0 collective-permute-done.3.gy_hi
  20.6 0.6 copy-done.4
  21.2 0.1 copy-done
  21.2 0.0 copy-done.1
  21.2 5.7 %shard_map.61 = (f32[2,32,16,256]{3,2,1,0:T(8,128)}, f32[2,2,16,256]{3,2,1,0:T(8,128)}) custom-call(s32[3]{0:T(128)} %pad_add_fusion.ctl_ref.r_0_, f32[32,16,256]{2,1,0:T(8,128)} %vac_ref.3, f32[32,16,256]{2,1,0:T(8,128)} %cot_ref.1, s32[32,16,256]{2,1,0:T(8,128)} %pore_ref.7, s32[32,16,256]{2,1,0:T(8,128)} %lab_ref.7, ...), custom_call_target="tpu_custom_call" | custom-call | tf_op jit(solution)/shard_map/pallas_call | solution.py:472
  27.0 1.1 %collective-permute-start.6 = (f32[2,2,16,256]{3,2,1,0:T(8,128)}, f32[2,2,16,256]{3,2,1,0:T(8,128)S(1)}, u32[]{:S(2)}, u32[]{:S(2)}) collective-permute-start(f32[2,2,16,256]{3,2,1,0:T(8,128)} %get-tuple-element.32.r_3_), channel_id=1, source_target_pairs={{0,16},{16,0},{1,17},{17,1},{2,18},{18,2},{3,19},{19,3},{4,20},{20... | collective-permute-start | bytes 196616 | tf_op jit(solution)/shard_map/ppermute | solution.py:409
  28.1 2.2 %collective-permute-done.6.r_4_ = f32[2,2,16,256]{3,2,1,0:T(8,128)S(1)} collective-permute-done((f32[2,2,16,256]{3,2,1,0:T(8,128)}, f32[2,2,16,256]{3,2,1,0:T(8,128)S(1)}, u32[]{:S(2)}, u32[]{:S(2)}) %collective-permute-start.6) | collective-permute-done | bytes 65568 | tf_op jit(solution)/shard_map/ppermute | solution.py:409
  30.3 0.0 collective-permute-done.1.r_2_
  30.3 0.6 copy-done.7
  30.9 0.1 copy-done.2
  31.0 3.5 %shard_map.62 = (f32[2,32,16,256]{3,2,1,0:T(8,128)}, f32[2,32,256]{2,1,0:T(8,128)}, f32[2,32,256]{2,1,0:T(8,128)}, f32[2,16,32]{2,1,0:T(8,128)}, f32[2,16,32]{2,1,0:T(8,128)}) custom-call(s32[3]{0:T(128)} %pad_add_fusion.ctl_ref.r_0_, f32[2,5,16,256]{3,2,1,0:T(8,128)} %get-tuple-element.26.r_1_, f32[2,5,16,256]{3,2,1,0:T(8,128)} %copy-done.2, ...), custom_call_target="tpu_custom_call" | custom-call | tf_op jit(solution)/shard_map/pallas_call | solution.py:478
  34.5 3.6 %collective-permute-start.7 = (f32[2,32,256]{2,1,0:T(8,128)}, f32[2,32,256]{2,1,0:T(8,128)S(1)}, u32[]{:S(2)}, u32[]{:S(2)}) collective-permute-start(f32[2,32,256]{2,1,0:T(8,128)} %get-tuple-element.36), channel_id=1, source_target_pairs={{0,4},{4,0},{8,12},{12,8},{1,5},{5,1},{9,13},{13,9},{2,6},{6,2},{1... | collective-permute-start | bytes 196616 | tf_op jit(solution)/shard_map/ppermute | solution.py:426
  38.2 3.0 %collective-permute-start.8 = (f32[2,32,256]{2,1,0:T(8,128)}, f32[2,32,256]{2,1,0:T(8,128)S(1)}, u32[]{:S(2)}, u32[]{:S(2)}) collective-permute-start(f32[2,32,256]{2,1,0:T(8,128)} %get-tuple-element.37), channel_id=1, source_target_pairs={{4,8},{8,4},{5,9},{9,5},{6,10},{10,6},{7,11},{11,7},{20,24},{24,20... | collective-permute-start | bytes 196616 | tf_op jit(solution)/shard_map/ppermute | solution.py:427
  41.2 0.1 collective-permute-start.9
  41.3 1.9 %collective-permute-start.10 = (f32[2,16,32]{2,1,0:T(8,128)}, f32[2,16,32]{2,1,0:T(8,128)S(1)}, u32[]{:S(2)}, u32[]{:S(2)}) collective-permute-start(f32[2,16,32]{2,1,0:T(8,128)} %get-tuple-element.39), channel_id=1, source_target_pairs={{1,2},{2,1},{5,6},{6,5},{9,10},{10,9},{13,14},{14,13},{17,18},{18,... | collective-permute-start | bytes 12296 | tf_op jit(solution)/shard_map/ppermute | solution.py:427
  43.2 1.2 %collective-permute-done.9.hz_lo = f32[2,16,32]{2,1,0:T(8,128)S(1)} collective-permute-done((f32[2,16,32]{2,1,0:T(8,128)}, f32[2,16,32]{2,1,0:T(8,128)S(1)}, u32[]{:S(2)}, u32[]{:S(2)}) %collective-permute-start.9) | collective-permute-done | bytes 4128 | tf_op jit(solution)/shard_map/ppermute | solution.py:426
  44.4 1.6 %collective-permute-done.10.hz_hi = f32[2,16,32]{2,1,0:T(8,128)S(1)} collective-permute-done((f32[2,16,32]{2,1,0:T(8,128)}, f32[2,16,32]{2,1,0:T(8,128)S(1)}, u32[]{:S(2)}, u32[]{:S(2)}) %collective-permute-start.10) | collective-permute-done | bytes 4128 | tf_op jit(solution)/shard_map/ppermute | solution.py:427
  46.0 0.6 copy-done.13
  46.6 0.0 copy-done.5
  46.6 0.0 copy-done.6
  46.7 6.1 %shard_map.63 = (f32[2,32,16,256]{3,2,1,0:T(8,128)}, f32[2,2,16,256]{3,2,1,0:T(8,128)}) custom-call(s32[3]{0:T(128)} %pad_add_fusion.ctl_ref.r_0_, s32[32,16,256]{2,1,0:T(8,128)} %pore_ref.7, s32[32,16,256]{2,1,0:T(8,128)} %lab_ref.7, f32[2,32,16,256]{3,2,1,0:T(8,128)} %get-tuple-element.35.fa_ref, f32[2,3,32,16,256]{4,3,2,1,0:T(8,128)} %get-tuple-element.27.fac_ref, ...), custom_call_target="tpu_custom_call" | custom-call | tf_op jit(solution)/shard_map/pallas_call | solution.py:488
  52.8 0.3 collective-permute-start.11
  53.1 3.1 %collective-permute-done.11.r_4_ = f32[2,2,16,256]{3,2,1,0:T(8,128)S(1)} collective-permute-done((f32[2,2,16,256]{3,2,1,0:T(8,128)}, f32[2,2,16,256]{3,2,1,0:T(8,128)S(1)}, u32[]{:S(2)}, u32[]{:S(2)}) %collective-permute-start.11) | collective-permute-done | bytes 65568 | tf_op jit(solution)/shard_map/ppermute | solution.py:409
  56.1 0.6 copy-done.8
  56.8 3.5 %shard_map.64 = (f32[32,16,256]{2,1,0:T(8,128)}, f32[32,16,256]{2,1,0:T(8,128)}, f32[1,32,256]{2,1,0:T(8,128)}, f32[1,32,256]{2,1,0:T(8,128)}, f32[1,16,32]{2,1,0:T(8,128)}, /*index=5*/f32[1,16,32]{2,1,0:T(8,128)}) custom-call(s32[3]{0:T(128)} %pad_add_fusion.ctl_ref.r_0_, f32[2,5,16,256]{3,2,1,0:T(8,128)} %get-tuple-element.26.r_1_, ...), custom_call_target="tpu_custom_call" | custom-call | tf_op jit(solution)/shard_map/pallas_call | solution.py:499
  60.2 4.8 %collective-permute-start.13 = (f32[1,32,256]{2,1,0:T(8,128)}, f32[1,32,256]{2,1,0:T(8,128)S(1)}, u32[]{:S(2)}, u32[]{:S(2)}) collective-permute-start(f32[1,32,256]{2,1,0:T(8,128)} %get-tuple-element.45), channel_id=1, source_target_pairs={{4,8},{8,4},{5,9},{9,5},{6,10},{10,6},{7,11},{11,7},{20,24},{24,20... | collective-permute-start | bytes 98312 | tf_op jit(solution)/shard_map/ppermute | solution.py:427
  65.1 0.1 collective-permute-start.14
  65.2 1.9 %collective-permute-start.15 = (f32[1,16,32]{2,1,0:T(8,128)}, f32[1,16,32]{2,1,0:T(8,128)S(1)}, u32[]{:S(2)}, u32[]{:S(2)}) collective-permute-start(f32[1,16,32]{2,1,0:T(8,128)} %get-tuple-element.47), channel_id=1, source_target_pairs={{1,2},{2,1},{5,6},{6,5},{9,10},{10,9},{13,14},{14,13},{17,18},{18,... | collective-permute-start | bytes 6152 | tf_op jit(solution)/shard_map/ppermute | solution.py:427
  67.1 0.8 %collective-permute-done.14.hz_lo = f32[1,16,32]{2,1,0:T(8,128)S(1)} collective-permute-done((f32[1,16,32]{2,1,0:T(8,128)}, f32[1,16,32]{2,1,0:T(8,128)S(1)}, u32[]{:S(2)}, u32[]{:S(2)}) %collective-permute-start.14) | collective-permute-done | bytes 2080 | tf_op jit(solution)/shard_map/ppermute | solution.py:426
  67.9 1.9 %collective-permute-done.15.hz_hi = f32[1,16,32]{2,1,0:T(8,128)S(1)} collective-permute-done((f32[1,16,32]{2,1,0:T(8,128)}, f32[1,16,32]{2,1,0:T(8,128)S(1)}, u32[]{:S(2)}, u32[]{:S(2)}) %collective-permute-start.15) | collective-permute-done | bytes 2080 | tf_op jit(solution)/shard_map/ppermute | solution.py:427
  69.8 0.6 copy-done.15
  70.4 0.0 copy-done.10
  70.4 0.0 copy-done.11
  70.4 3.9 %shard_map.65 = f32[32,16,256]{2,1,0:T(8,128)} custom-call(s32[3]{0:T(128)} %pad_add_fusion.ctl_ref.r_0_, s32[32,16,256]{2,1,0:T(8,128)} %pore_ref.7, s32[32,16,256]{2,1,0:T(8,128)} %lab_ref.7, f32[32,16,256]{2,1,0:T(8,128)} %get-tuple-element.43.a2_ref, f32[3,32,256]{2,1,0:T(8,128)} %copy-done, f32[3,32,256]{2,1,0:T(8,128)} %copy-done.1, ...), custom_call_target="tpu_custom_call" | custom-call | tf_op jit(solution)/shard_map/pallas_call | solution.py:509
  (24 shorter events, 0.0 us)
Async XLA Ops:
  3.9 5.2 %collective-permute-start = (f32[2,2,16,256]{3,2,1,0:T(8,128)}, f32[2,2,16,256]{3,2,1,0:T(8,128)S(1)}, u32[]{:S(2)}, u32[]{:S(2)}) collective-permute-start(f32[2,2,16,256]{3,2,1,0:T(8,128)} %get-tuple-element.25), channel_id=1, source_target_pairs={{0,16},{16,0},{1,17},{17,1},{2,18},{18,2},{3,19},{19,3},{4,20},{20... | collective-permute-start | bytes 196616 | tf_op jit(solution)/shard_map/ppermute | solution.py:452
  5.1 15.5 %collective-permute-start.2 = (f32[3,32,256]{2,1,0:T(8,128)}, f32[3,32,256]{2,1,0:T(8,128)S(1)}, u32[]{:S(2)}, u32[]{:S(2)}) collective-permute-start(f32[3,32,256]{2,1,0:T(8,128)} %get-tuple-element.28), channel_id=1, source_target_pairs={{0,4},{4,0},{8,12},{12,8},{1,5},{5,1},{9,13},{13,9},{2,6},{6,2},{1... | collective-permute-start | bytes 294920 | tf_op jit(solution)/shard_map/ppermute | solution.py:426
  6.0 14.5 %collective-permute-start.3 = (f32[3,32,256]{2,1,0:T(8,128)}, f32[3,32,256]{2,1,0:T(8,128)S(1)}, u32[]{:S(2)}, u32[]{:S(2)}) collective-permute-start(f32[3,32,256]{2,1,0:T(8,128)} %get-tuple-element.29), channel_id=1, source_target_pairs={{4,8},{8,4},{5,9},{9,5},{6,10},{10,6},{7,11},{11,7},{20,24},{24,20... | collective-permute-start | bytes 294920 | tf_op jit(solution)/shard_map/ppermute | solution.py:427
  9.1 0.6 copy-start.9
  14.1 16.2 %collective-permute-start.1 = (f32[2,5,16,256]{3,2,1,0:T(8,128)}, f32[2,5,16,256]{3,2,1,0:T(8,128)S(1)}, u32[]{:S(2)}, u32[]{:S(2)}) collective-permute-start(f32[2,5,16,256]{3,2,1,0:T(8,128)} %get-tuple-element.26.r_1_), channel_id=1, source_target_pairs={{0,16},{16,0},{1,17},{17,1},{2,18},{18,2},{3,19},{19,3},{4,20},{20... | collective-permute-start | bytes 491528 | tf_op jit(solution)/shard_map/ppermute | solution.py:409
  14.4 3.2 %collective-permute-start.4 = (f32[3,16,32]{2,1,0:T(8,128)}, f32[3,16,32]{2,1,0:T(8,128)S(1)}, u32[]{:S(2)}, u32[]{:S(2)}) collective-permute-start(f32[3,16,32]{2,1,0:T(8,128)} %get-tuple-element.30), channel_id=1, source_target_pairs={{0,1},{1,0},{2,3},{3,2},{4,5},{5,4},{6,7},{7,6},{8,9},{9,8},{10,11... | collective-permute-start | bytes 18440 | tf_op jit(solution)/shard_map/ppermute | solution.py:426
  15.7 4.9 %collective-permute-start.5 = (f32[3,16,32]{2,1,0:T(8,128)}, f32[3,16,32]{2,1,0:T(8,128)S(1)}, u32[]{:S(2)}, u32[]{:S(2)}) collective-permute-start(f32[3,16,32]{2,1,0:T(8,128)} %get-tuple-element.31), channel_id=1, source_target_pairs={{1,2},{2,1},{5,6},{6,5},{9,10},{10,9},{13,14},{14,13},{17,18},{18,... | collective-permute-start | bytes 18440 | tf_op jit(solution)/shard_map/ppermute | solution.py:427
  17.6 3.0 %copy-start.3 = (f32[3,16,32]{2,1,0:T(8,128)}, f32[3,16,32]{2,1,0:T(8,128)S(1)}, u32[]{:S(2)}) copy-start(f32[3,16,32]{2,1,0:T(8,128)S(1)} %collective-permute-done.4.gz_lo) | copy-start | bytes 18436
  20.6 0.6 copy-start.4
  20.6 0.6 copy-start
  20.6 0.7 copy-start.1
  27.0 3.3 %collective-permute-start.6 = (f32[2,2,16,256]{3,2,1,0:T(8,128)}, f32[2,2,16,256]{3,2,1,0:T(8,128)S(1)}, u32[]{:S(2)}, u32[]{:S(2)}) collective-permute-start(f32[2,2,16,256]{3,2,1,0:T(8,128)} %get-tuple-element.32.r_3_), channel_id=1, source_target_pairs={{0,16},{16,0},{1,17},{17,1},{2,18},{18,2},{3,19},{19,3},{4,20},{20... | collective-permute-start | bytes 196616 | tf_op jit(solution)/shard_map/ppermute | solution.py:409
  30.3 0.6 copy-start.7
  30.3 0.7 copy-start.2
  34.5 11.5 %collective-permute-start.7 = (f32[2,32,256]{2,1,0:T(8,128)}, f32[2,32,256]{2,1,0:T(8,128)S(1)}, u32[]{:S(2)}, u32[]{:S(2)}) collective-permute-start(f32[2,32,256]{2,1,0:T(8,128)} %get-tuple-element.36), channel_id=1, source_target_pairs={{0,4},{4,0},{8,12},{12,8},{1,5},{5,1},{9,13},{13,9},{2,6},{6,2},{1... | collective-permute-start | bytes 196616 | tf_op jit(solution)/shard_map/ppermute | solution.py:426
  38.2 7.8 %collective-permute-start.8 = (f32[2,32,256]{2,1,0:T(8,128)}, f32[2,32,256]{2,1,0:T(8,128)S(1)}, u32[]{:S(2)}, u32[]{:S(2)}) collective-permute-start(f32[2,32,256]{2,1,0:T(8,128)} %get-tuple-element.37), channel_id=1, source_target_pairs={{4,8},{8,4},{5,9},{9,5},{6,10},{10,6},{7,11},{11,7},{20,24},{24,20... | collective-permute-start | bytes 196616 | tf_op jit(solution)/shard_map/ppermute | solution.py:427
  41.2 3.2 %collective-permute-start.9 = (f32[2,16,32]{2,1,0:T(8,128)}, f32[2,16,32]{2,1,0:T(8,128)S(1)}, u32[]{:S(2)}, u32[]{:S(2)}) collective-permute-start(f32[2,16,32]{2,1,0:T(8,128)} %get-tuple-element.38), channel_id=1, source_target_pairs={{0,1},{1,0},{2,3},{3,2},{4,5},{5,4},{6,7},{7,6},{8,9},{9,8},{10,11... | collective-permute-start | bytes 12296 | tf_op jit(solution)/shard_map/ppermute | solution.py:426
  41.3 4.7 %collective-permute-start.10 = (f32[2,16,32]{2,1,0:T(8,128)}, f32[2,16,32]{2,1,0:T(8,128)S(1)}, u32[]{:S(2)}, u32[]{:S(2)}) collective-permute-start(f32[2,16,32]{2,1,0:T(8,128)} %get-tuple-element.39), channel_id=1, source_target_pairs={{1,2},{2,1},{5,6},{6,5},{9,10},{10,9},{13,14},{14,13},{17,18},{18,... | collective-permute-start | bytes 12296 | tf_op jit(solution)/shard_map/ppermute | solution.py:427
  44.4 1.6 %copy-start.12 = (f32[2,16,32]{2,1,0:T(8,128)}, f32[2,16,32]{2,1,0:T(8,128)S(1)}, u32[]{:S(2)}) copy-start(f32[2,16,32]{2,1,0:T(8,128)S(1)} %collective-permute-done.9.hz_lo) | copy-start | bytes 12292
  46.0 0.6 copy-start.13
  46.0 0.6 copy-start.5
  46.0 0.6 copy-start.6
  52.8 3.3 %collective-permute-start.11 = (f32[2,2,16,256]{3,2,1,0:T(8,128)}, f32[2,2,16,256]{3,2,1,0:T(8,128)S(1)}, u32[]{:S(2)}, u32[]{:S(2)}) collective-permute-start(f32[2,2,16,256]{3,2,1,0:T(8,128)} %get-tuple-element.40.r_3_), channel_id=1, source_target_pairs={{0,16},{16,0},{1,17},{17,1},{2,18},{18,2},{3,19},{19,3},{4,20},{20... | collective-permute-start | bytes 196616 | tf_op jit(solution)/shard_map/ppermute | solution.py:409
  56.1 0.6 copy-start.8
  60.2 9.5 %collective-permute-start.12 = (f32[1,32,256]{2,1,0:T(8,128)}, f32[1,32,256]{2,1,0:T(8,128)S(1)}, u32[]{:S(2)}, u32[]{:S(2)}) collective-permute-start(f32[1,32,256]{2,1,0:T(8,128)} %get-tuple-element.44), channel_id=1, source_target_pairs={{0,4},{4,0},{8,12},{12,8},{1,5},{5,1},{9,13},{13,9},{2,6},{6,2},{1... | collective-permute-start | bytes 98312 | tf_op jit(solution)/shard_map/ppermute | solution.py:426
  60.2 9.5 %collective-permute-start.13 = (f32[1,32,256]{2,1,0:T(8,128)}, f32[1,32,256]{2,1,0:T(8,128)S(1)}, u32[]{:S(2)}, u32[]{:S(2)}) collective-permute-start(f32[1,32,256]{2,1,0:T(8,128)} %get-tuple-element.45), channel_id=1, source_target_pairs={{4,8},{8,4},{5,9},{9,5},{6,10},{10,6},{7,11},{11,7},{20,24},{24,20... | collective-permute-start | bytes 98312 | tf_op jit(solution)/shard_map/ppermute | solution.py:427
  65.1 2.8 %collective-permute-start.14 = (f32[1,16,32]{2,1,0:T(8,128)}, f32[1,16,32]{2,1,0:T(8,128)S(1)}, u32[]{:S(2)}, u32[]{:S(2)}) collective-permute-start(f32[1,16,32]{2,1,0:T(8,128)} %get-tuple-element.46), channel_id=1, source_target_pairs={{0,1},{1,0},{2,3},{3,2},{4,5},{5,4},{6,7},{7,6},{8,9},{9,8},{10,11... | collective-permute-start | bytes 6152 | tf_op jit(solution)/shard_map/ppermute | solution.py:426
  65.2 4.6 %collective-permute-start.15 = (f32[1,16,32]{2,1,0:T(8,128)}, f32[1,16,32]{2,1,0:T(8,128)S(1)}, u32[]{:S(2)}, u32[]{:S(2)}) collective-permute-start(f32[1,16,32]{2,1,0:T(8,128)} %get-tuple-element.47), channel_id=1, source_target_pairs={{1,2},{2,1},{5,6},{6,5},{9,10},{10,9},{13,14},{14,13},{17,18},{18,... | collective-permute-start | bytes 6152 | tf_op jit(solution)/shard_map/ppermute | solution.py:427
  67.8 1.9 %copy-start.14 = (f32[1,16,32]{2,1,0:T(8,128)}, f32[1,16,32]{2,1,0:T(8,128)S(1)}, u32[]{:S(2)}) copy-start(f32[1,16,32]{2,1,0:T(8,128)S(1)} %collective-permute-done.14.hz_lo) | copy-start | bytes 6148
  69.8 0.6 copy-start.15
  69.8 0.6 copy-start.10
  69.8 0.6 copy-start.11

commit v3 on v2

--- a/solution.py
+++ b/solution.py
@@ -40,17 +40,6 @@
         _shift(x, zhi, 1, True),
         _shift(x, zlo, 1, False),
     )
-
-
-def _faces(mob, lab, mob_n, lab_n):
-    ups = (True, False, True, False)
-    out = []
-    for up, mn, ln in zip(ups, mob_n, lab_n):
-        if up:
-            out.append(face_value(mob, mn, lab, ln))
-        else:
-            out.append(face_value(mn, mob, ln, lab))
-    return out
 
 
 def _flux(u, u_n, faces):
@@ -129,12 +118,20 @@
 def _geo_row(i, pore_ref, lab_ref, gy_lo, gy_hi, gz_lo, gz_hi):
     mob = 1.0 + 2.0 * pore_ref[i].astype(F32)
     lab = lab_ref[i].astype(F32)
-    mob_n = _neighbours(mob, _yrow(gy_lo, 0, i), _yrow(gy_hi, 0, i), _zcol(gz_lo, 0, i), _zcol(gz_hi, 0, i))
-    lab_n = _neighbours(lab, _yrow(gy_lo, 1, i), _yrow(gy_hi, 1, i), _zcol(gz_lo, 1, i), _zcol(gz_hi, 1, i))
-    return mob, lab, mob_n, _faces(mob, lab, mob_n, lab_n)
-
-
-def _sweep(m, lower, pivots, ratios, source):
+    ny, nz = mob.shape
+    m_ylo, m_yhi, m_zlo, m_zhi = _yrow(gy_lo, 0, i), _yrow(gy_hi, 0, i), _zcol(gz_lo, 0, i), _zcol(gz_hi, 0, i)
+    l_ylo, l_yhi, l_zlo, l_zhi = _yrow(gy_lo, 1, i), _yrow(gy_hi, 1, i), _zcol(gz_lo, 1, i), _zcol(gz_hi, 1, i)
+    mob_n = _neighbours(mob, m_ylo, m_yhi, m_zlo, m_zhi)
+    lab_yp = _shift(lab, l_yhi, 0, True)
+    lab_zp = _shift(lab, l_zhi, 1, True)
+    face_yp = face_value(mob, mob_n[0], lab, lab_yp)
+    face_zp = face_value(mob, mob_n[2], lab, lab_zp)
+    face_ym = _shift(face_yp, face_value(m_ylo, mob[0:1, :], l_ylo, lab[0:1, :]), 0, False)
+    face_zm = _shift(face_zp, face_value(m_zlo, mob[:, 0:1], l_zlo, lab[:, 0:1]), 1, False)
+    return mob, lab, mob_n, [face_yp, face_ym, face_zp, face_zm]
+
+
+def _sweep(m, lower, inv_pivots, ratios, source):
     ys = [None] * m
     prev = None
     for r in range(m - 1):
@@ -145,7 +142,7 @@
             num = -(lower[r] * prev)
         elif prev is not None:
             num = num - lower[r] * prev
-        ys[r] = num / pivots[r]
+        ys[r] = num * inv_pivots[r]
         prev = ys[r]
     xs = [None] * m
     prev = None
@@ -192,14 +189,15 @@
             pivots.append(piv)
             ratios.append(rat)
             prev = rat
+        inv_piv = [1.0 / x for x in pivots]
         left_src = [lower[0]] + [None] * (m - 1)
         right_src = [None] * (m - 2) + [upper[m - 2], None]
-        left = _sweep(m, lower, pivots, ratios, left_src)
-        right = _sweep(m, lower, pivots, ratios, right_src)
+        left = _sweep(m, lower, inv_piv, ratios, left_src)
+        right = _sweep(m, lower, inv_piv, ratios, right_src)
         for r in range(m):
             fac_ref[c, 0, r] = lower[r]
             fac_ref[c, 1, r] = ratios[r] if r < m - 1 else zero
-            fac_ref[c, 2, r] = pivots[r] if r < m - 1 else zero + 1.0
+            fac_ref[c, 2, r] = inv_piv[r] if r < m - 1 else zero + 1.0
             lr_ref[c, 0, r] = left[r] if r < m - 1 else zero
             lr_ref[c, 1, r] = right[r] if r < m - 1 else zero - 1.0
         last_lower = lower[m - 1]

time: 74.6 us -> 79.9 us (1.071)
  Pallas kernels: 29.9 us -> 35.1 us
    pallas_call x1, Pallas kernels: 6.14 us -> 7.95 us  [_shards(): pl.pallas_call(_second_kernel, out_shape=(jax.ShapeDtypeStruct((2, m, ny,...]
    pallas_call x1, Pallas kernels: 3.95 us -> 5.73 us  [_shards(): pl.pallas_call(_gradient_kernel, out_shape=shape, in_specs=[_smem()] + [_...]
    pallas_call x1, Pallas kernels: 5.73 us -> 7.42 us  [_shards(): _first_call(m, ny, nz)]
  transfers between devices with their start and end apart: 16 -> 16, of which waited for: 7 -> 7; matrix products, arithmetic and copies ran while one was open for 0% -> 0% of each run, Pallas kernels for 14% -> 15%
where the time goes in v3:
time: 79.9 us; the launch traced here: 79.6 us
  Pallas kernels  35.1 us (44%)
  starting transfers between devices  25.7 us (32%)
  waiting for transfers between devices  13.5 us (17%)
  local copies, waits for them, and re-layouts  3.82 us (5%)
  between operations  0.83 us (1%)
    ppermute x6, starting transfers between devices, _swap(): lax.ppermute(x_b, axis, pairs_b)  16.8 us
    pallas_call x1, Pallas kernels, _shards(): pl.pallas_call(_second_kernel, out_shape=(jax.ShapeDtypeStruct((2, m, ny,...  7.95 us
    pallas_call x1, Pallas kernels, _shards(): _first_call(m, ny, nz)  7.42 us
    ppermute x6, waiting for transfers between devices, _swap(): lax.ppermute(x_b, axis, pairs_b)  6.46 us
    ppermute x6, starting transfers between devices, _swap(): recv_a = lax.ppermute(x_a, axis, pairs_a)  6.03 us
    pallas_call x1, Pallas kernels, _shards(): pl.pallas_call(_gradient_kernel, out_shape=shape, in_specs=[_smem()] + [_...  5.73 us
    ppermute x3, waiting for transfers between devices, _gather_blk(): parts.append(lax.ppermute(x, 'blk', [(j, (j + k) % n) for j in range(n)]))  5.3 us
    pallas_call x1, Pallas kernels, _shards(): pl.pallas_call(lambda *r: _factor_kernel(cycle_step, lo_i, hi_i, *r), out...  4.45 us
  transfers between devices with their start and end apart: 16, of which 7 were waited for; matrix products, arithmetic and copies ran while one was open for 0% of the time, Pallas kernels for 15%

profile of v3, /device:TPU:17, one launch (start us, length us, event | category | flops | bytes accessed | tf_op | source)
XLA Modules:
  0.0 79.6 jit_solution(4661023267941006492)
XLA Ops:
  0.6 0.6 pad_add_fusion.ctl_ref.r_0_
  1.3 2.6 %shard_map.59 = (f32[3,32,256]{2,1,0:T(8,128)}, f32[3,32,256]{2,1,0:T(8,128)}, f32[3,16,32]{2,1,0:T(8,128)}, f32[3,16,32]{2,1,0:T(8,128)}, f32[2,2,16,256]{3,2,1,0:T(8,128)}) custom-call(s32[3]{0:T(128)} %pad_add_fusion.ctl_ref.r_0_, f32[32,16,256]{2,1,0:T(8,128)} %vac_ref.3, s32[32,16,256]{2,1,0:T(8,128)} %pore_ref.7, s32[32,16,256]{2,1,0:T(8,128)} %lab_ref.7), custom_call_target="tpu_custom_call" | custom-call | tf_op jit(solution)/shard_map/pallas_call | solution.py:442
  3.9 1.2 %collective-permute-start = (f32[2,2,16,256]{3,2,1,0:T(8,128)}, f32[2,2,16,256]{3,2,1,0:T(8,128)S(1)}, u32[]{:S(2)}, u32[]{:S(2)}) collective-permute-start(f32[2,2,16,256]{3,2,1,0:T(8,128)} %get-tuple-element.25), channel_id=1, source_target_pairs={{0,16},{16,0},{1,17},{17,1},{2,18},{18,2},{3,19},{19,3},{4,20},{20... | collective-permute-start | bytes 196616 | tf_op jit(solution)/shard_map/ppermute | solution.py:450
  5.1 0.9 %collective-permute-start.2 = (f32[3,32,256]{2,1,0:T(8,128)}, f32[3,32,256]{2,1,0:T(8,128)S(1)}, u32[]{:S(2)}, u32[]{:S(2)}) collective-permute-start(f32[3,32,256]{2,1,0:T(8,128)} %get-tuple-element.28), channel_id=1, source_target_pairs={{0,4},{4,0},{8,12},{12,8},{1,5},{5,1},{9,13},{13,9},{2,6},{6,2},{1... | collective-permute-start | bytes 294920 | tf_op jit(solution)/shard_map/ppermute | solution.py:424
  6.0 3.0 %collective-permute-start.3 = (f32[3,32,256]{2,1,0:T(8,128)}, f32[3,32,256]{2,1,0:T(8,128)S(1)}, u32[]{:S(2)}, u32[]{:S(2)}) collective-permute-start(f32[3,32,256]{2,1,0:T(8,128)} %get-tuple-element.29), channel_id=1, source_target_pairs={{4,8},{8,4},{5,9},{9,5},{6,10},{10,6},{7,11},{11,7},{20,24},{24,20... | collective-permute-start | bytes 294920 | tf_op jit(solution)/shard_map/ppermute | solution.py:425
  9.1 0.0 collective-permute-done.r_2_
  9.1 0.6 copy-done.9
  9.7 4.4 %shard_map.60 = (f32[2,3,32,16,256]{4,3,2,1,0:T(8,128)}, f32[2,2,32,16,256]{4,3,2,1,0:T(8,128)}, f32[2,5,16,256]{3,2,1,0:T(8,128)}) custom-call(s32[32,16,256]{2,1,0:T(8,128)} %pore_ref.7, s32[32,16,256]{2,1,0:T(8,128)} %lab_ref.7, f32[2,2,16,256]{3,2,1,0:T(8,128)} %copy-done.9), custom_call_target="tpu_custom_call" | custom-call | tf_op jit(solution)/shard_map/pallas_call | solution.py:458
  14.1 0.3 collective-permute-start.1
  14.4 1.3 %collective-permute-start.4 = (f32[3,16,32]{2,1,0:T(8,128)}, f32[3,16,32]{2,1,0:T(8,128)S(1)}, u32[]{:S(2)}, u32[]{:S(2)}) collective-permute-start(f32[3,16,32]{2,1,0:T(8,128)} %get-tuple-element.30), channel_id=1, source_target_pairs={{0,1},{1,0},{2,3},{3,2},{4,5},{5,4},{6,7},{7,6},{8,9},{9,8},{10,11... | collective-permute-start | bytes 18440 | tf_op jit(solution)/shard_map/ppermute | solution.py:424
  15.7 1.9 %collective-permute-start.5 = (f32[3,16,32]{2,1,0:T(8,128)}, f32[3,16,32]{2,1,0:T(8,128)S(1)}, u32[]{:S(2)}, u32[]{:S(2)}) collective-permute-start(f32[3,16,32]{2,1,0:T(8,128)} %get-tuple-element.31), channel_id=1, source_target_pairs={{1,2},{2,1},{5,6},{6,5},{9,10},{10,9},{13,14},{14,13},{17,18},{18,... | collective-permute-start | bytes 18440 | tf_op jit(solution)/shard_map/ppermute | solution.py:425
  17.6 0.0 collective-permute-done.4.gz_lo
  17.6 2.9 %collective-permute-done.5.gz_hi = f32[3,16,32]{2,1,0:T(8,128)S(1)} collective-permute-done((f32[3,16,32]{2,1,0:T(8,128)}, f32[3,16,32]{2,1,0:T(8,128)S(1)}, u32[]{:S(2)}, u32[]{:S(2)}) %collective-permute-start.5) | collective-permute-done | bytes 6176 | tf_op jit(solution)/shard_map/ppermute | solution.py:425
  20.6 0.6 copy-done.4
  21.2 0.1 copy-done
  21.2 0.0 copy-done.1
  21.2 7.4 %shard_map.61 = (f32[2,32,16,256]{3,2,1,0:T(8,128)}, f32[2,2,16,256]{3,2,1,0:T(8,128)}) custom-call(s32[3]{0:T(128)} %pad_add_fusion.ctl_ref.r_0_, f32[32,16,256]{2,1,0:T(8,128)} %vac_ref.3, f32[32,16,256]{2,1,0:T(8,128)} %cot_ref.1, s32[32,16,256]{2,1,0:T(8,128)} %pore_ref.7, s32[32,16,256]{2,1,0:T(8,128)} %lab_ref.7, ...), custom_call_target="tpu_custom_call" | custom-call | tf_op jit(solution)/shard_map/pallas_call | solution.py:470
  28.7 1.1 %collective-permute-start.6 = (f32[2,2,16,256]{3,2,1,0:T(8,128)}, f32[2,2,16,256]{3,2,1,0:T(8,128)S(1)}, u32[]{:S(2)}, u32[]{:S(2)}) collective-permute-start(f32[2,2,16,256]{3,2,1,0:T(8,128)} %get-tuple-element.32.r_3_), channel_id=1, source_target_pairs={{0,16},{16,0},{1,17},{17,1},{2,18},{18,2},{3,19},{19,3},{4,20},{20... | collective-permute-start | bytes 196616 | tf_op jit(solution)/shard_map/ppermute | solution.py:407
  29.8 2.2 %collective-permute-done.6.r_4_ = f32[2,2,16,256]{3,2,1,0:T(8,128)S(1)} collective-permute-done((f32[2,2,16,256]{3,2,1,0:T(8,128)}, f32[2,2,16,256]{3,2,1,0:T(8,128)S(1)}, u32[]{:S(2)}, u32[]{:S(2)}) %collective-permute-start.6) | collective-permute-done | bytes 65568 | tf_op jit(solution)/shard_map/ppermute | solution.py:407
  32.0 0.0 collective-permute-done.1.r_2_
  32.0 0.6 copy-done.7
  32.6 0.1 copy-done.2
  32.7 3.5 %shard_map.62 = (f32[2,32,16,256]{3,2,1,0:T(8,128)}, f32[2,32,256]{2,1,0:T(8,128)}, f32[2,32,256]{2,1,0:T(8,128)}, f32[2,16,32]{2,1,0:T(8,128)}, f32[2,16,32]{2,1,0:T(8,128)}) custom-call(s32[3]{0:T(128)} %pad_add_fusion.ctl_ref.r_0_, f32[2,5,16,256]{3,2,1,0:T(8,128)} %get-tuple-element.26.r_1_, f32[2,5,16,256]{3,2,1,0:T(8,128)} %copy-done.2, ...), custom_call_target="tpu_custom_call" | custom-call | tf_op jit(solution)/shard_map/pallas_call | solution.py:476
  36.2 3.6 %collective-permute-start.7 = (f32[2,32,256]{2,1,0:T(8,128)}, f32[2,32,256]{2,1,0:T(8,128)S(1)}, u32[]{:S(2)}, u32[]{:S(2)}) collective-permute-start(f32[2,32,256]{2,1,0:T(8,128)} %get-tuple-element.36), channel_id=1, source_target_pairs={{0,4},{4,0},{8,12},{12,8},{1,5},{5,1},{9,13},{13,9},{2,6},{6,2},{1... | collective-permute-start | bytes 196616 | tf_op jit(solution)/shard_map/ppermute | solution.py:424
  39.9 3.0 %collective-permute-start.8 = (f32[2,32,256]{2,1,0:T(8,128)}, f32[2,32,256]{2,1,0:T(8,128)S(1)}, u32[]{:S(2)}, u32[]{:S(2)}) collective-permute-start(f32[2,32,256]{2,1,0:T(8,128)} %get-tuple-element.37), channel_id=1, source_target_pairs={{4,8},{8,4},{5,9},{9,5},{6,10},{10,6},{7,11},{11,7},{20,24},{24,20... | collective-permute-start | bytes 196616 | tf_op jit(solution)/shard_map/ppermute | solution.py:425
  42.9 0.1 collective-permute-start.9
  43.0 1.9 %collective-permute-start.10 = (f32[2,16,32]{2,1,0:T(8,128)}, f32[2,16,32]{2,1,0:T(8,128)S(1)}, u32[]{:S(2)}, u32[]{:S(2)}) collective-permute-start(f32[2,16,32]{2,1,0:T(8,128)} %get-tuple-element.39), channel_id=1, source_target_pairs={{1,2},{2,1},{5,6},{6,5},{9,10},{10,9},{13,14},{14,13},{17,18},{18,... | collective-permute-start | bytes 12296 | tf_op jit(solution)/shard_map/ppermute | solution.py:425
  44.9 1.2 %collective-permute-done.9.hz_lo = f32[2,16,32]{2,1,0:T(8,128)S(1)} collective-permute-done((f32[2,16,32]{2,1,0:T(8,128)}, f32[2,16,32]{2,1,0:T(8,128)S(1)}, u32[]{:S(2)}, u32[]{:S(2)}) %collective-permute-start.9) | collective-permute-done | bytes 4128 | tf_op jit(solution)/shard_map/ppermute | solution.py:424
  46.1 1.6 %collective-permute-done.10.hz_hi = f32[2,16,32]{2,1,0:T(8,128)S(1)} collective-permute-done((f32[2,16,32]{2,1,0:T(8,128)}, f32[2,16,32]{2,1,0:T(8,128)S(1)}, u32[]{:S(2)}, u32[]{:S(2)}) %collective-permute-start.10) | collective-permute-done | bytes 4128 | tf_op jit(solution)/shard_map/ppermute | solution.py:425
  47.7 0.0 collective-permute-done.7.hy_lo
  47.7 0.0 collective-permute-done.8.hy_hi
  47.7 0.6 copy-done.13
  48.3 0.0 copy-done.5
  48.3 0.0 copy-done.6
  48.3 8.0 %shard_map.63 = (f32[2,32,16,256]{3,2,1,0:T(8,128)}, f32[2,2,16,256]{3,2,1,0:T(8,128)}) custom-call(s32[3]{0:T(128)} %pad_add_fusion.ctl_ref.r_0_, s32[32,16,256]{2,1,0:T(8,128)} %pore_ref.7, s32[32,16,256]{2,1,0:T(8,128)} %lab_ref.7, f32[2,32,16,256]{3,2,1,0:T(8,128)} %get-tuple-element.35.fa_ref, f32[2,3,32,16,256]{4,3,2,1,0:T(8,128)} %get-tuple-element.27.fac_ref, ...), custom_call_target="tpu_custom_call" | custom-call | tf_op jit(solution)/shard_map/pallas_call | solution.py:486
  56.3 0.3 collective-permute-start.11
  56.6 3.1 %collective-permute-done.11.r_4_ = f32[2,2,16,256]{3,2,1,0:T(8,128)S(1)} collective-permute-done((f32[2,2,16,256]{3,2,1,0:T(8,128)}, f32[2,2,16,256]{3,2,1,0:T(8,128)S(1)}, u32[]{:S(2)}, u32[]{:S(2)}) %collective-permute-start.11) | collective-permute-done | bytes 65568 | tf_op jit(solution)/shard_map/ppermute | solution.py:407
  59.6 0.6 copy-done.8
  60.3 3.5 %shard_map.64 = (f32[32,16,256]{2,1,0:T(8,128)}, f32[32,16,256]{2,1,0:T(8,128)}, f32[1,32,256]{2,1,0:T(8,128)}, f32[1,32,256]{2,1,0:T(8,128)}, f32[1,16,32]{2,1,0:T(8,128)}, /*index=5*/f32[1,16,32]{2,1,0:T(8,128)}) custom-call(s32[3]{0:T(128)} %pad_add_fusion.ctl_ref.r_0_, f32[2,5,16,256]{3,2,1,0:T(8,128)} %get-tuple-element.26.r_1_, ...), custom_call_target="tpu_custom_call" | custom-call | tf_op jit(solution)/shard_map/pallas_call | solution.py:497
  63.7 4.8 %collective-permute-start.13 = (f32[1,32,256]{2,1,0:T(8,128)}, f32[1,32,256]{2,1,0:T(8,128)S(1)}, u32[]{:S(2)}, u32[]{:S(2)}) collective-permute-start(f32[1,32,256]{2,1,0:T(8,128)} %get-tuple-element.45), channel_id=1, source_target_pairs={{4,8},{8,4},{5,9},{9,5},{6,10},{10,6},{7,11},{11,7},{20,24},{24,20... | collective-permute-start | bytes 98312 | tf_op jit(solution)/shard_map/ppermute | solution.py:425
  68.6 0.1 collective-permute-start.14
  68.7 2.1 %collective-permute-start.15 = (f32[1,16,32]{2,1,0:T(8,128)}, f32[1,16,32]{2,1,0:T(8,128)S(1)}, u32[]{:S(2)}, u32[]{:S(2)}) collective-permute-start(f32[1,16,32]{2,1,0:T(8,128)} %get-tuple-element.47), channel_id=1, source_target_pairs={{1,2},{2,1},{5,6},{6,5},{9,10},{10,9},{13,14},{14,13},{17,18},{18,... | collective-permute-start | bytes 6152 | tf_op jit(solution)/shard_map/ppermute | solution.py:425
  70.8 0.6 collective-permute-done.14.hz_lo
  71.4 1.9 %collective-permute-done.15.hz_hi = f32[1,16,32]{2,1,0:T(8,128)S(1)} collective-permute-done((f32[1,16,32]{2,1,0:T(8,128)}, f32[1,16,32]{2,1,0:T(8,128)S(1)}, u32[]{:S(2)}, u32[]{:S(2)}) %collective-permute-start.15) | collective-permute-done | bytes 2080 | tf_op jit(solution)/shard_map/ppermute | solution.py:425
  73.3 0.6 copy-done.15
  73.9 0.0 copy-done.10
  73.9 0.0 copy-done.11
  73.9 5.7 %shard_map.65 = f32[32,16,256]{2,1,0:T(8,128)} custom-call(s32[3]{0:T(128)} %pad_add_fusion.ctl_ref.r_0_, s32[32,16,256]{2,1,0:T(8,128)} %pore_ref.7, s32[32,16,256]{2,1,0:T(8,128)} %lab_ref.7, f32[32,16,256]{2,1,0:T(8,128)} %get-tuple-element.43.a2_ref, f32[3,32,256]{2,1,0:T(8,128)} %copy-done, f32[3,32,256]{2,1,0:T(8,128)} %copy-done.1, ...), custom_call_target="tpu_custom_call" | custom-call | tf_op jit(solution)/shard_map/pallas_call | solution.py:507
  (24 shorter events, 0.0 us)
Async XLA Ops:
  3.9 5.2 %collective-permute-start = (f32[2,2,16,256]{3,2,1,0:T(8,128)}, f32[2,2,16,256]{3,2,1,0:T(8,128)S(1)}, u32[]{:S(2)}, u32[]{:S(2)}) collective-permute-start(f32[2,2,16,256]{3,2,1,0:T(8,128)} %get-tuple-element.25), channel_id=1, source_target_pairs={{0,16},{16,0},{1,17},{17,1},{2,18},{18,2},{3,19},{19,3},{4,20},{20... | collective-permute-start | bytes 196616 | tf_op jit(solution)/shard_map/ppermute | solution.py:450
  5.1 15.5 %collective-permute-start.2 = (f32[3,32,256]{2,1,0:T(8,128)}, f32[3,32,256]{2,1,0:T(8,128)S(1)}, u32[]{:S(2)}, u32[]{:S(2)}) collective-permute-start(f32[3,32,256]{2,1,0:T(8,128)} %get-tuple-element.28), channel_id=1, source_target_pairs={{0,4},{4,0},{8,12},{12,8},{1,5},{5,1},{9,13},{13,9},{2,6},{6,2},{1... | collective-permute-start | bytes 294920 | tf_op jit(solution)/shard_map/ppermute | solution.py:424
  6.0 14.5 %collective-permute-start.3 = (f32[3,32,256]{2,1,0:T(8,128)}, f32[3,32,256]{2,1,0:T(8,128)S(1)}, u32[]{:S(2)}, u32[]{:S(2)}) collective-permute-start(f32[3,32,256]{2,1,0:T(8,128)} %get-tuple-element.29), channel_id=1, source_target_pairs={{4,8},{8,4},{5,9},{9,5},{6,10},{10,6},{7,11},{11,7},{20,24},{24,20... | collective-permute-start | bytes 294920 | tf_op jit(solution)/shard_map/ppermute | solution.py:425
  9.1 0.6 copy-start.9
  14.1 17.9 %collective-permute-start.1 = (f32[2,5,16,256]{3,2,1,0:T(8,128)}, f32[2,5,16,256]{3,2,1,0:T(8,128)S(1)}, u32[]{:S(2)}, u32[]{:S(2)}) collective-permute-start(f32[2,5,16,256]{3,2,1,0:T(8,128)} %get-tuple-element.26.r_1_), channel_id=1, source_target_pairs={{0,16},{16,0},{1,17},{17,1},{2,18},{18,2},{3,19},{19,3},{4,20},{20... | collective-permute-start | bytes 491528 | tf_op jit(solution)/shard_map/ppermute | solution.py:407
  14.4 3.2 %collective-permute-start.4 = (f32[3,16,32]{2,1,0:T(8,128)}, f32[3,16,32]{2,1,0:T(8,128)S(1)}, u32[]{:S(2)}, u32[]{:S(2)}) collective-permute-start(f32[3,16,32]{2,1,0:T(8,128)} %get-tuple-element.30), channel_id=1, source_target_pairs={{0,1},{1,0},{2,3},{3,2},{4,5},{5,4},{6,7},{7,6},{8,9},{9,8},{10,11... | collective-permute-start | bytes 18440 | tf_op jit(solution)/shard_map/ppermute | solution.py:424
  15.7 4.9 %collective-permute-start.5 = (f32[3,16,32]{2,1,0:T(8,128)}, f32[3,16,32]{2,1,0:T(8,128)S(1)}, u32[]{:S(2)}, u32[]{:S(2)}) collective-permute-start(f32[3,16,32]{2,1,0:T(8,128)} %get-tuple-element.31), channel_id=1, source_target_pairs={{1,2},{2,1},{5,6},{6,5},{9,10},{10,9},{13,14},{14,13},{17,18},{18,... | collective-permute-start | bytes 18440 | tf_op jit(solution)/shard_map/ppermute | solution.py:425
  17.6 3.0 %copy-start.3 = (f32[3,16,32]{2,1,0:T(8,128)}, f32[3,16,32]{2,1,0:T(8,128)S(1)}, u32[]{:S(2)}) copy-start(f32[3,16,32]{2,1,0:T(8,128)S(1)} %collective-permute-done.4.gz_lo) | copy-start | bytes 18436
  20.6 0.6 copy-start.4
  20.6 0.6 copy-start
  20.6 0.7 copy-start.1
  28.7 3.3 %collective-permute-start.6 = (f32[2,2,16,256]{3,2,1,0:T(8,128)}, f32[2,2,16,256]{3,2,1,0:T(8,128)S(1)}, u32[]{:S(2)}, u32[]{:S(2)}) collective-permute-start(f32[2,2,16,256]{3,2,1,0:T(8,128)} %get-tuple-element.32.r_3_), channel_id=1, source_target_pairs={{0,16},{16,0},{1,17},{17,1},{2,18},{18,2},{3,19},{19,3},{4,20},{20... | collective-permute-start | bytes 196616 | tf_op jit(solution)/shard_map/ppermute | solution.py:407
  32.0 0.6 copy-start.7
  32.0 0.7 copy-start.2
  36.2 11.5 %collective-permute-start.7 = (f32[2,32,256]{2,1,0:T(8,128)}, f32[2,32,256]{2,1,0:T(8,128)S(1)}, u32[]{:S(2)}, u32[]{:S(2)}) collective-permute-start(f32[2,32,256]{2,1,0:T(8,128)} %get-tuple-element.36), channel_id=1, source_target_pairs={{0,4},{4,0},{8,12},{12,8},{1,5},{5,1},{9,13},{13,9},{2,6},{6,2},{1... | collective-permute-start | bytes 196616 | tf_op jit(solution)/shard_map/ppermute | solution.py:424
  39.9 7.8 %collective-permute-start.8 = (f32[2,32,256]{2,1,0:T(8,128)}, f32[2,32,256]{2,1,0:T(8,128)S(1)}, u32[]{:S(2)}, u32[]{:S(2)}) collective-permute-start(f32[2,32,256]{2,1,0:T(8,128)} %get-tuple-element.37), channel_id=1, source_target_pairs={{4,8},{8,4},{5,9},{9,5},{6,10},{10,6},{7,11},{11,7},{20,24},{24,20... | collective-permute-start | bytes 196616 | tf_op jit(solution)/shard_map/ppermute | solution.py:425
  42.9 3.2 %collective-permute-start.9 = (f32[2,16,32]{2,1,0:T(8,128)}, f32[2,16,32]{2,1,0:T(8,128)S(1)}, u32[]{:S(2)}, u32[]{:S(2)}) collective-permute-start(f32[2,16,32]{2,1,0:T(8,128)} %get-tuple-element.38), channel_id=1, source_target_pairs={{0,1},{1,0},{2,3},{3,2},{4,5},{5,4},{6,7},{7,6},{8,9},{9,8},{10,11... | collective-permute-start | bytes 12296 | tf_op jit(solution)/shard_map/ppermute | solution.py:424
  43.0 4.7 %collective-permute-start.10 = (f32[2,16,32]{2,1,0:T(8,128)}, f32[2,16,32]{2,1,0:T(8,128)S(1)}, u32[]{:S(2)}, u32[]{:S(2)}) collective-permute-start(f32[2,16,32]{2,1,0:T(8,128)} %get-tuple-element.39), channel_id=1, source_target_pairs={{1,2},{2,1},{5,6},{6,5},{9,10},{10,9},{13,14},{14,13},{17,18},{18,... | collective-permute-start | bytes 12296 | tf_op jit(solution)/shard_map/ppermute | solution.py:425
  46.1 1.6 %copy-start.12 = (f32[2,16,32]{2,1,0:T(8,128)}, f32[2,16,32]{2,1,0:T(8,128)S(1)}, u32[]{:S(2)}) copy-start(f32[2,16,32]{2,1,0:T(8,128)S(1)} %collective-permute-done.9.hz_lo) | copy-start | bytes 12292
  47.7 0.6 copy-start.13
  47.7 0.6 copy-start.5
  47.7 0.6 copy-start.6
  56.3 3.3 %collective-permute-start.11 = (f32[2,2,16,256]{3,2,1,0:T(8,128)}, f32[2,2,16,256]{3,2,1,0:T(8,128)S(1)}, u32[]{:S(2)}, u32[]{:S(2)}) collective-permute-start(f32[2,2,16,256]{3,2,1,0:T(8,128)} %get-tuple-element.40.r_3_), channel_id=1, source_target_pairs={{0,16},{16,0},{1,17},{17,1},{2,18},{18,2},{3,19},{19,3},{4,20},{20... | collective-permute-start | bytes 196616 | tf_op jit(solution)/shard_map/ppermute | solution.py:407
  59.6 0.6 copy-start.8
  63.7 9.5 %collective-permute-start.12 = (f32[1,32,256]{2,1,0:T(8,128)}, f32[1,32,256]{2,1,0:T(8,128)S(1)}, u32[]{:S(2)}, u32[]{:S(2)}) collective-permute-start(f32[1,32,256]{2,1,0:T(8,128)} %get-tuple-element.44), channel_id=1, source_target_pairs={{0,4},{4,0},{8,12},{12,8},{1,5},{5,1},{9,13},{13,9},{2,6},{6,2},{1... | collective-permute-start | bytes 98312 | tf_op jit(solution)/shard_map/ppermute | solution.py:424
  63.7 9.5 %collective-permute-start.13 = (f32[1,32,256]{2,1,0:T(8,128)}, f32[1,32,256]{2,1,0:T(8,128)S(1)}, u32[]{:S(2)}, u32[]{:S(2)}) collective-permute-start(f32[1,32,256]{2,1,0:T(8,128)} %get-tuple-element.45), channel_id=1, source_target_pairs={{4,8},{8,4},{5,9},{9,5},{6,10},{10,6},{7,11},{11,7},{20,24},{24,20... | collective-permute-start | bytes 98312 | tf_op jit(solution)/shard_map/ppermute | solution.py:425
  68.6 2.8 %collective-permute-start.14 = (f32[1,16,32]{2,1,0:T(8,128)}, f32[1,16,32]{2,1,0:T(8,128)S(1)}, u32[]{:S(2)}, u32[]{:S(2)}) collective-permute-start(f32[1,16,32]{2,1,0:T(8,128)} %get-tuple-element.46), channel_id=1, source_target_pairs={{0,1},{1,0},{2,3},{3,2},{4,5},{5,4},{6,7},{7,6},{8,9},{9,8},{10,11... | collective-permute-start | bytes 6152 | tf_op jit(solution)/shard_map/ppermute | solution.py:424
  68.7 4.6 %collective-permute-start.15 = (f32[1,16,32]{2,1,0:T(8,128)}, f32[1,16,32]{2,1,0:T(8,128)S(1)}, u32[]{:S(2)}, u32[]{:S(2)}) collective-permute-start(f32[1,16,32]{2,1,0:T(8,128)} %get-tuple-element.47), channel_id=1, source_target_pairs={{1,2},{2,1},{5,6},{6,5},{9,10},{10,9},{13,14},{14,13},{17,18},{18,... | collective-permute-start | bytes 6152 | tf_op jit(solution)/shard_map/ppermute | solution.py:425
  71.4 1.9 %copy-start.14 = (f32[1,16,32]{2,1,0:T(8,128)}, f32[1,16,32]{2,1,0:T(8,128)S(1)}, u32[]{:S(2)}) copy-start(f32[1,16,32]{2,1,0:T(8,128)S(1)} %collective-permute-done.14.hz_lo) | copy-start | bytes 6148
  73.3 0.6 copy-start.15
  73.3 0.6 copy-start.10
  73.3 0.6 copy-start.11

commit v4 on v2

--- a/solution.py
+++ b/solution.py
@@ -14,6 +14,10 @@
 def face_value(mobility_here, mobility_there, label_here, label_there):
     harmonic = 2.0 * mobility_here * mobility_there / (mobility_here + mobility_there)
     return harmonic * jnp.where(label_here != label_there, boundary_gain, 1.0)
+
+
+def _kernel_call(*args, **kwargs):
+    return pl.pallas_call(*args, **kwargs)
 
 
 def _vmem():
@@ -134,7 +138,7 @@
     return mob, lab, mob_n, _faces(mob, lab, mob_n, lab_n)
 
 
-def _sweep(m, lower, pivots, ratios, source):
+def _sweep(m, lower, inv_pivots, ratios, source):
     ys = [None] * m
     prev = None
     for r in range(m - 1):
@@ -145,7 +149,7 @@
             num = -(lower[r] * prev)
         elif prev is not None:
             num = num - lower[r] * prev
-        ys[r] = num / pivots[r]
+        ys[r] = num * inv_pivots[r]
         prev = ys[r]
     xs = [None] * m
     prev = None
@@ -192,14 +196,15 @@
             pivots.append(piv)
             ratios.append(rat)
             prev = rat
+        inv_piv = [1.0 / x for x in pivots]
         left_src = [lower[0]] + [None] * (m - 1)
         right_src = [None] * (m - 2) + [upper[m - 2], None]
-        left = _sweep(m, lower, pivots, ratios, left_src)
-        right = _sweep(m, lower, pivots, ratios, right_src)
+        left = _sweep(m, lower, inv_piv, ratios, left_src)
+        right = _sweep(m, lower, inv_piv, ratios, right_src)
         for r in range(m):
             fac_ref[c, 0, r] = lower[r]
             fac_ref[c, 1, r] = ratios[r] if r < m - 1 else zero
-            fac_ref[c, 2, r] = pivots[r] if r < m - 1 else zero + 1.0
+            fac_ref[c, 2, r] = inv_piv[r] if r < m - 1 else zero + 1.0
             lr_ref[c, 0, r] = left[r] if r < m - 1 else zero
             lr_ref[c, 1, r] = right[r] if r < m - 1 else zero - 1.0
         last_lower = lower[m - 1]
@@ -383,7 +388,7 @@
 
 
 def _first_call(m, ny, nz):
-    return pl.pallas_call(
+    return _kernel_call(
         _first_kernel,
         out_shape=(
             jax.ShapeDtypeStruct((2, m, ny, nz), F32),
@@ -441,7 +446,7 @@
     ctl = jnp.stack(
         [lax.axis_index("blk"), 1 - lax.axis_index("gy") % 2, 1 - lax.axis_index("gz") % 2]
     ).astype(jnp.int32)
-    outs = pl.pallas_call(
+    outs = _kernel_call(
         _edge_kernel,
         out_shape=_edge_shapes(3, m, ny, nz) + (jax.ShapeDtypeStruct((2, 2, ny, nz), F32),),
         in_specs=[_smem()] + [_vmem()] * 3,
@@ -457,7 +462,7 @@
         lo_i, hi_i = 0, 1
     gy_lo, gy_hi, gz_lo, gz_hi = _yz_halos(*outs[:4])
 
-    fac, lr, rows = pl.pallas_call(
+    fac, lr, rows = _kernel_call(
         lambda *r: _factor_kernel(cycle_step, lo_i, hi_i, *r),
         out_shape=(
             jax.ShapeDtypeStruct((2, 3, m, ny, nz), F32),
@@ -469,13 +474,11 @@
     )(pore_mask, grain_label, bx)
     gathered = _gather_blk(rows)
 
-    loc, vals = _first_call(m, ny, nz)(
-        ctl, vacancy, cotangent, pore_mask, grain_label, fac, gy_lo, gy_hi, gz_lo, gz_hi
-    )
+    loc, vals = _first_call(m, ny, nz)(ctl, vacancy, cotangent, pore_mask, grain_label, fac, gy_lo, gy_hi, gz_lo, gz_hi)
     gathered1 = _gather_blk(vals)
     pos = ctl
 
-    outs = pl.pallas_call(
+    outs = _kernel_call(
         lambda *r: _combine_kernel(n_blk, True, {0: 0, 1: 1}, *r),
         out_shape=(jax.ShapeDtypeStruct((2, m, ny, nz), F32),) + _edge_shapes(2, m, ny, nz),
         in_specs=[_smem()] + [_vmem()] * (2 * n_blk + 2),
@@ -485,7 +488,7 @@
     fa = outs[0]
 
     hy_lo, hy_hi, hz_lo, hz_hi = _yz_halos(*outs[1:])
-    loc2, vals2 = pl.pallas_call(
+    loc2, vals2 = _kernel_call(
         _second_kernel,
         out_shape=(
             jax.ShapeDtypeStruct((2, m, ny, nz), F32),
@@ -496,7 +499,7 @@
     )(ctl, pore_mask, grain_label, fa, fac, gy_lo, gy_hi, gz_lo, gz_hi, hy_lo, hy_hi, hz_lo, hz_hi)
 
     gathered2 = _gather_blk(vals2)
-    outs = pl.pallas_call(
+    outs = _kernel_call(
         lambda *r: _combine_kernel(n_blk, False, {1: 0}, *r),
         out_shape=(shape, shape) + _edge_shapes(1, m, ny, nz),
         in_specs=[_smem()] + [_vmem()] * (2 * n_blk + 2),
@@ -506,7 +509,7 @@
     final_field, adjoint_two = outs[:2]
 
     a2_lo, a2_hi, a2z_lo, a2z_hi = _yz_halos(*outs[2:])
-    gradient = pl.pallas_call(
+    gradient = _kernel_call(
         _gradient_kernel,
         out_shape=shape,
         in_specs=[_smem()] + [_vmem()] * 11,

time: 74.6 us -> 74.6 us (level)
  no operation moved by 1% of the time
where the time goes in v4:
time: 74.6 us; the launch traced here: 74.3 us
  Pallas kernels  29.8 us (40%)
  starting transfers between devices  25.5 us (34%)
  waiting for transfers between devices  13.7 us (18%)
  local copies, waits for them, and re-layouts  3.82 us (5%)
  between operations  0.83 us (1%)
    ppermute x6, starting transfers between devices, _swap(): lax.ppermute(x_b, axis, pairs_b)  16.6 us
    ppermute x6, waiting for transfers between devices, _swap(): lax.ppermute(x_b, axis, pairs_b)  6.46 us
    pallas_call x1, Pallas kernels, _shards(): _kernel_call(_second_kernel, out_shape=(jax.ShapeDtypeStruct((2, m, ny, n...  6.1 us
    ppermute x6, starting transfers between devices, _swap(): recv_a = lax.ppermute(x_a, axis, pairs_a)  6.03 us
    pallas_call x1, Pallas kernels, _shards(): _first_call(m, ny, nz)  5.69 us
    ppermute x3, waiting for transfers between devices, _gather_blk(): parts.append(lax.ppermute(x, 'blk', [(j, (j + k) % n) for j in range(n)]))  5.3 us
    pallas_call x1, Pallas kernels, _shards(): _kernel_call(lambda *r: _factor_kernel(cycle_step, lo_i, hi_i, *r), out_s...  4.45 us
    pallas_call x1, Pallas kernels, _shards(): _kernel_call(_gradient_kernel, out_shape=shape, in_specs=[_smem()] + [_vm...  3.95 us
  transfers between devices with their start and end apart: 16, of which 7 were waited for; matrix products, arithmetic and copies ran while one was open for 0% of the time, Pallas kernels for 14%

profile of v4, /device:TPU:17, one launch (start us, length us, event | category | flops | bytes accessed | tf_op | source)
XLA Modules:
  0.0 74.3 jit_solution(17964540890256752510)
XLA Ops:
  0.6 0.6 pad_add_fusion.ctl_ref.r_0_
  1.3 2.6 %shard_map.59 = (f32[3,32,256]{2,1,0:T(8,128)}, f32[3,32,256]{2,1,0:T(8,128)}, f32[3,16,32]{2,1,0:T(8,128)}, f32[3,16,32]{2,1,0:T(8,128)}, f32[2,2,16,256]{3,2,1,0:T(8,128)}) custom-call(s32[3]{0:T(128)} %pad_add_fusion.ctl_ref.r_0_, f32[32,16,256]{2,1,0:T(8,128)} %vac_ref.3, s32[32,16,256]{2,1,0:T(8,128)} %pore_ref.7, s32[32,16,256]{2,1,0:T(8,128)} %lab_ref.7), custom_call_target="tpu_custom_call" | custom-call | tf_op jit(solution)/shard_map/pallas_call | solution.py:449
  3.9 1.2 %collective-permute-start = (f32[2,2,16,256]{3,2,1,0:T(8,128)}, f32[2,2,16,256]{3,2,1,0:T(8,128)S(1)}, u32[]{:S(2)}, u32[]{:S(2)}) collective-permute-start(f32[2,2,16,256]{3,2,1,0:T(8,128)} %get-tuple-element.25), channel_id=1, source_target_pairs={{0,16},{16,0},{1,17},{17,1},{2,18},{18,2},{3,19},{19,3},{4,20},{20... | collective-permute-start | bytes 196616 | tf_op jit(solution)/shard_map/ppermute | solution.py:457
  5.1 0.9 %collective-permute-start.2 = (f32[3,32,256]{2,1,0:T(8,128)}, f32[3,32,256]{2,1,0:T(8,128)S(1)}, u32[]{:S(2)}, u32[]{:S(2)}) collective-permute-start(f32[3,32,256]{2,1,0:T(8,128)} %get-tuple-element.28), channel_id=1, source_target_pairs={{0,4},{4,0},{8,12},{12,8},{1,5},{5,1},{9,13},{13,9},{2,6},{6,2},{1... | collective-permute-start | bytes 294920 | tf_op jit(solution)/shard_map/ppermute | solution.py:431
  6.0 3.0 %collective-permute-start.3 = (f32[3,32,256]{2,1,0:T(8,128)}, f32[3,32,256]{2,1,0:T(8,128)S(1)}, u32[]{:S(2)}, u32[]{:S(2)}) collective-permute-start(f32[3,32,256]{2,1,0:T(8,128)} %get-tuple-element.29), channel_id=1, source_target_pairs={{4,8},{8,4},{5,9},{9,5},{6,10},{10,6},{7,11},{11,7},{20,24},{24,20... | collective-permute-start | bytes 294920 | tf_op jit(solution)/shard_map/ppermute | solution.py:432
  9.1 0.0 collective-permute-done.r_2_
  9.1 0.6 copy-done.9
  9.7 4.4 %shard_map.60 = (f32[2,3,32,16,256]{4,3,2,1,0:T(8,128)}, f32[2,2,32,16,256]{4,3,2,1,0:T(8,128)}, f32[2,5,16,256]{3,2,1,0:T(8,128)}) custom-call(s32[32,16,256]{2,1,0:T(8,128)} %pore_ref.7, s32[32,16,256]{2,1,0:T(8,128)} %lab_ref.7, f32[2,2,16,256]{3,2,1,0:T(8,128)} %copy-done.9), custom_call_target="tpu_custom_call" | custom-call | tf_op jit(solution)/shard_map/pallas_call | solution.py:465
  14.1 0.3 collective-permute-start.1
  14.4 1.3 %collective-permute-start.4 = (f32[3,16,32]{2,1,0:T(8,128)}, f32[3,16,32]{2,1,0:T(8,128)S(1)}, u32[]{:S(2)}, u32[]{:S(2)}) collective-permute-start(f32[3,16,32]{2,1,0:T(8,128)} %get-tuple-element.30), channel_id=1, source_target_pairs={{0,1},{1,0},{2,3},{3,2},{4,5},{5,4},{6,7},{7,6},{8,9},{9,8},{10,11... | collective-permute-start | bytes 18440 | tf_op jit(solution)/shard_map/ppermute | solution.py:431
  15.7 1.9 %collective-permute-start.5 = (f32[3,16,32]{2,1,0:T(8,128)}, f32[3,16,32]{2,1,0:T(8,128)S(1)}, u32[]{:S(2)}, u32[]{:S(2)}) collective-permute-start(f32[3,16,32]{2,1,0:T(8,128)} %get-tuple-element.31), channel_id=1, source_target_pairs={{1,2},{2,1},{5,6},{6,5},{9,10},{10,9},{13,14},{14,13},{17,18},{18,... | collective-permute-start | bytes 18440 | tf_op jit(solution)/shard_map/ppermute | solution.py:432
  17.6 0.0 collective-permute-done.4.gz_lo
  17.6 2.9 %collective-permute-done.5.gz_hi = f32[3,16,32]{2,1,0:T(8,128)S(1)} collective-permute-done((f32[3,16,32]{2,1,0:T(8,128)}, f32[3,16,32]{2,1,0:T(8,128)S(1)}, u32[]{:S(2)}, u32[]{:S(2)}) %collective-permute-start.5) | collective-permute-done | bytes 6176 | tf_op jit(solution)/shard_map/ppermute | solution.py:432
  20.6 0.0 collective-permute-done.2.gy_lo
  20.6 0.0 collective-permute-done.3.gy_hi
  20.6 0.6 copy-done.4
  21.2 0.1 copy-done
  21.2 0.0 copy-done.1
  21.2 5.7 %shard_map.61 = (f32[2,32,16,256]{3,2,1,0:T(8,128)}, f32[2,2,16,256]{3,2,1,0:T(8,128)}) custom-call(s32[3]{0:T(128)} %pad_add_fusion.ctl_ref.r_0_, f32[32,16,256]{2,1,0:T(8,128)} %vac_ref.3, f32[32,16,256]{2,1,0:T(8,128)} %cot_ref.1, s32[32,16,256]{2,1,0:T(8,128)} %pore_ref.7, s32[32,16,256]{2,1,0:T(8,128)} %lab_ref.7, ...), custom_call_target="tpu_custom_call" | custom-call | tf_op jit(solution)/shard_map/pallas_call | solution.py:477
  26.9 1.1 %collective-permute-start.6 = (f32[2,2,16,256]{3,2,1,0:T(8,128)}, f32[2,2,16,256]{3,2,1,0:T(8,128)S(1)}, u32[]{:S(2)}, u32[]{:S(2)}) collective-permute-start(f32[2,2,16,256]{3,2,1,0:T(8,128)} %get-tuple-element.32.r_3_), channel_id=1, source_target_pairs={{0,16},{16,0},{1,17},{17,1},{2,18},{18,2},{3,19},{19,3},{4,20},{20... | collective-permute-start | bytes 196616 | tf_op jit(solution)/shard_map/ppermute | solution.py:414
  28.0 2.2 %collective-permute-done.6.r_4_ = f32[2,2,16,256]{3,2,1,0:T(8,128)S(1)} collective-permute-done((f32[2,2,16,256]{3,2,1,0:T(8,128)}, f32[2,2,16,256]{3,2,1,0:T(8,128)S(1)}, u32[]{:S(2)}, u32[]{:S(2)}) %collective-permute-start.6) | collective-permute-done | bytes 65568 | tf_op jit(solution)/shard_map/ppermute | solution.py:414
  30.3 0.0 collective-permute-done.1.r_2_
  30.3 0.6 copy-done.7
  30.9 0.1 copy-done.2
  31.0 3.5 %shard_map.62 = (f32[2,32,16,256]{3,2,1,0:T(8,128)}, f32[2,32,256]{2,1,0:T(8,128)}, f32[2,32,256]{2,1,0:T(8,128)}, f32[2,16,32]{2,1,0:T(8,128)}, f32[2,16,32]{2,1,0:T(8,128)}) custom-call(s32[3]{0:T(128)} %pad_add_fusion.ctl_ref.r_0_, f32[2,5,16,256]{3,2,1,0:T(8,128)} %get-tuple-element.26.r_1_, f32[2,5,16,256]{3,2,1,0:T(8,128)} %copy-done.2, ...), custom_call_target="tpu_custom_call" | custom-call | tf_op jit(solution)/shard_map/pallas_call | solution.py:481
  34.5 3.6 %collective-permute-start.7 = (f32[2,32,256]{2,1,0:T(8,128)}, f32[2,32,256]{2,1,0:T(8,128)S(1)}, u32[]{:S(2)}, u32[]{:S(2)}) collective-permute-start(f32[2,32,256]{2,1,0:T(8,128)} %get-tuple-element.36), channel_id=1, source_target_pairs={{0,4},{4,0},{8,12},{12,8},{1,5},{5,1},{9,13},{13,9},{2,6},{6,2},{1... | collective-permute-start | bytes 196616 | tf_op jit(solution)/shard_map/ppermute | solution.py:431
  38.1 3.0 %collective-permute-start.8 = (f32[2,32,256]{2,1,0:T(8,128)}, f32[2,32,256]{2,1,0:T(8,128)S(1)}, u32[]{:S(2)}, u32[]{:S(2)}) collective-permute-start(f32[2,32,256]{2,1,0:T(8,128)} %get-tuple-element.37), channel_id=1, source_target_pairs={{4,8},{8,4},{5,9},{9,5},{6,10},{10,6},{7,11},{11,7},{20,24},{24,20... | collective-permute-start | bytes 196616 | tf_op jit(solution)/shard_map/ppermute | solution.py:432
  41.2 0.1 collective-permute-start.9
  41.3 1.9 %collective-permute-start.10 = (f32[2,16,32]{2,1,0:T(8,128)}, f32[2,16,32]{2,1,0:T(8,128)S(1)}, u32[]{:S(2)}, u32[]{:S(2)}) collective-permute-start(f32[2,16,32]{2,1,0:T(8,128)} %get-tuple-element.39), channel_id=1, source_target_pairs={{1,2},{2,1},{5,6},{6,5},{9,10},{10,9},{13,14},{14,13},{17,18},{18,... | collective-permute-start | bytes 12296 | tf_op jit(solution)/shard_map/ppermute | solution.py:432
  43.2 1.2 %collective-permute-done.9.hz_lo = f32[2,16,32]{2,1,0:T(8,128)S(1)} collective-permute-done((f32[2,16,32]{2,1,0:T(8,128)}, f32[2,16,32]{2,1,0:T(8,128)S(1)}, u32[]{:S(2)}, u32[]{:S(2)}) %collective-permute-start.9) | collective-permute-done | bytes 4128 | tf_op jit(solution)/shard_map/ppermute | solution.py:431
  44.4 1.6 %collective-permute-done.10.hz_hi = f32[2,16,32]{2,1,0:T(8,128)S(1)} collective-permute-done((f32[2,16,32]{2,1,0:T(8,128)}, f32[2,16,32]{2,1,0:T(8,128)S(1)}, u32[]{:S(2)}, u32[]{:S(2)}) %collective-permute-start.10) | collective-permute-done | bytes 4128 | tf_op jit(solution)/shard_map/ppermute | solution.py:432
  46.0 0.6 copy-done.13
  46.6 0.0 copy-done.5
  46.6 0.0 copy-done.6
  46.6 6.1 %shard_map.63 = (f32[2,32,16,256]{3,2,1,0:T(8,128)}, f32[2,2,16,256]{3,2,1,0:T(8,128)}) custom-call(s32[3]{0:T(128)} %pad_add_fusion.ctl_ref.r_0_, s32[32,16,256]{2,1,0:T(8,128)} %pore_ref.7, s32[32,16,256]{2,1,0:T(8,128)} %lab_ref.7, f32[2,32,16,256]{3,2,1,0:T(8,128)} %get-tuple-element.35.fa_ref, f32[2,3,32,16,256]{4,3,2,1,0:T(8,128)} %get-tuple-element.27.fac_ref, ...), custom_call_target="tpu_custom_call" | custom-call | tf_op jit(solution)/shard_map/pallas_call | solution.py:491
  52.7 0.3 collective-permute-start.11
  53.0 3.1 %collective-permute-done.11.r_4_ = f32[2,2,16,256]{3,2,1,0:T(8,128)S(1)} collective-permute-done((f32[2,2,16,256]{3,2,1,0:T(8,128)}, f32[2,2,16,256]{3,2,1,0:T(8,128)S(1)}, u32[]{:S(2)}, u32[]{:S(2)}) %collective-permute-start.11) | collective-permute-done | bytes 65568 | tf_op jit(solution)/shard_map/ppermute | solution.py:414
  56.1 0.6 copy-done.8
  56.7 3.5 %shard_map.64 = (f32[32,16,256]{2,1,0:T(8,128)}, f32[32,16,256]{2,1,0:T(8,128)}, f32[1,32,256]{2,1,0:T(8,128)}, f32[1,32,256]{2,1,0:T(8,128)}, f32[1,16,32]{2,1,0:T(8,128)}, /*index=5*/f32[1,16,32]{2,1,0:T(8,128)}) custom-call(s32[3]{0:T(128)} %pad_add_fusion.ctl_ref.r_0_, f32[2,5,16,256]{3,2,1,0:T(8,128)} %get-tuple-element.26.r_1_, ...), custom_call_target="tpu_custom_call" | custom-call | tf_op jit(solution)/shard_map/pallas_call | solution.py:502
  60.2 4.8 %collective-permute-start.13 = (f32[1,32,256]{2,1,0:T(8,128)}, f32[1,32,256]{2,1,0:T(8,128)S(1)}, u32[]{:S(2)}, u32[]{:S(2)}) collective-permute-start(f32[1,32,256]{2,1,0:T(8,128)} %get-tuple-element.45), channel_id=1, source_target_pairs={{4,8},{8,4},{5,9},{9,5},{6,10},{10,6},{7,11},{11,7},{20,24},{24,20... | collective-permute-start | bytes 98312 | tf_op jit(solution)/shard_map/ppermute | solution.py:432
  65.0 0.1 collective-permute-start.14
  65.1 1.9 %collective-permute-start.15 = (f32[1,16,32]{2,1,0:T(8,128)}, f32[1,16,32]{2,1,0:T(8,128)S(1)}, u32[]{:S(2)}, u32[]{:S(2)}) collective-permute-start(f32[1,16,32]{2,1,0:T(8,128)} %get-tuple-element.47), channel_id=1, source_target_pairs={{1,2},{2,1},{5,6},{6,5},{9,10},{10,9},{13,14},{14,13},{17,18},{18,... | collective-permute-start | bytes 6152 | tf_op jit(solution)/shard_map/ppermute | solution.py:432
  67.0 0.8 %collective-permute-done.14.hz_lo = f32[1,16,32]{2,1,0:T(8,128)S(1)} collective-permute-done((f32[1,16,32]{2,1,0:T(8,128)}, f32[1,16,32]{2,1,0:T(8,128)S(1)}, u32[]{:S(2)}, u32[]{:S(2)}) %collective-permute-start.14) | collective-permute-done | bytes 2080 | tf_op jit(solution)/shard_map/ppermute | solution.py:431
  67.8 1.9 %collective-permute-done.15.hz_hi = f32[1,16,32]{2,1,0:T(8,128)S(1)} collective-permute-done((f32[1,16,32]{2,1,0:T(8,128)}, f32[1,16,32]{2,1,0:T(8,128)S(1)}, u32[]{:S(2)}, u32[]{:S(2)}) %collective-permute-start.15) | collective-permute-done | bytes 2080 | tf_op jit(solution)/shard_map/ppermute | solution.py:432
  69.7 0.6 copy-done.15
  70.3 0.0 copy-done.10
  70.3 0.0 copy-done.11
  70.3 3.9 %shard_map.65 = f32[32,16,256]{2,1,0:T(8,128)} custom-call(s32[3]{0:T(128)} %pad_add_fusion.ctl_ref.r_0_, s32[32,16,256]{2,1,0:T(8,128)} %pore_ref.7, s32[32,16,256]{2,1,0:T(8,128)} %lab_ref.7, f32[32,16,256]{2,1,0:T(8,128)} %get-tuple-element.43.a2_ref, f32[3,32,256]{2,1,0:T(8,128)} %copy-done, f32[3,32,256]{2,1,0:T(8,128)} %copy-done.1, ...), custom_call_target="tpu_custom_call" | custom-call | tf_op jit(solution)/shard_map/pallas_call | solution.py:512
  (24 shorter events, 0.0 us)
Async XLA Ops:
  3.9 5.2 %collective-permute-start = (f32[2,2,16,256]{3,2,1,0:T(8,128)}, f32[2,2,16,256]{3,2,1,0:T(8,128)S(1)}, u32[]{:S(2)}, u32[]{:S(2)}) collective-permute-start(f32[2,2,16,256]{3,2,1,0:T(8,128)} %get-tuple-element.25), channel_id=1, source_target_pairs={{0,16},{16,0},{1,17},{17,1},{2,18},{18,2},{3,19},{19,3},{4,20},{20... | collective-permute-start | bytes 196616 | tf_op jit(solution)/shard_map/ppermute | solution.py:457
  5.1 15.5 %collective-permute-start.2 = (f32[3,32,256]{2,1,0:T(8,128)}, f32[3,32,256]{2,1,0:T(8,128)S(1)}, u32[]{:S(2)}, u32[]{:S(2)}) collective-permute-start(f32[3,32,256]{2,1,0:T(8,128)} %get-tuple-element.28), channel_id=1, source_target_pairs={{0,4},{4,0},{8,12},{12,8},{1,5},{5,1},{9,13},{13,9},{2,6},{6,2},{1... | collective-permute-start | bytes 294920 | tf_op jit(solution)/shard_map/ppermute | solution.py:431
  6.0 14.5 %collective-permute-start.3 = (f32[3,32,256]{2,1,0:T(8,128)}, f32[3,32,256]{2,1,0:T(8,128)S(1)}, u32[]{:S(2)}, u32[]{:S(2)}) collective-permute-start(f32[3,32,256]{2,1,0:T(8,128)} %get-tuple-element.29), channel_id=1, source_target_pairs={{4,8},{8,4},{5,9},{9,5},{6,10},{10,6},{7,11},{11,7},{20,24},{24,20... | collective-permute-start | bytes 294920 | tf_op jit(solution)/shard_map/ppermute | solution.py:432
  9.1 0.6 copy-start.9
  14.1 16.1 %collective-permute-start.1 = (f32[2,5,16,256]{3,2,1,0:T(8,128)}, f32[2,5,16,256]{3,2,1,0:T(8,128)S(1)}, u32[]{:S(2)}, u32[]{:S(2)}) collective-permute-start(f32[2,5,16,256]{3,2,1,0:T(8,128)} %get-tuple-element.26.r_1_), channel_id=1, source_target_pairs={{0,16},{16,0},{1,17},{17,1},{2,18},{18,2},{3,19},{19,3},{4,20},{20... | collective-permute-start | bytes 491528 | tf_op jit(solution)/shard_map/ppermute | solution.py:414
  14.4 3.2 %collective-permute-start.4 = (f32[3,16,32]{2,1,0:T(8,128)}, f32[3,16,32]{2,1,0:T(8,128)S(1)}, u32[]{:S(2)}, u32[]{:S(2)}) collective-permute-start(f32[3,16,32]{2,1,0:T(8,128)} %get-tuple-element.30), channel_id=1, source_target_pairs={{0,1},{1,0},{2,3},{3,2},{4,5},{5,4},{6,7},{7,6},{8,9},{9,8},{10,11... | collective-permute-start | bytes 18440 | tf_op jit(solution)/shard_map/ppermute | solution.py:431
  15.7 4.9 %collective-permute-start.5 = (f32[3,16,32]{2,1,0:T(8,128)}, f32[3,16,32]{2,1,0:T(8,128)S(1)}, u32[]{:S(2)}, u32[]{:S(2)}) collective-permute-start(f32[3,16,32]{2,1,0:T(8,128)} %get-tuple-element.31), channel_id=1, source_target_pairs={{1,2},{2,1},{5,6},{6,5},{9,10},{10,9},{13,14},{14,13},{17,18},{18,... | collective-permute-start | bytes 18440 | tf_op jit(solution)/shard_map/ppermute | solution.py:432
  17.6 3.0 %copy-start.3 = (f32[3,16,32]{2,1,0:T(8,128)}, f32[3,16,32]{2,1,0:T(8,128)S(1)}, u32[]{:S(2)}) copy-start(f32[3,16,32]{2,1,0:T(8,128)S(1)} %collective-permute-done.4.gz_lo) | copy-start | bytes 18436
  20.6 0.6 copy-start.4
  20.6 0.6 copy-start
  20.6 0.7 copy-start.1
  26.9 3.3 %collective-permute-start.6 = (f32[2,2,16,256]{3,2,1,0:T(8,128)}, f32[2,2,16,256]{3,2,1,0:T(8,128)S(1)}, u32[]{:S(2)}, u32[]{:S(2)}) collective-permute-start(f32[2,2,16,256]{3,2,1,0:T(8,128)} %get-tuple-element.32.r_3_), channel_id=1, source_target_pairs={{0,16},{16,0},{1,17},{17,1},{2,18},{18,2},{3,19},{19,3},{4,20},{20... | collective-permute-start | bytes 196616 | tf_op jit(solution)/shard_map/ppermute | solution.py:414
  30.3 0.6 copy-start.7
  30.3 0.7 copy-start.2
  34.5 11.5 %collective-permute-start.7 = (f32[2,32,256]{2,1,0:T(8,128)}, f32[2,32,256]{2,1,0:T(8,128)S(1)}, u32[]{:S(2)}, u32[]{:S(2)}) collective-permute-start(f32[2,32,256]{2,1,0:T(8,128)} %get-tuple-element.36), channel_id=1, source_target_pairs={{0,4},{4,0},{8,12},{12,8},{1,5},{5,1},{9,13},{13,9},{2,6},{6,2},{1... | collective-permute-start | bytes 196616 | tf_op jit(solution)/shard_map/ppermute | solution.py:431
  38.1 7.8 %collective-permute-start.8 = (f32[2,32,256]{2,1,0:T(8,128)}, f32[2,32,256]{2,1,0:T(8,128)S(1)}, u32[]{:S(2)}, u32[]{:S(2)}) collective-permute-start(f32[2,32,256]{2,1,0:T(8,128)} %get-tuple-element.37), channel_id=1, source_target_pairs={{4,8},{8,4},{5,9},{9,5},{6,10},{10,6},{7,11},{11,7},{20,24},{24,20... | collective-permute-start | bytes 196616 | tf_op jit(solution)/shard_map/ppermute | solution.py:432
  41.2 3.2 %collective-permute-start.9 = (f32[2,16,32]{2,1,0:T(8,128)}, f32[2,16,32]{2,1,0:T(8,128)S(1)}, u32[]{:S(2)}, u32[]{:S(2)}) collective-permute-start(f32[2,16,32]{2,1,0:T(8,128)} %get-tuple-element.38), channel_id=1, source_target_pairs={{0,1},{1,0},{2,3},{3,2},{4,5},{5,4},{6,7},{7,6},{8,9},{9,8},{10,11... | collective-permute-start | bytes 12296 | tf_op jit(solution)/shard_map/ppermute | solution.py:431
  41.3 4.7 %collective-permute-start.10 = (f32[2,16,32]{2,1,0:T(8,128)}, f32[2,16,32]{2,1,0:T(8,128)S(1)}, u32[]{:S(2)}, u32[]{:S(2)}) collective-permute-start(f32[2,16,32]{2,1,0:T(8,128)} %get-tuple-element.39), channel_id=1, source_target_pairs={{1,2},{2,1},{5,6},{6,5},{9,10},{10,9},{13,14},{14,13},{17,18},{18,... | collective-permute-start | bytes 12296 | tf_op jit(solution)/shard_map/ppermute | solution.py:432
  44.3 1.6 %copy-start.12 = (f32[2,16,32]{2,1,0:T(8,128)}, f32[2,16,32]{2,1,0:T(8,128)S(1)}, u32[]{:S(2)}) copy-start(f32[2,16,32]{2,1,0:T(8,128)S(1)} %collective-permute-done.9.hz_lo) | copy-start | bytes 12292
  46.0 0.6 copy-start.13
  46.0 0.6 copy-start.5
  46.0 0.6 copy-start.6
  52.7 3.3 %collective-permute-start.11 = (f32[2,2,16,256]{3,2,1,0:T(8,128)}, f32[2,2,16,256]{3,2,1,0:T(8,128)S(1)}, u32[]{:S(2)}, u32[]{:S(2)}) collective-permute-start(f32[2,2,16,256]{3,2,1,0:T(8,128)} %get-tuple-element.40.r_3_), channel_id=1, source_target_pairs={{0,16},{16,0},{1,17},{17,1},{2,18},{18,2},{3,19},{19,3},{4,20},{20... | collective-permute-start | bytes 196616 | tf_op jit(solution)/shard_map/ppermute | solution.py:414
  56.1 0.6 copy-start.8
  60.2 9.5 %collective-permute-start.12 = (f32[1,32,256]{2,1,0:T(8,128)}, f32[1,32,256]{2,1,0:T(8,128)S(1)}, u32[]{:S(2)}, u32[]{:S(2)}) collective-permute-start(f32[1,32,256]{2,1,0:T(8,128)} %get-tuple-element.44), channel_id=1, source_target_pairs={{0,4},{4,0},{8,12},{12,8},{1,5},{5,1},{9,13},{13,9},{2,6},{6,2},{1... | collective-permute-start | bytes 98312 | tf_op jit(solution)/shard_map/ppermute | solution.py:431
  60.2 9.5 %collective-permute-start.13 = (f32[1,32,256]{2,1,0:T(8,128)}, f32[1,32,256]{2,1,0:T(8,128)S(1)}, u32[]{:S(2)}, u32[]{:S(2)}) collective-permute-start(f32[1,32,256]{2,1,0:T(8,128)} %get-tuple-element.45), channel_id=1, source_target_pairs={{4,8},{8,4},{5,9},{9,5},{6,10},{10,6},{7,11},{11,7},{20,24},{24,20... | collective-permute-start | bytes 98312 | tf_op jit(solution)/shard_map/ppermute | solution.py:432
  65.0 2.8 %collective-permute-start.14 = (f32[1,16,32]{2,1,0:T(8,128)}, f32[1,16,32]{2,1,0:T(8,128)S(1)}, u32[]{:S(2)}, u32[]{:S(2)}) collective-permute-start(f32[1,16,32]{2,1,0:T(8,128)} %get-tuple-element.46), channel_id=1, source_target_pairs={{0,1},{1,0},{2,3},{3,2},{4,5},{5,4},{6,7},{7,6},{8,9},{9,8},{10,11... | collective-permute-start | bytes 6152 | tf_op jit(solution)/shard_map/ppermute | solution.py:431
  65.1 4.6 %collective-permute-start.15 = (f32[1,16,32]{2,1,0:T(8,128)}, f32[1,16,32]{2,1,0:T(8,128)S(1)}, u32[]{:S(2)}, u32[]{:S(2)}) collective-permute-start(f32[1,16,32]{2,1,0:T(8,128)} %get-tuple-element.47), channel_id=1, source_target_pairs={{1,2},{2,1},{5,6},{6,5},{9,10},{10,9},{13,14},{14,13},{17,18},{18,... | collective-permute-start | bytes 6152 | tf_op jit(solution)/shard_map/ppermute | solution.py:432
  67.8 1.9 %copy-start.14 = (f32[1,16,32]{2,1,0:T(8,128)}, f32[1,16,32]{2,1,0:T(8,128)S(1)}, u32[]{:S(2)}) copy-start(f32[1,16,32]{2,1,0:T(8,128)S(1)} %collective-permute-done.14.hz_lo) | copy-start | bytes 6148
  69.7 0.6 copy-start.15
  69.7 0.6 copy-start.10
  69.7 0.6 copy-start.11

commit v5 on v2

--- a/solution.py
+++ b/solution.py
@@ -134,7 +134,7 @@
     return mob, lab, mob_n, _faces(mob, lab, mob_n, lab_n)
 
 
-def _sweep(m, lower, pivots, ratios, source):
+def _sweep(m, lower, inv_pivots, ratios, source):
     ys = [None] * m
     prev = None
     for r in range(m - 1):
@@ -145,7 +145,7 @@
             num = -(lower[r] * prev)
         elif prev is not None:
             num = num - lower[r] * prev
-        ys[r] = num / pivots[r]
+        ys[r] = num * inv_pivots[r]
         prev = ys[r]
     xs = [None] * m
     prev = None
@@ -192,14 +192,15 @@
             pivots.append(piv)
             ratios.append(rat)
             prev = rat
+        inv_piv = [1.0 / x for x in pivots]
         left_src = [lower[0]] + [None] * (m - 1)
         right_src = [None] * (m - 2) + [upper[m - 2], None]
-        left = _sweep(m, lower, pivots, ratios, left_src)
-        right = _sweep(m, lower, pivots, ratios, right_src)
+        left = _sweep(m, lower, inv_piv, ratios, left_src)
+        right = _sweep(m, lower, inv_piv, ratios, right_src)
         for r in range(m):
             fac_ref[c, 0, r] = lower[r]
             fac_ref[c, 1, r] = ratios[r] if r < m - 1 else zero
-            fac_ref[c, 2, r] = pivots[r] if r < m - 1 else zero + 1.0
+            fac_ref[c, 2, r] = inv_piv[r] if r < m - 1 else zero + 1.0
             lr_ref[c, 0, r] = left[r] if r < m - 1 else zero
             lr_ref[c, 1, r] = right[r] if r < m - 1 else zero - 1.0
         last_lower = lower[m - 1]
@@ -441,6 +442,16 @@
     ctl = jnp.stack(
         [lax.axis_index("blk"), 1 - lax.axis_index("gy") % 2, 1 - lax.axis_index("gz") % 2]
     ).astype(jnp.int32)
+    mob_ends = 1.0 + 2.0 * jnp.stack([pore_mask[0], pore_mask[m - 1]]).astype(F32)
+    lab_ends = jnp.stack([grain_label[0], grain_label[m - 1]]).astype(F32)
+    ends = jnp.stack([mob_ends, lab_ends], axis=1)
+    if n_blk == 2:
+        bx = lax.ppermute(ends, "blk", [(0, 1), (1, 0)])
+        lo_i, hi_i = 1, 0
+    else:
+        bx_lo, bx_hi = _exchange(ends[0], ends[1], "blk", True)
+        bx = jnp.stack([bx_lo, bx_hi])
+        lo_i, hi_i = 0, 1
     outs = pl.pallas_call(
         _edge_kernel,
         out_shape=_edge_shapes(3, m, ny, nz) + (jax.ShapeDtypeStruct((2, 2, ny, nz), F32),),
@@ -448,13 +459,6 @@
         out_specs=tuple(_vmem() for _ in range(5)),
         scratch_shapes=_edge_scratch(3, m, ny, nz),
     )(ctl, vacancy, pore_mask, grain_label)
-    if n_blk == 2:
-        bx = lax.ppermute(outs[4], "blk", [(0, 1), (1, 0)])
-        lo_i, hi_i = 1, 0
-    else:
-        bx_lo, bx_hi = _exchange(outs[4][0], outs[4][1], "blk", True)
-        bx = jnp.stack([bx_lo, bx_hi])
-        lo_i, hi_i = 0, 1
     gy_lo, gy_hi, gz_lo, gz_hi = _yz_halos(*outs[:4])
 
     fac, lr, rows = pl.pallas_call(

time: 74.6 us -> 74.4 us (level)
  the two profiles are of different devices: /device:TPU:17 before, /device:TPU:19 now
where the time goes in v5:
time: 74.4 us; the launch traced here: 73.8 us
  Pallas kernels  29.8 us (40%)
  starting transfers between devices  22.2 us (30%)
  waiting for transfers between devices  15 us (20%)
  local copies, waits for them, and re-layouts  5.29 us (7%)
  between operations  0.83 us (1%)
    ppermute x6, starting transfers between devices, _swap(): lax.ppermute(x_b, axis, pairs_b)  17.4 us
    ppermute x3, waiting for transfers between devices, _gather_blk(): parts.append(lax.ppermute(x, 'blk', [(j, (j + k) % n) for j in range(n)]))  6.75 us
    ppermute x6, waiting for transfers between devices, _swap(): lax.ppermute(x_b, axis, pairs_b)  6.65 us
    pallas_call x1, Pallas kernels, _shards(): pl.pallas_call(_second_kernel, out_shape=(jax.ShapeDtypeStruct((2, m, ny,...  6.11 us
    pallas_call x1, Pallas kernels, _shards(): _first_call(m, ny, nz)  5.7 us
    pallas_call x1, Pallas kernels, _shards(): pl.pallas_call(lambda *r: _factor_kernel(cycle_step, lo_i, hi_i, *r), out...  4.45 us
    pallas_call x1, Pallas kernels, _shards(): pl.pallas_call(_gradient_kernel, out_shape=shape, in_specs=[_smem()] + [_...  3.95 us
    unnamed x32, local copies, waits for them, and re-layouts  3.81 us
  transfers between devices with their start and end apart: 16, of which 7 were waited for; matrix products, arithmetic and copies ran while one was open for 1% of the time, Pallas kernels for 17%

profile of v5, /device:TPU:19, one launch (start us, length us, event | category | flops | bytes accessed | tf_op | source)
XLA Modules:
  0.0 73.8 jit_solution(11578113274119549300)
XLA Ops:
  0.6 0.7 %slice_bitcast_fusion.1 = (s32[1,1,16,256]{3,2,1,0:T(8,128)S(1)}, s32[1,1,16,256]{3,2,1,0:T(8,128)S(1)}) fusion(s32[32,16,256]{2,1,0:T(8,128)} %lab_ref.7), kind=kLoop, calls=%fused_computation.6 | loop fusion | bytes 65536 | tf_op jit(solution)/shard_map/stack | solution.py:446
  1.4 0.7 slice_bitcast_fusion.3
  2.1 0.3 collective-permute-start
  2.5 0.6 pad_add_fusion.ctl_ref.r_0_
  3.1 2.6 %shard_map.60 = (f32[3,32,256]{2,1,0:T(8,128)}, f32[3,32,256]{2,1,0:T(8,128)}, f32[3,16,32]{2,1,0:T(8,128)}, f32[3,16,32]{2,1,0:T(8,128)}, f32[2,2,16,256]{3,2,1,0:T(8,128)}) custom-call(s32[3]{0:T(128)} %pad_add_fusion.ctl_ref.r_0_, f32[32,16,256]{2,1,0:T(8,128)} %vac_ref.3, s32[32,16,256]{2,1,0:T(8,128)} %pore_ref.7, s32[32,16,256]{2,1,0:T(8,128)} %lab_ref.7), custom_call_target="tpu_custom_call" | custom-call | tf_op jit(solution)/shard_map/pallas_call | solution.py:455
  5.6 0.9 %collective-permute-start.2 = (f32[3,32,256]{2,1,0:T(8,128)}, f32[3,32,256]{2,1,0:T(8,128)S(1)}, u32[]{:S(2)}, u32[]{:S(2)}) collective-permute-start(f32[3,32,256]{2,1,0:T(8,128)} %get-tuple-element.26), channel_id=1, source_target_pairs={{0,4},{4,0},{8,12},{12,8},{1,5},{5,1},{9,13},{13,9},{2,6},{6,2},{1... | collective-permute-start | bytes 294920 | tf_op jit(solution)/shard_map/ppermute | solution.py:427
  6.6 3.0 %collective-permute-start.3 = (f32[3,32,256]{2,1,0:T(8,128)}, f32[3,32,256]{2,1,0:T(8,128)S(1)}, u32[]{:S(2)}, u32[]{:S(2)}) collective-permute-start(f32[3,32,256]{2,1,0:T(8,128)} %get-tuple-element.27), channel_id=1, source_target_pairs={{4,8},{8,4},{5,9},{9,5},{6,10},{10,6},{7,11},{11,7},{20,24},{24,20... | collective-permute-start | bytes 294920 | tf_op jit(solution)/shard_map/ppermute | solution.py:428
  9.6 0.0 collective-permute-done.r_2_
  9.6 0.6 copy-done.9
  10.2 4.4 %shard_map.59 = (f32[2,3,32,16,256]{4,3,2,1,0:T(8,128)}, f32[2,2,32,16,256]{4,3,2,1,0:T(8,128)}, f32[2,5,16,256]{3,2,1,0:T(8,128)}) custom-call(s32[32,16,256]{2,1,0:T(8,128)} %pore_ref.7, s32[32,16,256]{2,1,0:T(8,128)} %lab_ref.7, f32[2,2,16,256]{3,2,1,0:T(8,128)} %copy-done.9), custom_call_target="tpu_custom_call" | custom-call | tf_op jit(solution)/shard_map/pallas_call | solution.py:464
  14.7 1.2 %collective-permute-start.1 = (f32[2,5,16,256]{3,2,1,0:T(8,128)}, f32[2,5,16,256]{3,2,1,0:T(8,128)S(1)}, u32[]{:S(2)}, u32[]{:S(2)}) collective-permute-start(f32[2,5,16,256]{3,2,1,0:T(8,128)} %get-tuple-element.24.r_1_), channel_id=1, source_target_pairs={{0,16},{16,0},{1,17},{17,1},{2,18},{18,2},{3,19},{19,3},{4,20},{20... | collective-permute-start | bytes 491528 | tf_op jit(solution)/shard_map/ppermute | solution.py:410
  15.9 1.3 %collective-permute-start.4 = (f32[3,16,32]{2,1,0:T(8,128)}, f32[3,16,32]{2,1,0:T(8,128)S(1)}, u32[]{:S(2)}, u32[]{:S(2)}) collective-permute-start(f32[3,16,32]{2,1,0:T(8,128)} %get-tuple-element.28), channel_id=1, source_target_pairs={{0,1},{1,0},{2,3},{3,2},{4,5},{5,4},{6,7},{7,6},{8,9},{9,8},{10,11... | collective-permute-start | bytes 18440 | tf_op jit(solution)/shard_map/ppermute | solution.py:427
  17.2 1.9 %collective-permute-start.5 = (f32[3,16,32]{2,1,0:T(8,128)}, f32[3,16,32]{2,1,0:T(8,128)S(1)}, u32[]{:S(2)}, u32[]{:S(2)}) collective-permute-start(f32[3,16,32]{2,1,0:T(8,128)} %get-tuple-element.29), channel_id=1, source_target_pairs={{1,2},{2,1},{5,6},{6,5},{9,10},{10,9},{13,14},{14,13},{17,18},{18,... | collective-permute-start | bytes 18440 | tf_op jit(solution)/shard_map/ppermute | solution.py:428
  19.1 0.0 collective-permute-done.4.gz_lo
  19.1 2.8 %collective-permute-done.5.gz_hi = f32[3,16,32]{2,1,0:T(8,128)S(1)} collective-permute-done((f32[3,16,32]{2,1,0:T(8,128)}, f32[3,16,32]{2,1,0:T(8,128)S(1)}, u32[]{:S(2)}, u32[]{:S(2)}) %collective-permute-start.5) | collective-permute-done | bytes 6176 | tf_op jit(solution)/shard_map/ppermute | solution.py:428
  22.0 0.6 copy-done.4
  22.6 0.0 copy-done
  22.6 0.1 copy-done.1
  22.6 5.7 %shard_map.61 = (f32[2,32,16,256]{3,2,1,0:T(8,128)}, f32[2,2,16,256]{3,2,1,0:T(8,128)}) custom-call(s32[3]{0:T(128)} %pad_add_fusion.ctl_ref.r_0_, f32[32,16,256]{2,1,0:T(8,128)} %vac_ref.3, f32[32,16,256]{2,1,0:T(8,128)} %cot_ref.1, s32[32,16,256]{2,1,0:T(8,128)} %pore_ref.7, s32[32,16,256]{2,1,0:T(8,128)} %lab_ref.7, ...), custom_call_target="tpu_custom_call" | custom-call | tf_op jit(solution)/shard_map/pallas_call | solution.py:476
  28.3 0.3 collective-permute-start.6
  28.6 3.7 %collective-permute-done.6.r_4_ = f32[2,2,16,256]{3,2,1,0:T(8,128)S(1)} collective-permute-done((f32[2,2,16,256]{3,2,1,0:T(8,128)}, f32[2,2,16,256]{3,2,1,0:T(8,128)S(1)}, u32[]{:S(2)}, u32[]{:S(2)}) %collective-permute-start.6) | collective-permute-done | bytes 65568 | tf_op jit(solution)/shard_map/ppermute | solution.py:410
  32.3 0.0 collective-permute-done.1.r_2_
  32.3 0.6 copy-done.7
  32.9 0.1 copy-done.2
  33.0 3.5 %shard_map.62 = (f32[2,32,16,256]{3,2,1,0:T(8,128)}, f32[2,32,256]{2,1,0:T(8,128)}, f32[2,32,256]{2,1,0:T(8,128)}, f32[2,16,32]{2,1,0:T(8,128)}, f32[2,16,32]{2,1,0:T(8,128)}) custom-call(s32[3]{0:T(128)} %pad_add_fusion.ctl_ref.r_0_, f32[2,5,16,256]{3,2,1,0:T(8,128)} %get-tuple-element.24.r_1_, f32[2,5,16,256]{3,2,1,0:T(8,128)} %copy-done.2, ...), custom_call_target="tpu_custom_call" | custom-call | tf_op jit(solution)/shard_map/pallas_call | solution.py:482
  36.5 0.4 collective-permute-start.7
  36.9 4.4 %collective-permute-start.8 = (f32[2,32,256]{2,1,0:T(8,128)}, f32[2,32,256]{2,1,0:T(8,128)S(1)}, u32[]{:S(2)}, u32[]{:S(2)}) collective-permute-start(f32[2,32,256]{2,1,0:T(8,128)} %get-tuple-element.35), channel_id=1, source_target_pairs={{4,8},{8,4},{5,9},{9,5},{6,10},{10,6},{7,11},{11,7},{20,24},{24,20... | collective-permute-start | bytes 196616 | tf_op jit(solution)/shard_map/ppermute | solution.py:428
  41.3 0.1 collective-permute-start.9
  41.4 1.9 %collective-permute-start.10 = (f32[2,16,32]{2,1,0:T(8,128)}, f32[2,16,32]{2,1,0:T(8,128)S(1)}, u32[]{:S(2)}, u32[]{:S(2)}) collective-permute-start(f32[2,16,32]{2,1,0:T(8,128)} %get-tuple-element.37), channel_id=1, source_target_pairs={{1,2},{2,1},{5,6},{6,5},{9,10},{10,9},{13,14},{14,13},{17,18},{18,... | collective-permute-start | bytes 12296 | tf_op jit(solution)/shard_map/ppermute | solution.py:428
  43.3 0.9 %collective-permute-done.9.hz_lo = f32[2,16,32]{2,1,0:T(8,128)S(1)} collective-permute-done((f32[2,16,32]{2,1,0:T(8,128)}, f32[2,16,32]{2,1,0:T(8,128)S(1)}, u32[]{:S(2)}, u32[]{:S(2)}) %collective-permute-start.9) | collective-permute-done | bytes 4128 | tf_op jit(solution)/shard_map/ppermute | solution.py:427
  44.2 1.9 %collective-permute-done.10.hz_hi = f32[2,16,32]{2,1,0:T(8,128)S(1)} collective-permute-done((f32[2,16,32]{2,1,0:T(8,128)}, f32[2,16,32]{2,1,0:T(8,128)S(1)}, u32[]{:S(2)}, u32[]{:S(2)}) %collective-permute-start.10) | collective-permute-done | bytes 4128 | tf_op jit(solution)/shard_map/ppermute | solution.py:428
  46.1 0.6 copy-done.13
  46.7 0.0 copy-done.5
  46.7 0.0 copy-done.6
  46.7 6.1 %shard_map.63 = (f32[2,32,16,256]{3,2,1,0:T(8,128)}, f32[2,2,16,256]{3,2,1,0:T(8,128)}) custom-call(s32[3]{0:T(128)} %pad_add_fusion.ctl_ref.r_0_, s32[32,16,256]{2,1,0:T(8,128)} %pore_ref.7, s32[32,16,256]{2,1,0:T(8,128)} %lab_ref.7, f32[2,32,16,256]{3,2,1,0:T(8,128)} %get-tuple-element.33.fa_ref, f32[2,3,32,16,256]{4,3,2,1,0:T(8,128)} %get-tuple-element.25.fac_ref, ...), custom_call_target="tpu_custom_call" | custom-call | tf_op jit(solution)/shard_map/pallas_call | solution.py:492
  52.8 0.3 collective-permute-start.11
  53.1 3.1 %collective-permute-done.11.r_4_ = f32[2,2,16,256]{3,2,1,0:T(8,128)S(1)} collective-permute-done((f32[2,2,16,256]{3,2,1,0:T(8,128)}, f32[2,2,16,256]{3,2,1,0:T(8,128)S(1)}, u32[]{:S(2)}, u32[]{:S(2)}) %collective-permute-start.11) | collective-permute-done | bytes 65568 | tf_op jit(solution)/shard_map/ppermute | solution.py:410
  56.2 0.6 copy-done.8
  56.8 3.5 %shard_map.64 = (f32[32,16,256]{2,1,0:T(8,128)}, f32[32,16,256]{2,1,0:T(8,128)}, f32[1,32,256]{2,1,0:T(8,128)}, f32[1,32,256]{2,1,0:T(8,128)}, f32[1,16,32]{2,1,0:T(8,128)}, /*index=5*/f32[1,16,32]{2,1,0:T(8,128)}) custom-call(s32[3]{0:T(128)} %pad_add_fusion.ctl_ref.r_0_, f32[2,5,16,256]{3,2,1,0:T(8,128)} %get-tuple-element.24.r_1_, ...), custom_call_target="tpu_custom_call" | custom-call | tf_op jit(solution)/shard_map/pallas_call | solution.py:503
  60.3 4.2 %collective-permute-start.13 = (f32[1,32,256]{2,1,0:T(8,128)}, f32[1,32,256]{2,1,0:T(8,128)S(1)}, u32[]{:S(2)}, u32[]{:S(2)}) collective-permute-start(f32[1,32,256]{2,1,0:T(8,128)} %get-tuple-element.43), channel_id=1, source_target_pairs={{4,8},{8,4},{5,9},{9,5},{6,10},{10,6},{7,11},{11,7},{20,24},{24,20... | collective-permute-start | bytes 98312 | tf_op jit(solution)/shard_map/ppermute | solution.py:428
  64.5 0.1 collective-permute-start.14
  64.6 1.9 %collective-permute-start.15 = (f32[1,16,32]{2,1,0:T(8,128)}, f32[1,16,32]{2,1,0:T(8,128)S(1)}, u32[]{:S(2)}, u32[]{:S(2)}) collective-permute-start(f32[1,16,32]{2,1,0:T(8,128)} %get-tuple-element.45), channel_id=1, source_target_pairs={{1,2},{2,1},{5,6},{6,5},{9,10},{10,9},{13,14},{14,13},{17,18},{18,... | collective-permute-start | bytes 6152 | tf_op jit(solution)/shard_map/ppermute | solution.py:428
  66.5 0.8 %collective-permute-done.14.hz_lo = f32[1,16,32]{2,1,0:T(8,128)S(1)} collective-permute-done((f32[1,16,32]{2,1,0:T(8,128)}, f32[1,16,32]{2,1,0:T(8,128)S(1)}, u32[]{:S(2)}, u32[]{:S(2)}) %collective-permute-start.14) | collective-permute-done | bytes 2080 | tf_op jit(solution)/shard_map/ppermute | solution.py:427
  67.3 1.9 %collective-permute-done.15.hz_hi = f32[1,16,32]{2,1,0:T(8,128)S(1)} collective-permute-done((f32[1,16,32]{2,1,0:T(8,128)}, f32[1,16,32]{2,1,0:T(8,128)S(1)}, u32[]{:S(2)}, u32[]{:S(2)}) %collective-permute-start.15) | collective-permute-done | bytes 2080 | tf_op jit(solution)/shard_map/ppermute | solution.py:428
  69.2 0.6 copy-done.15
  69.8 0.0 copy-done.10
  69.8 0.0 copy-done.11
  69.8 3.9 %shard_map.65 = f32[32,16,256]{2,1,0:T(8,128)} custom-call(s32[3]{0:T(128)} %pad_add_fusion.ctl_ref.r_0_, s32[32,16,256]{2,1,0:T(8,128)} %pore_ref.7, s32[32,16,256]{2,1,0:T(8,128)} %lab_ref.7, f32[32,16,256]{2,1,0:T(8,128)} %get-tuple-element.41.a2_ref, f32[3,32,256]{2,1,0:T(8,128)} %copy-done, f32[3,32,256]{2,1,0:T(8,128)} %copy-done.1, ...), custom_call_target="tpu_custom_call" | custom-call | tf_op jit(solution)/shard_map/pallas_call | solution.py:513
  (29 shorter events, 0.1 us)
Async XLA Ops:
  2.1 7.5 %collective-permute-start = (f32[2,2,16,256]{3,2,1,0:T(8,128)S(1)}, f32[2,2,16,256]{3,2,1,0:T(8,128)S(1)}, u32[]{:S(2)}, u32[]{:S(2)}) collective-permute-start(f32[2,2,16,256]{3,2,1,0:T(8,128)S(1)} %pad_maximum_fusion), channel_id=1, source_target_pairs={{0,16},{16,0},{1,17},{17,1},{2,18},{18,2},{3,19},{19,3},{4,20},{20... | collective-permute-start | bytes 196616 | tf_op jit(solution)/shard_map/ppermute | solution.py:449
  5.6 16.3 %collective-permute-start.2 = (f32[3,32,256]{2,1,0:T(8,128)}, f32[3,32,256]{2,1,0:T(8,128)S(1)}, u32[]{:S(2)}, u32[]{:S(2)}) collective-permute-start(f32[3,32,256]{2,1,0:T(8,128)} %get-tuple-element.26), channel_id=1, source_target_pairs={{0,4},{4,0},{8,12},{12,8},{1,5},{5,1},{9,13},{13,9},{2,6},{6,2},{1... | collective-permute-start | bytes 294920 | tf_op jit(solution)/shard_map/ppermute | solution.py:427
  6.6 15.4 %collective-permute-start.3 = (f32[3,32,256]{2,1,0:T(8,128)}, f32[3,32,256]{2,1,0:T(8,128)S(1)}, u32[]{:S(2)}, u32[]{:S(2)}) collective-permute-start(f32[3,32,256]{2,1,0:T(8,128)} %get-tuple-element.27), channel_id=1, source_target_pairs={{4,8},{8,4},{5,9},{9,5},{6,10},{10,6},{7,11},{11,7},{20,24},{24,20... | collective-permute-start | bytes 294920 | tf_op jit(solution)/shard_map/ppermute | solution.py:428
  9.6 0.6 copy-start.9
  14.7 17.6 %collective-permute-start.1 = (f32[2,5,16,256]{3,2,1,0:T(8,128)}, f32[2,5,16,256]{3,2,1,0:T(8,128)S(1)}, u32[]{:S(2)}, u32[]{:S(2)}) collective-permute-start(f32[2,5,16,256]{3,2,1,0:T(8,128)} %get-tuple-element.24.r_1_), channel_id=1, source_target_pairs={{0,16},{16,0},{1,17},{17,1},{2,18},{18,2},{3,19},{19,3},{4,20},{20... | collective-permute-start | bytes 491528 | tf_op jit(solution)/shard_map/ppermute | solution.py:410
  15.9 3.2 %collective-permute-start.4 = (f32[3,16,32]{2,1,0:T(8,128)}, f32[3,16,32]{2,1,0:T(8,128)S(1)}, u32[]{:S(2)}, u32[]{:S(2)}) collective-permute-start(f32[3,16,32]{2,1,0:T(8,128)} %get-tuple-element.28), channel_id=1, source_target_pairs={{0,1},{1,0},{2,3},{3,2},{4,5},{5,4},{6,7},{7,6},{8,9},{9,8},{10,11... | collective-permute-start | bytes 18440 | tf_op jit(solution)/shard_map/ppermute | solution.py:427
  17.2 4.8 %collective-permute-start.5 = (f32[3,16,32]{2,1,0:T(8,128)}, f32[3,16,32]{2,1,0:T(8,128)S(1)}, u32[]{:S(2)}, u32[]{:S(2)}) collective-permute-start(f32[3,16,32]{2,1,0:T(8,128)} %get-tuple-element.29), channel_id=1, source_target_pairs={{1,2},{2,1},{5,6},{6,5},{9,10},{10,9},{13,14},{14,13},{17,18},{18,... | collective-permute-start | bytes 18440 | tf_op jit(solution)/shard_map/ppermute | solution.py:428
  19.1 2.9 %copy-start.3 = (f32[3,16,32]{2,1,0:T(8,128)}, f32[3,16,32]{2,1,0:T(8,128)S(1)}, u32[]{:S(2)}) copy-start(f32[3,16,32]{2,1,0:T(8,128)S(1)} %collective-permute-done.4.gz_lo) | copy-start | bytes 18436
  22.0 0.6 copy-start.4
  22.0 0.6 copy-start
  22.0 0.7 copy-start.1
  28.3 3.9 %collective-permute-start.6 = (f32[2,2,16,256]{3,2,1,0:T(8,128)}, f32[2,2,16,256]{3,2,1,0:T(8,128)S(1)}, u32[]{:S(2)}, u32[]{:S(2)}) collective-permute-start(f32[2,2,16,256]{3,2,1,0:T(8,128)} %get-tuple-element.30.r_3_), channel_id=1, source_target_pairs={{0,16},{16,0},{1,17},{17,1},{2,18},{18,2},{3,19},{19,3},{4,20},{20... | collective-permute-start | bytes 196616 | tf_op jit(solution)/shard_map/ppermute | solution.py:410
  32.3 0.6 copy-start.7
  32.3 0.7 copy-start.2
  36.5 9.6 %collective-permute-start.7 = (f32[2,32,256]{2,1,0:T(8,128)}, f32[2,32,256]{2,1,0:T(8,128)S(1)}, u32[]{:S(2)}, u32[]{:S(2)}) collective-permute-start(f32[2,32,256]{2,1,0:T(8,128)} %get-tuple-element.34), channel_id=1, source_target_pairs={{0,4},{4,0},{8,12},{12,8},{1,5},{5,1},{9,13},{13,9},{2,6},{6,2},{1... | collective-permute-start | bytes 196616 | tf_op jit(solution)/shard_map/ppermute | solution.py:427
  36.9 9.2 %collective-permute-start.8 = (f32[2,32,256]{2,1,0:T(8,128)}, f32[2,32,256]{2,1,0:T(8,128)S(1)}, u32[]{:S(2)}, u32[]{:S(2)}) collective-permute-start(f32[2,32,256]{2,1,0:T(8,128)} %get-tuple-element.35), channel_id=1, source_target_pairs={{4,8},{8,4},{5,9},{9,5},{6,10},{10,6},{7,11},{11,7},{20,24},{24,20... | collective-permute-start | bytes 196616 | tf_op jit(solution)/shard_map/ppermute | solution.py:428
  41.3 2.9 %collective-permute-start.9 = (f32[2,16,32]{2,1,0:T(8,128)}, f32[2,16,32]{2,1,0:T(8,128)S(1)}, u32[]{:S(2)}, u32[]{:S(2)}) collective-permute-start(f32[2,16,32]{2,1,0:T(8,128)} %get-tuple-element.36), channel_id=1, source_target_pairs={{0,1},{1,0},{2,3},{3,2},{4,5},{5,4},{6,7},{7,6},{8,9},{9,8},{10,11... | collective-permute-start | bytes 12296 | tf_op jit(solution)/shard_map/ppermute | solution.py:427
  41.4 4.7 %collective-permute-start.10 = (f32[2,16,32]{2,1,0:T(8,128)}, f32[2,16,32]{2,1,0:T(8,128)S(1)}, u32[]{:S(2)}, u32[]{:S(2)}) collective-permute-start(f32[2,16,32]{2,1,0:T(8,128)} %get-tuple-element.37), channel_id=1, source_target_pairs={{1,2},{2,1},{5,6},{6,5},{9,10},{10,9},{13,14},{14,13},{17,18},{18,... | collective-permute-start | bytes 12296 | tf_op jit(solution)/shard_map/ppermute | solution.py:428
  44.2 1.9 %copy-start.12 = (f32[2,16,32]{2,1,0:T(8,128)}, f32[2,16,32]{2,1,0:T(8,128)S(1)}, u32[]{:S(2)}) copy-start(f32[2,16,32]{2,1,0:T(8,128)S(1)} %collective-permute-done.9.hz_lo) | copy-start | bytes 12292
  46.1 0.6 copy-start.13
  46.1 0.6 copy-start.5
  46.1 0.6 copy-start.6
  52.8 3.3 %collective-permute-start.11 = (f32[2,2,16,256]{3,2,1,0:T(8,128)}, f32[2,2,16,256]{3,2,1,0:T(8,128)S(1)}, u32[]{:S(2)}, u32[]{:S(2)}) collective-permute-start(f32[2,2,16,256]{3,2,1,0:T(8,128)} %get-tuple-element.38.r_3_), channel_id=1, source_target_pairs={{0,16},{16,0},{1,17},{17,1},{2,18},{18,2},{3,19},{19,3},{4,20},{20... | collective-permute-start | bytes 196616 | tf_op jit(solution)/shard_map/ppermute | solution.py:410
  56.2 0.6 copy-start.8
  60.3 8.9 %collective-permute-start.12 = (f32[1,32,256]{2,1,0:T(8,128)}, f32[1,32,256]{2,1,0:T(8,128)S(1)}, u32[]{:S(2)}, u32[]{:S(2)}) collective-permute-start(f32[1,32,256]{2,1,0:T(8,128)} %get-tuple-element.42), channel_id=1, source_target_pairs={{0,4},{4,0},{8,12},{12,8},{1,5},{5,1},{9,13},{13,9},{2,6},{6,2},{1... | collective-permute-start | bytes 98312 | tf_op jit(solution)/shard_map/ppermute | solution.py:427
  60.3 8.9 %collective-permute-start.13 = (f32[1,32,256]{2,1,0:T(8,128)}, f32[1,32,256]{2,1,0:T(8,128)S(1)}, u32[]{:S(2)}, u32[]{:S(2)}) collective-permute-start(f32[1,32,256]{2,1,0:T(8,128)} %get-tuple-element.43), channel_id=1, source_target_pairs={{4,8},{8,4},{5,9},{9,5},{6,10},{10,6},{7,11},{11,7},{20,24},{24,20... | collective-permute-start | bytes 98312 | tf_op jit(solution)/shard_map/ppermute | solution.py:428
  64.5 2.8 %collective-permute-start.14 = (f32[1,16,32]{2,1,0:T(8,128)}, f32[1,16,32]{2,1,0:T(8,128)S(1)}, u32[]{:S(2)}, u32[]{:S(2)}) collective-permute-start(f32[1,16,32]{2,1,0:T(8,128)} %get-tuple-element.44), channel_id=1, source_target_pairs={{0,1},{1,0},{2,3},{3,2},{4,5},{5,4},{6,7},{7,6},{8,9},{9,8},{10,11... | collective-permute-start | bytes 6152 | tf_op jit(solution)/shard_map/ppermute | solution.py:427
  64.6 4.6 %collective-permute-start.15 = (f32[1,16,32]{2,1,0:T(8,128)}, f32[1,16,32]{2,1,0:T(8,128)S(1)}, u32[]{:S(2)}, u32[]{:S(2)}) collective-permute-start(f32[1,16,32]{2,1,0:T(8,128)} %get-tuple-element.45), channel_id=1, source_target_pairs={{1,2},{2,1},{5,6},{6,5},{9,10},{10,9},{13,14},{14,13},{17,18},{18,... | collective-permute-start | bytes 6152 | tf_op jit(solution)/shard_map/ppermute | solution.py:428
  67.3 1.9 %copy-start.14 = (f32[1,16,32]{2,1,0:T(8,128)}, f32[1,16,32]{2,1,0:T(8,128)S(1)}, u32[]{:S(2)}) copy-start(f32[1,16,32]{2,1,0:T(8,128)S(1)} %collective-permute-done.14.hz_lo) | copy-start | bytes 6148
  69.2 0.6 copy-start.15
  69.2 0.6 copy-start.10
  69.2 0.6 copy-start.11

commit v6 on v2

--- a/solution.py
+++ b/solution.py
@@ -134,7 +134,7 @@
     return mob, lab, mob_n, _faces(mob, lab, mob_n, lab_n)
 
 
-def _sweep(m, lower, pivots, ratios, source):
+def _sweep(m, lower, inv_pivots, ratios, source):
     ys = [None] * m
     prev = None
     for r in range(m - 1):
@@ -145,7 +145,7 @@
             num = -(lower[r] * prev)
         elif prev is not None:
             num = num - lower[r] * prev
-        ys[r] = num / pivots[r]
+        ys[r] = num * inv_pivots[r]
         prev = ys[r]
     xs = [None] * m
     prev = None
@@ -192,14 +192,15 @@
             pivots.append(piv)
             ratios.append(rat)
             prev = rat
+        inv_piv = [1.0 / x for x in pivots]
         left_src = [lower[0]] + [None] * (m - 1)
         right_src = [None] * (m - 2) + [upper[m - 2], None]
-        left = _sweep(m, lower, pivots, ratios, left_src)
-        right = _sweep(m, lower, pivots, ratios, right_src)
+        left = _sweep(m, lower, inv_piv, ratios, left_src)
+        right = _sweep(m, lower, inv_piv, ratios, right_src)
         for r in range(m):
             fac_ref[c, 0, r] = lower[r]
             fac_ref[c, 1, r] = ratios[r] if r < m - 1 else zero
-            fac_ref[c, 2, r] = pivots[r] if r < m - 1 else zero + 1.0
+            fac_ref[c, 2, r] = inv_piv[r] if r < m - 1 else zero + 1.0
             lr_ref[c, 0, r] = left[r] if r < m - 1 else zero
             lr_ref[c, 1, r] = right[r] if r < m - 1 else zero - 1.0
         last_lower = lower[m - 1]
@@ -429,7 +430,9 @@
 
 
 def _yz_halos(y_a, y_b, z_a, z_b):
-    return _swap(y_a, y_b, "gy") + _swap(z_a, z_b, "gz")
+    z_pair = _swap(z_a, z_b, "gz")
+    y_pair = _swap(y_a, y_b, "gy")
+    return y_pair + z_pair
 
 
 def _shards(vacancy, grain_label, pore_mask, cotangent):

time: 74.6 us -> 74.6 us (level)
  no operation moved by 1% of the time
where the time goes in v6:
time: 74.6 us; the launch traced here: 74.3 us
  Pallas kernels  29.8 us (40%)
  starting transfers between devices  25.5 us (34%)
  waiting for transfers between devices  13.7 us (18%)
  local copies, waits for them, and re-layouts  3.82 us (5%)
  between operations  0.83 us (1%)
    ppermute x6, starting transfers between devices, _swap(): lax.ppermute(x_b, axis, pairs_b)  16.6 us
    ppermute x6, waiting for transfers between devices, _swap(): lax.ppermute(x_b, axis, pairs_b)  6.46 us
    pallas_call x1, Pallas kernels, _shards(): pl.pallas_call(_second_kernel, out_shape=(jax.ShapeDtypeStruct((2, m, ny,...  6.1 us
    ppermute x6, starting transfers between devices, _swap(): recv_a = lax.ppermute(x_a, axis, pairs_a)  6.03 us
    pallas_call x1, Pallas kernels, _shards(): _first_call(m, ny, nz)  5.69 us
    ppermute x3, waiting for transfers between devices, _gather_blk(): parts.append(lax.ppermute(x, 'blk', [(j, (j + k) % n) for j in range(n)]))  5.3 us
    pallas_call x1, Pallas kernels, _shards(): pl.pallas_call(lambda *r: _factor_kernel(cycle_step, lo_i, hi_i, *r), out...  4.45 us
    pallas_call x1, Pallas kernels, _shards(): pl.pallas_call(_gradient_kernel, out_shape=shape, in_specs=[_smem()] + [_...  3.95 us
  transfers between devices with their start and end apart: 16, of which 7 were waited for; matrix products, arithmetic and copies ran while one was open for 0% of the time, Pallas kernels for 14%

profile of v6, /device:TPU:17, one launch (start us, length us, event | category | flops | bytes accessed | tf_op | source)
XLA Modules:
  0.0 74.3 jit_solution(17964540890256752510)
XLA Ops:
  0.6 0.6 pad_add_fusion.ctl_ref.r_0_
  1.3 2.6 %shard_map.59 = (f32[3,32,256]{2,1,0:T(8,128)}, f32[3,32,256]{2,1,0:T(8,128)}, f32[3,16,32]{2,1,0:T(8,128)}, f32[3,16,32]{2,1,0:T(8,128)}, f32[2,2,16,256]{3,2,1,0:T(8,128)}) custom-call(s32[3]{0:T(128)} %pad_add_fusion.ctl_ref.r_0_, f32[32,16,256]{2,1,0:T(8,128)} %vac_ref.3, s32[32,16,256]{2,1,0:T(8,128)} %pore_ref.7, s32[32,16,256]{2,1,0:T(8,128)} %lab_ref.7), custom_call_target="tpu_custom_call" | custom-call | tf_op jit(solution)/shard_map/pallas_call | solution.py:447
  3.9 1.2 %collective-permute-start = (f32[2,2,16,256]{3,2,1,0:T(8,128)}, f32[2,2,16,256]{3,2,1,0:T(8,128)S(1)}, u32[]{:S(2)}, u32[]{:S(2)}) collective-permute-start(f32[2,2,16,256]{3,2,1,0:T(8,128)} %get-tuple-element.25), channel_id=1, source_target_pairs={{0,16},{16,0},{1,17},{17,1},{2,18},{18,2},{3,19},{19,3},{4,20},{20... | collective-permute-start | bytes 196616 | tf_op jit(solution)/shard_map/ppermute | solution.py:455
  5.1 0.9 %collective-permute-start.2 = (f32[3,32,256]{2,1,0:T(8,128)}, f32[3,32,256]{2,1,0:T(8,128)S(1)}, u32[]{:S(2)}, u32[]{:S(2)}) collective-permute-start(f32[3,32,256]{2,1,0:T(8,128)} %get-tuple-element.28), channel_id=1, source_target_pairs={{0,4},{4,0},{8,12},{12,8},{1,5},{5,1},{9,13},{13,9},{2,6},{6,2},{1... | collective-permute-start | bytes 294920 | tf_op jit(solution)/shard_map/ppermute | solution.py:427
  6.0 3.0 %collective-permute-start.3 = (f32[3,32,256]{2,1,0:T(8,128)}, f32[3,32,256]{2,1,0:T(8,128)S(1)}, u32[]{:S(2)}, u32[]{:S(2)}) collective-permute-start(f32[3,32,256]{2,1,0:T(8,128)} %get-tuple-element.29), channel_id=1, source_target_pairs={{4,8},{8,4},{5,9},{9,5},{6,10},{10,6},{7,11},{11,7},{20,24},{24,20... | collective-permute-start | bytes 294920 | tf_op jit(solution)/shard_map/ppermute | solution.py:428
  9.1 0.0 collective-permute-done.r_2_
  9.1 0.6 copy-done.9
  9.7 4.4 %shard_map.60 = (f32[2,3,32,16,256]{4,3,2,1,0:T(8,128)}, f32[2,2,32,16,256]{4,3,2,1,0:T(8,128)}, f32[2,5,16,256]{3,2,1,0:T(8,128)}) custom-call(s32[32,16,256]{2,1,0:T(8,128)} %pore_ref.7, s32[32,16,256]{2,1,0:T(8,128)} %lab_ref.7, f32[2,2,16,256]{3,2,1,0:T(8,128)} %copy-done.9), custom_call_target="tpu_custom_call" | custom-call | tf_op jit(solution)/shard_map/pallas_call | solution.py:463
  14.1 0.3 collective-permute-start.1
  14.4 1.3 %collective-permute-start.4 = (f32[3,16,32]{2,1,0:T(8,128)}, f32[3,16,32]{2,1,0:T(8,128)S(1)}, u32[]{:S(2)}, u32[]{:S(2)}) collective-permute-start(f32[3,16,32]{2,1,0:T(8,128)} %get-tuple-element.30), channel_id=1, source_target_pairs={{0,1},{1,0},{2,3},{3,2},{4,5},{5,4},{6,7},{7,6},{8,9},{9,8},{10,11... | collective-permute-start | bytes 18440 | tf_op jit(solution)/shard_map/ppermute | solution.py:427
  15.7 1.9 %collective-permute-start.5 = (f32[3,16,32]{2,1,0:T(8,128)}, f32[3,16,32]{2,1,0:T(8,128)S(1)}, u32[]{:S(2)}, u32[]{:S(2)}) collective-permute-start(f32[3,16,32]{2,1,0:T(8,128)} %get-tuple-element.31), channel_id=1, source_target_pairs={{1,2},{2,1},{5,6},{6,5},{9,10},{10,9},{13,14},{14,13},{17,18},{18,... | collective-permute-start | bytes 18440 | tf_op jit(solution)/shard_map/ppermute | solution.py:428
  17.6 0.0 collective-permute-done.4.gz_lo
  17.6 2.9 %collective-permute-done.5.gz_hi = f32[3,16,32]{2,1,0:T(8,128)S(1)} collective-permute-done((f32[3,16,32]{2,1,0:T(8,128)}, f32[3,16,32]{2,1,0:T(8,128)S(1)}, u32[]{:S(2)}, u32[]{:S(2)}) %collective-permute-start.5) | collective-permute-done | bytes 6176 | tf_op jit(solution)/shard_map/ppermute | solution.py:428
  20.6 0.0 collective-permute-done.2.gy_lo
  20.6 0.0 collective-permute-done.3.gy_hi
  20.6 0.6 copy-done.4
  21.2 0.1 copy-done
  21.2 0.0 copy-done.1
  21.2 5.7 %shard_map.61 = (f32[2,32,16,256]{3,2,1,0:T(8,128)}, f32[2,2,16,256]{3,2,1,0:T(8,128)}) custom-call(s32[3]{0:T(128)} %pad_add_fusion.ctl_ref.r_0_, f32[32,16,256]{2,1,0:T(8,128)} %vac_ref.3, f32[32,16,256]{2,1,0:T(8,128)} %cot_ref.1, s32[32,16,256]{2,1,0:T(8,128)} %pore_ref.7, s32[32,16,256]{2,1,0:T(8,128)} %lab_ref.7, ...), custom_call_target="tpu_custom_call" | custom-call | tf_op jit(solution)/shard_map/pallas_call | solution.py:475
  26.9 1.1 %collective-permute-start.6 = (f32[2,2,16,256]{3,2,1,0:T(8,128)}, f32[2,2,16,256]{3,2,1,0:T(8,128)S(1)}, u32[]{:S(2)}, u32[]{:S(2)}) collective-permute-start(f32[2,2,16,256]{3,2,1,0:T(8,128)} %get-tuple-element.32.r_3_), channel_id=1, source_target_pairs={{0,16},{16,0},{1,17},{17,1},{2,18},{18,2},{3,19},{19,3},{4,20},{20... | collective-permute-start | bytes 196616 | tf_op jit(solution)/shard_map/ppermute | solution.py:410
  28.0 2.2 %collective-permute-done.6.r_4_ = f32[2,2,16,256]{3,2,1,0:T(8,128)S(1)} collective-permute-done((f32[2,2,16,256]{3,2,1,0:T(8,128)}, f32[2,2,16,256]{3,2,1,0:T(8,128)S(1)}, u32[]{:S(2)}, u32[]{:S(2)}) %collective-permute-start.6) | collective-permute-done | bytes 65568 | tf_op jit(solution)/shard_map/ppermute | solution.py:410
  30.3 0.0 collective-permute-done.1.r_2_
  30.3 0.6 copy-done.7
  30.9 0.1 copy-done.2
  31.0 3.5 %shard_map.62 = (f32[2,32,16,256]{3,2,1,0:T(8,128)}, f32[2,32,256]{2,1,0:T(8,128)}, f32[2,32,256]{2,1,0:T(8,128)}, f32[2,16,32]{2,1,0:T(8,128)}, f32[2,16,32]{2,1,0:T(8,128)}) custom-call(s32[3]{0:T(128)} %pad_add_fusion.ctl_ref.r_0_, f32[2,5,16,256]{3,2,1,0:T(8,128)} %get-tuple-element.26.r_1_, f32[2,5,16,256]{3,2,1,0:T(8,128)} %copy-done.2, ...), custom_call_target="tpu_custom_call" | custom-call | tf_op jit(solution)/shard_map/pallas_call | solution.py:481
  34.5 3.6 %collective-permute-start.7 = (f32[2,32,256]{2,1,0:T(8,128)}, f32[2,32,256]{2,1,0:T(8,128)S(1)}, u32[]{:S(2)}, u32[]{:S(2)}) collective-permute-start(f32[2,32,256]{2,1,0:T(8,128)} %get-tuple-element.36), channel_id=1, source_target_pairs={{0,4},{4,0},{8,12},{12,8},{1,5},{5,1},{9,13},{13,9},{2,6},{6,2},{1... | collective-permute-start | bytes 196616 | tf_op jit(solution)/shard_map/ppermute | solution.py:427
  38.1 3.0 %collective-permute-start.8 = (f32[2,32,256]{2,1,0:T(8,128)}, f32[2,32,256]{2,1,0:T(8,128)S(1)}, u32[]{:S(2)}, u32[]{:S(2)}) collective-permute-start(f32[2,32,256]{2,1,0:T(8,128)} %get-tuple-element.37), channel_id=1, source_target_pairs={{4,8},{8,4},{5,9},{9,5},{6,10},{10,6},{7,11},{11,7},{20,24},{24,20... | collective-permute-start | bytes 196616 | tf_op jit(solution)/shard_map/ppermute | solution.py:428
  41.2 0.1 collective-permute-start.9
  41.3 1.9 %collective-permute-start.10 = (f32[2,16,32]{2,1,0:T(8,128)}, f32[2,16,32]{2,1,0:T(8,128)S(1)}, u32[]{:S(2)}, u32[]{:S(2)}) collective-permute-start(f32[2,16,32]{2,1,0:T(8,128)} %get-tuple-element.39), channel_id=1, source_target_pairs={{1,2},{2,1},{5,6},{6,5},{9,10},{10,9},{13,14},{14,13},{17,18},{18,... | collective-permute-start | bytes 12296 | tf_op jit(solution)/shard_map/ppermute | solution.py:428
  43.2 1.2 %collective-permute-done.9.hz_lo = f32[2,16,32]{2,1,0:T(8,128)S(1)} collective-permute-done((f32[2,16,32]{2,1,0:T(8,128)}, f32[2,16,32]{2,1,0:T(8,128)S(1)}, u32[]{:S(2)}, u32[]{:S(2)}) %collective-permute-start.9) | collective-permute-done | bytes 4128 | tf_op jit(solution)/shard_map/ppermute | solution.py:427
  44.4 1.6 %collective-permute-done.10.hz_hi = f32[2,16,32]{2,1,0:T(8,128)S(1)} collective-permute-done((f32[2,16,32]{2,1,0:T(8,128)}, f32[2,16,32]{2,1,0:T(8,128)S(1)}, u32[]{:S(2)}, u32[]{:S(2)}) %collective-permute-start.10) | collective-permute-done | bytes 4128 | tf_op jit(solution)/shard_map/ppermute | solution.py:428
  46.0 0.6 copy-done.13
  46.6 0.0 copy-done.5
  46.6 0.0 copy-done.6
  46.6 6.1 %shard_map.63 = (f32[2,32,16,256]{3,2,1,0:T(8,128)}, f32[2,2,16,256]{3,2,1,0:T(8,128)}) custom-call(s32[3]{0:T(128)} %pad_add_fusion.ctl_ref.r_0_, s32[32,16,256]{2,1,0:T(8,128)} %pore_ref.7, s32[32,16,256]{2,1,0:T(8,128)} %lab_ref.7, f32[2,32,16,256]{3,2,1,0:T(8,128)} %get-tuple-element.35.fa_ref, f32[2,3,32,16,256]{4,3,2,1,0:T(8,128)} %get-tuple-element.27.fac_ref, ...), custom_call_target="tpu_custom_call" | custom-call | tf_op jit(solution)/shard_map/pallas_call | solution.py:491
  52.7 0.3 collective-permute-start.11
  53.0 3.1 %collective-permute-done.11.r_4_ = f32[2,2,16,256]{3,2,1,0:T(8,128)S(1)} collective-permute-done((f32[2,2,16,256]{3,2,1,0:T(8,128)}, f32[2,2,16,256]{3,2,1,0:T(8,128)S(1)}, u32[]{:S(2)}, u32[]{:S(2)}) %collective-permute-start.11) | collective-permute-done | bytes 65568 | tf_op jit(solution)/shard_map/ppermute | solution.py:410
  56.1 0.6 copy-done.8
  56.7 3.5 %shard_map.64 = (f32[32,16,256]{2,1,0:T(8,128)}, f32[32,16,256]{2,1,0:T(8,128)}, f32[1,32,256]{2,1,0:T(8,128)}, f32[1,32,256]{2,1,0:T(8,128)}, f32[1,16,32]{2,1,0:T(8,128)}, /*index=5*/f32[1,16,32]{2,1,0:T(8,128)}) custom-call(s32[3]{0:T(128)} %pad_add_fusion.ctl_ref.r_0_, f32[2,5,16,256]{3,2,1,0:T(8,128)} %get-tuple-element.26.r_1_, ...), custom_call_target="tpu_custom_call" | custom-call | tf_op jit(solution)/shard_map/pallas_call | solution.py:502
  60.2 4.8 %collective-permute-start.13 = (f32[1,32,256]{2,1,0:T(8,128)}, f32[1,32,256]{2,1,0:T(8,128)S(1)}, u32[]{:S(2)}, u32[]{:S(2)}) collective-permute-start(f32[1,32,256]{2,1,0:T(8,128)} %get-tuple-element.45), channel_id=1, source_target_pairs={{4,8},{8,4},{5,9},{9,5},{6,10},{10,6},{7,11},{11,7},{20,24},{24,20... | collective-permute-start | bytes 98312 | tf_op jit(solution)/shard_map/ppermute | solution.py:428
  65.0 0.1 collective-permute-start.14
  65.1 1.9 %collective-permute-start.15 = (f32[1,16,32]{2,1,0:T(8,128)}, f32[1,16,32]{2,1,0:T(8,128)S(1)}, u32[]{:S(2)}, u32[]{:S(2)}) collective-permute-start(f32[1,16,32]{2,1,0:T(8,128)} %get-tuple-element.47), channel_id=1, source_target_pairs={{1,2},{2,1},{5,6},{6,5},{9,10},{10,9},{13,14},{14,13},{17,18},{18,... | collective-permute-start | bytes 6152 | tf_op jit(solution)/shard_map/ppermute | solution.py:428
  67.0 0.8 %collective-permute-done.14.hz_lo = f32[1,16,32]{2,1,0:T(8,128)S(1)} collective-permute-done((f32[1,16,32]{2,1,0:T(8,128)}, f32[1,16,32]{2,1,0:T(8,128)S(1)}, u32[]{:S(2)}, u32[]{:S(2)}) %collective-permute-start.14) | collective-permute-done | bytes 2080 | tf_op jit(solution)/shard_map/ppermute | solution.py:427
  67.8 1.9 %collective-permute-done.15.hz_hi = f32[1,16,32]{2,1,0:T(8,128)S(1)} collective-permute-done((f32[1,16,32]{2,1,0:T(8,128)}, f32[1,16,32]{2,1,0:T(8,128)S(1)}, u32[]{:S(2)}, u32[]{:S(2)}) %collective-permute-start.15) | collective-permute-done | bytes 2080 | tf_op jit(solution)/shard_map/ppermute | solution.py:428
  69.7 0.6 copy-done.15
  70.3 0.0 copy-done.10
  70.3 0.0 copy-done.11
  70.3 3.9 %shard_map.65 = f32[32,16,256]{2,1,0:T(8,128)} custom-call(s32[3]{0:T(128)} %pad_add_fusion.ctl_ref.r_0_, s32[32,16,256]{2,1,0:T(8,128)} %pore_ref.7, s32[32,16,256]{2,1,0:T(8,128)} %lab_ref.7, f32[32,16,256]{2,1,0:T(8,128)} %get-tuple-element.43.a2_ref, f32[3,32,256]{2,1,0:T(8,128)} %copy-done, f32[3,32,256]{2,1,0:T(8,128)} %copy-done.1, ...), custom_call_target="tpu_custom_call" | custom-call | tf_op jit(solution)/shard_map/pallas_call | solution.py:512
  (24 shorter events, 0.0 us)
Async XLA Ops:
  3.9 5.2 %collective-permute-start = (f32[2,2,16,256]{3,2,1,0:T(8,128)}, f32[2,2,16,256]{3,2,1,0:T(8,128)S(1)}, u32[]{:S(2)}, u32[]{:S(2)}) collective-permute-start(f32[2,2,16,256]{3,2,1,0:T(8,128)} %get-tuple-element.25), channel_id=1, source_target_pairs={{0,16},{16,0},{1,17},{17,1},{2,18},{18,2},{3,19},{19,3},{4,20},{20... | collective-permute-start | bytes 196616 | tf_op jit(solution)/shard_map/ppermute | solution.py:455
  5.1 15.5 %collective-permute-start.2 = (f32[3,32,256]{2,1,0:T(8,128)}, f32[3,32,256]{2,1,0:T(8,128)S(1)}, u32[]{:S(2)}, u32[]{:S(2)}) collective-permute-start(f32[3,32,256]{2,1,0:T(8,128)} %get-tuple-element.28), channel_id=1, source_target_pairs={{0,4},{4,0},{8,12},{12,8},{1,5},{5,1},{9,13},{13,9},{2,6},{6,2},{1... | collective-permute-start | bytes 294920 | tf_op jit(solution)/shard_map/ppermute | solution.py:427
  6.0 14.5 %collective-permute-start.3 = (f32[3,32,256]{2,1,0:T(8,128)}, f32[3,32,256]{2,1,0:T(8,128)S(1)}, u32[]{:S(2)}, u32[]{:S(2)}) collective-permute-start(f32[3,32,256]{2,1,0:T(8,128)} %get-tuple-element.29), channel_id=1, source_target_pairs={{4,8},{8,4},{5,9},{9,5},{6,10},{10,6},{7,11},{11,7},{20,24},{24,20... | collective-permute-start | bytes 294920 | tf_op jit(solution)/shard_map/ppermute | solution.py:428
  9.1 0.6 copy-start.9
  14.1 16.1 %collective-permute-start.1 = (f32[2,5,16,256]{3,2,1,0:T(8,128)}, f32[2,5,16,256]{3,2,1,0:T(8,128)S(1)}, u32[]{:S(2)}, u32[]{:S(2)}) collective-permute-start(f32[2,5,16,256]{3,2,1,0:T(8,128)} %get-tuple-element.26.r_1_), channel_id=1, source_target_pairs={{0,16},{16,0},{1,17},{17,1},{2,18},{18,2},{3,19},{19,3},{4,20},{20... | collective-permute-start | bytes 491528 | tf_op jit(solution)/shard_map/ppermute | solution.py:410
  14.4 3.2 %collective-permute-start.4 = (f32[3,16,32]{2,1,0:T(8,128)}, f32[3,16,32]{2,1,0:T(8,128)S(1)}, u32[]{:S(2)}, u32[]{:S(2)}) collective-permute-start(f32[3,16,32]{2,1,0:T(8,128)} %get-tuple-element.30), channel_id=1, source_target_pairs={{0,1},{1,0},{2,3},{3,2},{4,5},{5,4},{6,7},{7,6},{8,9},{9,8},{10,11... | collective-permute-start | bytes 18440 | tf_op jit(solution)/shard_map/ppermute | solution.py:427
  15.7 4.9 %collective-permute-start.5 = (f32[3,16,32]{2,1,0:T(8,128)}, f32[3,16,32]{2,1,0:T(8,128)S(1)}, u32[]{:S(2)}, u32[]{:S(2)}) collective-permute-start(f32[3,16,32]{2,1,0:T(8,128)} %get-tuple-element.31), channel_id=1, source_target_pairs={{1,2},{2,1},{5,6},{6,5},{9,10},{10,9},{13,14},{14,13},{17,18},{18,... | collective-permute-start | bytes 18440 | tf_op jit(solution)/shard_map/ppermute | solution.py:428
  17.6 3.0 %copy-start.3 = (f32[3,16,32]{2,1,0:T(8,128)}, f32[3,16,32]{2,1,0:T(8,128)S(1)}, u32[]{:S(2)}) copy-start(f32[3,16,32]{2,1,0:T(8,128)S(1)} %collective-permute-done.4.gz_lo) | copy-start | bytes 18436
  20.6 0.6 copy-start.4
  20.6 0.6 copy-start
  20.6 0.7 copy-start.1
  26.9 3.3 %collective-permute-start.6 = (f32[2,2,16,256]{3,2,1,0:T(8,128)}, f32[2,2,16,256]{3,2,1,0:T(8,128)S(1)}, u32[]{:S(2)}, u32[]{:S(2)}) collective-permute-start(f32[2,2,16,256]{3,2,1,0:T(8,128)} %get-tuple-element.32.r_3_), channel_id=1, source_target_pairs={{0,16},{16,0},{1,17},{17,1},{2,18},{18,2},{3,19},{19,3},{4,20},{20... | collective-permute-start | bytes 196616 | tf_op jit(solution)/shard_map/ppermute | solution.py:410
  30.3 0.6 copy-start.7
  30.3 0.7 copy-start.2
  34.5 11.5 %collective-permute-start.7 = (f32[2,32,256]{2,1,0:T(8,128)}, f32[2,32,256]{2,1,0:T(8,128)S(1)}, u32[]{:S(2)}, u32[]{:S(2)}) collective-permute-start(f32[2,32,256]{2,1,0:T(8,128)} %get-tuple-element.36), channel_id=1, source_target_pairs={{0,4},{4,0},{8,12},{12,8},{1,5},{5,1},{9,13},{13,9},{2,6},{6,2},{1... | collective-permute-start | bytes 196616 | tf_op jit(solution)/shard_map/ppermute | solution.py:427
  38.1 7.8 %collective-permute-start.8 = (f32[2,32,256]{2,1,0:T(8,128)}, f32[2,32,256]{2,1,0:T(8,128)S(1)}, u32[]{:S(2)}, u32[]{:S(2)}) collective-permute-start(f32[2,32,256]{2,1,0:T(8,128)} %get-tuple-element.37), channel_id=1, source_target_pairs={{4,8},{8,4},{5,9},{9,5},{6,10},{10,6},{7,11},{11,7},{20,24},{24,20... | collective-permute-start | bytes 196616 | tf_op jit(solution)/shard_map/ppermute | solution.py:428
  41.2 3.2 %collective-permute-start.9 = (f32[2,16,32]{2,1,0:T(8,128)}, f32[2,16,32]{2,1,0:T(8,128)S(1)}, u32[]{:S(2)}, u32[]{:S(2)}) collective-permute-start(f32[2,16,32]{2,1,0:T(8,128)} %get-tuple-element.38), channel_id=1, source_target_pairs={{0,1},{1,0},{2,3},{3,2},{4,5},{5,4},{6,7},{7,6},{8,9},{9,8},{10,11... | collective-permute-start | bytes 12296 | tf_op jit(solution)/shard_map/ppermute | solution.py:427
  41.3 4.7 %collective-permute-start.10 = (f32[2,16,32]{2,1,0:T(8,128)}, f32[2,16,32]{2,1,0:T(8,128)S(1)}, u32[]{:S(2)}, u32[]{:S(2)}) collective-permute-start(f32[2,16,32]{2,1,0:T(8,128)} %get-tuple-element.39), channel_id=1, source_target_pairs={{1,2},{2,1},{5,6},{6,5},{9,10},{10,9},{13,14},{14,13},{17,18},{18,... | collective-permute-start | bytes 12296 | tf_op jit(solution)/shard_map/ppermute | solution.py:428
  44.3 1.6 %copy-start.12 = (f32[2,16,32]{2,1,0:T(8,128)}, f32[2,16,32]{2,1,0:T(8,128)S(1)}, u32[]{:S(2)}) copy-start(f32[2,16,32]{2,1,0:T(8,128)S(1)} %collective-permute-done.9.hz_lo) | copy-start | bytes 12292
  46.0 0.6 copy-start.13
  46.0 0.6 copy-start.5
  46.0 0.6 copy-start.6
  52.7 3.3 %collective-permute-start.11 = (f32[2,2,16,256]{3,2,1,0:T(8,128)}, f32[2,2,16,256]{3,2,1,0:T(8,128)S(1)}, u32[]{:S(2)}, u32[]{:S(2)}) collective-permute-start(f32[2,2,16,256]{3,2,1,0:T(8,128)} %get-tuple-element.40.r_3_), channel_id=1, source_target_pairs={{0,16},{16,0},{1,17},{17,1},{2,18},{18,2},{3,19},{19,3},{4,20},{20... | collective-permute-start | bytes 196616 | tf_op jit(solution)/shard_map/ppermute | solution.py:410
  56.1 0.6 copy-start.8
  60.2 9.5 %collective-permute-start.12 = (f32[1,32,256]{2,1,0:T(8,128)}, f32[1,32,256]{2,1,0:T(8,128)S(1)}, u32[]{:S(2)}, u32[]{:S(2)}) collective-permute-start(f32[1,32,256]{2,1,0:T(8,128)} %get-tuple-element.44), channel_id=1, source_target_pairs={{0,4},{4,0},{8,12},{12,8},{1,5},{5,1},{9,13},{13,9},{2,6},{6,2},{1... | collective-permute-start | bytes 98312 | tf_op jit(solution)/shard_map/ppermute | solution.py:427
  60.2 9.5 %collective-permute-start.13 = (f32[1,32,256]{2,1,0:T(8,128)}, f32[1,32,256]{2,1,0:T(8,128)S(1)}, u32[]{:S(2)}, u32[]{:S(2)}) collective-permute-start(f32[1,32,256]{2,1,0:T(8,128)} %get-tuple-element.45), channel_id=1, source_target_pairs={{4,8},{8,4},{5,9},{9,5},{6,10},{10,6},{7,11},{11,7},{20,24},{24,20... | collective-permute-start | bytes 98312 | tf_op jit(solution)/shard_map/ppermute | solution.py:428
  65.0 2.8 %collective-permute-start.14 = (f32[1,16,32]{2,1,0:T(8,128)}, f32[1,16,32]{2,1,0:T(8,128)S(1)}, u32[]{:S(2)}, u32[]{:S(2)}) collective-permute-start(f32[1,16,32]{2,1,0:T(8,128)} %get-tuple-element.46), channel_id=1, source_target_pairs={{0,1},{1,0},{2,3},{3,2},{4,5},{5,4},{6,7},{7,6},{8,9},{9,8},{10,11... | collective-permute-start | bytes 6152 | tf_op jit(solution)/shard_map/ppermute | solution.py:427
  65.1 4.6 %collective-permute-start.15 = (f32[1,16,32]{2,1,0:T(8,128)}, f32[1,16,32]{2,1,0:T(8,128)S(1)}, u32[]{:S(2)}, u32[]{:S(2)}) collective-permute-start(f32[1,16,32]{2,1,0:T(8,128)} %get-tuple-element.47), channel_id=1, source_target_pairs={{1,2},{2,1},{5,6},{6,5},{9,10},{10,9},{13,14},{14,13},{17,18},{18,... | collective-permute-start | bytes 6152 | tf_op jit(solution)/shard_map/ppermute | solution.py:428
  67.8 1.9 %copy-start.14 = (f32[1,16,32]{2,1,0:T(8,128)}, f32[1,16,32]{2,1,0:T(8,128)S(1)}, u32[]{:S(2)}) copy-start(f32[1,16,32]{2,1,0:T(8,128)S(1)} %collective-permute-done.14.hz_lo) | copy-start | bytes 6148
  69.7 0.6 copy-start.15
  69.7 0.6 copy-start.10
  69.7 0.6 copy-start.11
